TPU v7x, 32 devices: a whole 2x2x4 slice. The times are simulated.
32 devices in a mesh: row: 8 (over y, x, core), col: 4 (over z).
Axes of the slice: x: 2, y: 2, z: 4, core: 2. Of those that a mesh axis runs over, the one named last changes fastest.
Arguments:
- left_values: bfloat16 [8, 4, 64, 128, 128], P('row', 'col'), may hold values from -6 to 6
- left_places: int32 [8, 4, 64], replicated, may hold values from 0 to 127, as said below
- right_values: bfloat16 [8, 4, 64, 128, 128], P('row', 'col'), may hold values from -0.25 to 0.25
- right_places: int32 [8, 4, 64], replicated, may hold values from 0 to 255, as said below
- owners: int32 [32, 128], P(('row', 'col')), may hold values from 0 to 31, as said below
Outputs:
- inbox: bfloat16 [32, 32, 8, 128, 128], P(('row', 'col'))
Inputs may be any that keep to these rules, and one draw needn't show every extreme that they name: `left_places`: within one tile's list the 64 positions are distinct. `right_places`: within one tile's list the 64 positions are distinct. Each row of owners names each device at most 8 times; in every draw some device is named exactly 8 times by every row.
All inputs are finite; a program needn't handle non-finite values.
Results may differ from a plain program's by a relative error of at most 0.001.
Values may be sent and summed in bfloat16 or wider, within the bound.
No kernel may reach another device: no remote copies, remote signals or barrier semaphores. Data moves between devices by JAX's collectives and lax.ppermute only.
A program may use at most 256 MiB of HBM per device.

v0:
```python
import jax
import jax.numpy as jnp
from jax import lax
from jax.sharding import PartitionSpec as P

ROWB = 8
KBLK = 16
COLB = 16


def from_behind(block, axis, distance):
    devices = range(lax.axis_size(axis))
    route = [((i - distance) % len(devices), i) for i in devices]
    return lax.ppermute(block, axis, route)


def column_stack(values, places):
    side_len = values.shape[-1]
    stacked = jnp.zeros((ROWB * KBLK, side_len, side_len), values.dtype)
    stacked = stacked.at[places].set(values)
    stacked = stacked.reshape(ROWB, KBLK, side_len, side_len).transpose(1, 0, 2, 3)
    return stacked.reshape(KBLK, ROWB * side_len, side_len)


def pair_terms(left_stack, right_here, right_list):
    taken = left_stack[right_list // COLB]
    return jnp.einsum("mik,mkj->mij", taken, right_here, preferred_element_type=jnp.float32)


def sum_columns(partial_value, right_list):
    side_len = partial_value.shape[-1]
    selector = (right_list[None, :] % COLB == jnp.arange(COLB, dtype=jnp.int32)[:, None]).astype(
        jnp.float32
    )
    summed = jnp.einsum(
        "cm,mij->cij",
        selector,
        partial_value,
        precision=lax.Precision.HIGHEST,
        preferred_element_type=jnp.float32,
    )
    summed = summed.reshape(COLB, ROWB, side_len, side_len).transpose(1, 0, 2, 3)
    return summed.reshape(ROWB * COLB, side_len, side_len)


def body(left_values, left_places, right_values, right_places, owners):
    rows_grid = lax.axis_size("row")
    cols_grid = lax.axis_size("col")
    devices_all = rows_grid * cols_grid
    row_here = lax.axis_index("row")
    col_here = lax.axis_index("col")
    row_next = (row_here + 1) % rows_grid
    col_next = (col_here + 1) % cols_grid
    left_here = left_values[0, 0]
    right_here = right_values[0, 0]
    side_len = left_here.shape[-1]
    left_next = from_behind(left_here, "col", -1)
    right_next = from_behind(right_here, "row", -1)
    places_left_first = left_places[row_here, col_here]
    places_right_first = right_places[row_here, col_here]
    places_left_second = left_places[row_here, col_next]
    places_right_second = right_places[row_next, col_here]
    stack_first = column_stack(left_here, places_left_first)
    stack_second = column_stack(left_next, places_left_second)
    terms_first = pair_terms(stack_first, right_here, places_right_first)
    product_blocks = sum_columns(terms_first, places_right_first)
    terms_second = pair_terms(stack_second, right_next, places_right_second)
    product_blocks = product_blocks + sum_columns(terms_second, places_right_second)
    blocks = product_blocks.astype(jnp.bfloat16)
    capacity = 2 * ROWB * COLB // devices_all
    owner_list = owners[0]
    positions = jnp.arange(ROWB * COLB, dtype=jnp.int32)
    same_owner = owner_list[None, :] == owner_list[:, None]
    earlier = positions[None, :] < positions[:, None]
    slot_index = jnp.sum((same_owner & earlier).astype(jnp.int32), axis=1)
    outgoing = jnp.zeros((devices_all * capacity, side_len, side_len), jnp.bfloat16)
    outgoing = outgoing.at[owner_list * capacity + slot_index].set(blocks)
    outgoing = outgoing.reshape(devices_all, capacity, side_len, side_len)
    received = lax.all_to_all(outgoing, ("row", "col"), split_axis=0, concat_axis=0, tiled=True)
    return received[None]


def solution(mesh):
    placed = (
        P("row", "col", None, None, None),
        P(),
        P("row", "col", None, None, None),
        P(),
        P(("row", "col"), None),
    )
    return jax.shard_map(
        body,
        mesh=mesh,
        in_specs=placed,
        out_specs=P(("row", "col"), None, None, None, None),
        check_vma=False,
    )
```

profile of v0, /device:TPU:1, one launch (start us, length us, event | category | flops | bytes accessed | tf_op | source)
XLA Modules:
  0.0 425.0 jit_solution(2701617845208975649)
XLA Ops:
  0.0 4.2 collective-permute-start
  4.2 1.0 collective-permute-start.1
  5.1 0.7 fusion.18
  5.8 0.7 and_select_fusion.3
  6.6 0.8 fusion.20
  7.3 3.1 broadcast.245.clone.1
  10.4 0.0 copy-start.1
  10.4 9.9 %scatter_fusion = bf16[128,128,128]{2,1,0:T(8,128)(2,1)} fusion(bf16[128,128,128]{2,1,0:T(8,128)(2,1)} %broadcast.245.clone.1, s32[64]{0:T(128)S(1)} %get-tuple-element.9, bf16[64,128,128]{2,1,0:T(8,128)(2,1)} %bitcast.90), kind=kCustom, calls=%fused_computation.2 | custom fusion | bytes 6291712 | tf_op jit(solution)/shard_map/scatter | solution.py:20
  20.3 4.7 %copy.12 = bf16[16,8,128,128]{3,2,1,0:T(8,128)(2,1)} copy(bf16[16,8,128,128]{3,2,0,1:T(8,128)(2,1)} %bitcast.85) | data formatting | bytes 8388608 | tf_op jit(solution)/shard_map/transpose | solution.py:21
  25.0 0.0 copy-done.1
  25.0 0.2 convert_reduce_fusion
  25.2 0.0 copy-start
  25.2 10.0 %gather_fusion = bf16[64,1024,128]{2,1,0:T(8,128)(2,1)} fusion(bf16[16,1024,128]{2,1,0:T(8,128)(2,1)} %bitcast.80, s32[1024]{0:T(1024)S(1)} %pad_clamp_fusion.1), kind=kCustom, calls=%fused_computation | custom fusion | bytes 33554688 | tf_op jit(solution)/shard_map/gather | solution.py:26
  35.3 0.0 copy-done
  35.3 16.4 %fusion.22 = f32[64,1024,128]{2,1,0:T(8,128)} fusion(bf16[64,1024,128]{2,1,0:T(8,128)(2,1)} %gather_fusion, bf16[1,1,64,128,128]{4,3,2,1,0:T(8,128)(2,1)S(1)} %copy-done), kind=kOutput, calls=%fused_computation.56 | convolution fusion | flops 2147483648 | bytes 52428800 | tf_op jit(solution)/shard_map/mik,mkj->mij/dot_general | solution.py:27
  51.7 0.0 collective-permute-done
  51.7 3.1 broadcast.245.clone
  54.8 9.9 %scatter_fusion.1 = bf16[128,128,128]{2,1,0:T(8,128)(2,1)} fusion(bf16[128,128,128]{2,1,0:T(8,128)(2,1)} %broadcast.245.clone, s32[64]{0:T(128)S(1)} %get-tuple-element.10, bf16[64,128,128]{2,1,0:T(8,128)(2,1)} %collective-permute-done), kind=kCustom, calls=%fused_computation.3 | custom fusion | bytes 6291712 | tf_op jit(solution)/shard_map/scatter | solution.py:20
  64.7 4.8 %copy.14 = bf16[16,8,128,128]{3,2,1,0:T(8,128)(2,1)} copy(bf16[16,8,128,128]{3,2,0,1:T(8,128)(2,1)} %bitcast.84) | data formatting | bytes 8388608 | tf_op jit(solution)/shard_map/transpose | solution.py:21
  69.5 9.9 %gather_fusion.1 = bf16[64,1024,128]{2,1,0:T(8,128)(2,1)} fusion(bf16[16,1024,128]{2,1,0:T(8,128)(2,1)} %bitcast.81, s32[1024]{0:T(1024)S(1)} %pad_clamp_fusion), kind=kCustom, calls=%fused_computation.1 | custom fusion | bytes 33554688 | tf_op jit(solution)/shard_map/gather | solution.py:26
  79.4 0.0 collective-permute-done.1
  79.4 17.0 %fusion.24 = f32[64,1024,128]{2,1,0:T(8,128)} fusion(bf16[64,1024,128]{2,1,0:T(8,128)(2,1)} %gather_fusion.1, bf16[64,128,128]{2,1,0:T(8,128)(2,1)} %collective-permute-done.1), kind=kOutput, calls=%fused_computation.58 | convolution fusion | flops 2147483648 | bytes 52428800 | tf_op jit(solution)/shard_map/mik,mkj->mij/dot_general | solution.py:27
  96.4 45.9 %fusion = f32[16,1024,128]{2,0,1:T(8,128)} fusion(f32[64,1024,128]{2,1,0:T(8,128)} %fusion.24, s32[64]{0:T(128)S(1)} %get-tuple-element.6), kind=kOutput, calls=%fused_computation.5 | convolution fusion | flops 1610613760 | bytes 41943296 | tf_op jit(solution)/shard_map/cm,mij->cij/dot_general | solution.py:35
  142.3 55.4 %add_convert_fusion = bf16[16,1024,128]{2,0,1:T(8,128)(2,1)S(1)} fusion(f32[16,1024,128]{2,0,1:T(8,128)} %fusion, f32[64,1024,128]{2,1,0:T(8,128)} %fusion.22, s32[64]{0:T(128)S(1)} %get-tuple-element.5), kind=kOutput, calls=%fused_computation.9 | convolution fusion | flops 1614808064 | bytes 46137600 | tf_op jit(solution)/shard_map/cm,mij->cij/dot_general | solution.py:35
  197.7 3.1 copy.16
  200.8 5.5 %broadcast_in_dim.4 = bf16[256,128,128]{2,1,0:T(8,128)(2,1)} broadcast(bf16[]{:T(256)} %constant.68.clone.1), dimensions={} | broadcast | bytes 8388610 | tf_op jit(solution)/shard_map/broadcast_in_dim | solution.py:76
  206.3 19.3 %scatter_fusion.2 = bf16[256,128,128]{2,1,0:T(8,128)(2,1)} fusion(bf16[256,128,128]{2,1,0:T(8,128)(2,1)} %broadcast_in_dim.4, s32[128]{0:T(128)S(1)} %fusion.17, bf16[128,128,128]{2,1,0:T(8,128)(2,1)} %bitcast.87), kind=kCustom, calls=%fused_computation.4 | custom fusion | bytes 12583424 | tf_op jit(solution)/shard_map/scatter | solution.py:77
  225.6 188.7 %all_to_all.5 = bf16[32,8,128,128]{3,2,1,0:T(8,128)(2,1)} all-to-all(bf16[32,8,128,128]{3,2,1,0:T(8,128)(2,1)} %bitcast.82), channel_id=1, replica_groups=mesh['row'=8,'col'=4] {'row','col'}, dimensions={0} | all-to-all | bytes 16777216 | tf_op jit(solution)/shard_map/all_to_all | solution.py:79
  414.2 10.5 %copy.27 = bf16[1,32,8,128,128]{4,3,2,1,0:T(8,128)(2,1)} copy(bf16[1,32,8,128,128]{4,3,2,1,0:T(8,128)(2,1)} %bitcast.83) | data formatting | bytes 16777216
  (3 shorter events, 0.0 us)
Async XLA Ops:
  0.0 51.7 %collective-permute-start = (bf16[64,128,128]{2,1,0:T(8,128)(2,1)}, bf16[64,128,128]{2,1,0:T(8,128)(2,1)}, u32[]{:S(2)}, u32[]{:S(2)}) collective-permute-start(bf16[64,128,128]{2,1,0:T(8,128)(2,1)} %bitcast.89), channel_id=1, source_target_pairs={{1,0},{2,1},{3,2},{0,3},{5,4},{6,5},{7,6},{4,7},{9,8},{10,9},{11,1... | collective-permute-start | bytes 6291464 | tf_op jit(solution)/shard_map/ppermute | solution.py:14
  4.2 75.2 %collective-permute-start.1 = (bf16[64,128,128]{2,1,0:T(8,128)(2,1)}, bf16[64,128,128]{2,1,0:T(8,128)(2,1)}, u32[]{:S(2)}, u32[]{:S(2)}) collective-permute-start(bf16[64,128,128]{2,1,0:T(8,128)(2,1)} %bitcast.88), channel_id=1, source_target_pairs={{4,0},{8,4},{12,8},{16,12},{20,16},{24,20},{28,24},{0,28},{5,1},{9... | collective-permute-start | bytes 6291464 | tf_op jit(solution)/shard_map/ppermute | solution.py:14
  10.4 14.6 %copy-start.1 = (s32[1,128]{1,0:T(1,128)S(1)}, s32[1,128]{1,0:T(1,128)}, u32[]{:S(2)}) copy-start(s32[1,128]{1,0:T(1,128)} %param.9) | copy-start | bytes 1540
  25.2 10.1 %copy-start = (bf16[1,1,64,128,128]{4,3,2,1,0:T(8,128)(2,1)S(1)}, bf16[1,1,64,128,128]{4,3,2,1,0:T(8,128)(2,1)}, u32[]{:S(2)}) copy-start(bf16[1,1,64,128,128]{4,3,2,1,0:T(8,128)(2,1)} %param.7) | copy-start | bytes 6291460
where the time goes:
time: 428 us; the launch traced here: 425 us
  blocking collectives  189 us (44%)
  matrix products  135 us (32%)
  local copies, waits for them, and re-layouts  93.8 us (22%)
  starting transfers between devices  5.11 us (1%)
    all_to_all x1, blocking collectives, body(): lax.all_to_all(outgoing, ('row', 'col'), split_axis=0, concat_axis=0, til...  189 us
    dot_general x2, matrix products, sum_columns(): jnp.einsum('cm,mij->cij', selector, partial_value, precision=lax.Precisio...  101 us
    dot_general x2, matrix products, pair_terms(): jnp.einsum('mik,mkj->mij', taken, right_here, preferred_element_type=jnp....  33.5 us
    gather x2, local copies, waits for them, and re-layouts, pair_terms(): taken = left_stack[right_list // COLB]  19.9 us
    scatter x2, local copies, waits for them, and re-layouts, column_stack(): stacked = stacked.at[places].set(values)  19.8 us
    scatter x1, local copies, waits for them, and re-layouts, body(): outgoing = outgoing.at[owner_list * capacity + slot_index].set(blocks)  19.3 us
    unnamed x5, local copies, waits for them, and re-layouts  10.5 us
    transpose x2, local copies, waits for them, and re-layouts, column_stack(): stacked.reshape(ROWB, KBLK, side_len, side_len).transpose(1, 0, 2, 3)  9.52 us
  transfers between devices with their start and end apart: 2, of which 0 were waited for; matrix products, arithmetic and copies ran while one was open for 17% of the time, Pallas kernels for 0%

commit v1 on v0

v1 whole, which is shorter than its diff:
```python
import jax
import jax.numpy as jnp
from jax import lax
from jax.sharding import PartitionSpec as P

ROWB = 8
KBLK = 16
COLB = 16


def from_behind(block, axis, distance):
    devices = range(lax.axis_size(axis))
    route = [((i - distance) % len(devices), i) for i in devices]
    return lax.ppermute(block, axis, route)


def dense_blocks(values, places, row_count, col_count):
    count = values.shape[0]
    positions = row_count * col_count
    index = jnp.full((positions,), count, jnp.int32).at[places].set(
        jnp.arange(count, dtype=jnp.int32)
    )
    present = index < count
    taken = values[jnp.minimum(index, count - 1)]
    taken = jnp.where(present[:, None, None], taken, jnp.zeros_like(taken))
    side_len = values.shape[-1]
    return taken.reshape(row_count, col_count, side_len, side_len)


def term(left_blocks, right_blocks):
    return jnp.einsum(
        "rkab,kcbd->rcad", left_blocks, right_blocks, preferred_element_type=jnp.float32
    )


def body(left_values, left_places, right_values, right_places, owners):
    rows_grid = lax.axis_size("row")
    cols_grid = lax.axis_size("col")
    devices_all = rows_grid * cols_grid
    row_here = lax.axis_index("row")
    col_here = lax.axis_index("col")
    row_next = (row_here + 1) % rows_grid
    col_next = (col_here + 1) % cols_grid
    left_here = left_values[0, 0]
    right_here = right_values[0, 0]
    side_len = left_here.shape[-1]
    left_next = from_behind(left_here, "col", -1)
    right_next = from_behind(right_here, "row", -1)
    left_first = dense_blocks(left_here, left_places[row_here, col_here], ROWB, KBLK)
    right_first = dense_blocks(right_here, right_places[row_here, col_here], KBLK, COLB)
    left_second = dense_blocks(left_next, left_places[row_here, col_next], ROWB, KBLK)
    right_second = dense_blocks(right_next, right_places[row_next, col_here], KBLK, COLB)
    product = term(left_first, right_first) + term(left_second, right_second)
    blocks = product.astype(jnp.bfloat16).reshape(ROWB * COLB, side_len, side_len)
    capacity = 2 * ROWB * COLB // devices_all
    owner_list = owners[0]
    product_count = ROWB * COLB
    positions = jnp.arange(product_count, dtype=jnp.int32)
    same_owner = owner_list[None, :] == owner_list[:, None]
    earlier = positions[None, :] < positions[:, None]
    slot_index = jnp.sum((same_owner & earlier).astype(jnp.int32), axis=1)
    slots = devices_all * capacity
    source_of = jnp.full((slots,), product_count, jnp.int32).at[
        owner_list * capacity + slot_index
    ].set(positions)
    filled = source_of < product_count
    outgoing = blocks[jnp.minimum(source_of, product_count - 1)]
    outgoing = jnp.where(filled[:, None, None], outgoing, jnp.zeros_like(outgoing))
    outgoing = outgoing.reshape(devices_all, capacity, side_len, side_len)
    received = lax.all_to_all(outgoing, ("row", "col"), split_axis=0, concat_axis=0, tiled=True)
    return received[None]


def solution(mesh):
    placed = (
        P("row", "col", None, None, None),
        P(),
        P("row", "col", None, None, None),
        P(),
        P(("row", "col"), None),
    )
    return jax.shard_map(
        body,
        mesh=mesh,
        in_specs=placed,
        out_specs=P(("row", "col"), None, None, None, None),
        check_vma=False,
    )
```

time: 428 us -> 320 us (0.75)
  matrix products: 135 us -> 28.6 us
  local copies, waits for them, and re-layouts: 93.8 us -> 85 us
  other arithmetic: 2.39 us -> 10.6 us
    dot_general x4 -> x2, matrix products: 135 us -> 28.6 us  [term(): jnp.einsum('rkab,kcbd->rcad', left_blocks, right_blocks, preferred_elemen...]
    gather x2 -> x7, local copies, waits for them, and re-layouts: 19.9 us -> 63.4 us  [the longest x6 52.4 us: dense_blocks(): taken = values[jnp.minimum(index, count - 1)]]
    scatter x3 -> x5, local copies, waits for them, and re-layouts: 39.1 us -> 4.06 us  [the longest x4 3.09 us: dense_blocks(): jnp.full((positions,), count, jnp.int32).at[places]]
    transpose x2 -> x0, local copies, waits for them, and re-layouts: 9.52 us -> none  [column_stack(): stacked.reshape(ROWB, KBLK, side_len, side_len).transpose(1, 0, 2, 3)]
    select_n x4 -> x8, other arithmetic: 2.21 us -> 9.59 us  [the longest x1 7.43 us: body(): jnp.where(filled[:, None, None], outgoing, jnp.zeros_like(outgoing))]
    another operation x2 -> x0, local copies, waits for them, and re-layouts: 6.12 us -> none
    broadcast_in_dim x1 -> x7, local copies, waits for them, and re-layouts: 5.52 us -> 0.61 us  [the longest x6 0.52 us: dense_blocks(): taken = jnp.where(present[:, None, None], taken, jnp.zeros_like(taken))]
    unnamed x5 -> x1, local copies, waits for them, and re-layouts: 10.5 us -> 10.5 us
  transfers between devices with their start and end apart: 2 -> 2, of which waited for: 0 -> 0; matrix products, arithmetic and copies ran while one was open for 17% -> 22% of each run, Pallas kernels for 0% -> 0%
where the time goes in v1:
time: 320 us; the launch traced here: 318 us
  blocking collectives  189 us (59%)
  local copies, waits for them, and re-layouts  85 us (27%)
  matrix products  28.6 us (9%)
  other arithmetic  10.6 us (3%)
  starting transfers between devices  4.83 us (2%)
    all_to_all x1, blocking collectives, body(): lax.all_to_all(outgoing, ('row', 'col'), split_axis=0, concat_axis=0, til...  189 us
    gather x6, local copies, waits for them, and re-layouts, dense_blocks(): taken = values[jnp.minimum(index, count - 1)]  52.4 us
    dot_general x2, matrix products, term(): jnp.einsum('rkab,kcbd->rcad', left_blocks, right_blocks, preferred_elemen...  28.6 us
    gather x1, local copies, waits for them, and re-layouts, body(): outgoing = blocks[jnp.minimum(source_of, product_count - 1)]  11 us
    unnamed x1, local copies, waits for them, and re-layouts  10.5 us
    select_n x1, other arithmetic, body(): jnp.where(filled[:, None, None], outgoing, jnp.zeros_like(outgoing))  7.43 us
    convert_element_type x1, local copies, waits for them, and re-layouts, body(): product.astype(jnp.bfloat16).reshape(ROWB * COLB, side_len, side_len)  6.45 us
  transfers between devices with their start and end apart: 2, of which 0 were waited for; matrix products, arithmetic and copies ran while one was open for 22% of the time, Pallas kernels for 0%

profile of v1, /device:TPU:1, one launch (start us, length us, event | category | flops | bytes accessed | tf_op | source)
XLA Modules:
  0.0 318.4 jit_solution(17908490352181064846)
XLA Ops:
  0.0 0.1 collective-permute-start
  0.1 4.8 %collective-permute-start.1 = (bf16[64,128,128]{2,1,0:T(8,128)(2,1)}, bf16[64,128,128]{2,1,0:T(8,128)(2,1)}, u32[]{:S(2)}, u32[]{:S(2)}) collective-permute-start(bf16[64,128,128]{2,1,0:T(8,128)(2,1)} %bitcast.91), channel_id=1, source_target_pairs={{1,0},{2,1},{3,2},{0,3},{5,4},{6,5},{7,6},{4,7},{9,8},{10,9},{11,1... | collective-permute-start | bytes 6291464 | tf_op jit(solution)/shard_map/ppermute | solution.py:14
  4.8 0.8 fusion.39
  5.6 0.8 scatter_custom_fusion.2
  6.4 0.8 scatter_custom_fusion.4
  7.2 0.7 fusion.38
  7.9 0.8 scatter_custom_fusion.3
  8.7 0.9 convert_reduce_fusion
  9.6 0.7 fusion.29
  10.3 0.8 scatter_custom_fusion.1
  11.1 1.0 scatter_custom_fusion
  12.1 10.1 %gather_fusion = bf16[256,128,128]{2,1,0:T(8,128)(2,1)} fusion(bf16[64,128,128]{2,1,0:T(8,128)(2,1)} %bitcast.90, s32[1024]{0:T(1024)S(1)} %pad_clamp_fusion.4), kind=kCustom, calls=%fused_computation | custom fusion | bytes 16778240 | tf_op jit(solution)/shard_map/gather | solution.py:24
  22.3 12.3 %copy.14 = bf16[16,16,128,128]{2,3,0,1:T(8,128)(2,1)} copy(bf16[16,16,128,128]{3,2,1,0:T(8,128)(2,1)} %bitcast.87) | data formatting | bytes 16777216 | tf_op jit(solution)/shard_map/gather | solution.py:24
  34.6 4.6 %gather_fusion.1 = bf16[128,128,128]{2,1,0:T(8,128)(2,1)} fusion(bf16[64,128,128]{2,1,0:T(8,128)(2,1)} %bitcast.92, s32[1024]{0:T(1024)S(1)} %pad_clamp_fusion.3), kind=kCustom, calls=%fused_computation.1 | custom fusion | bytes 8389120 | tf_op jit(solution)/shard_map/gather | solution.py:24
  39.2 0.1 broadcast_in_dim.76
  39.3 0.1 broadcast_in_dim.73
  39.4 0.1 copy.13
  39.5 0.1 broadcast_in_dim.82
  39.6 0.1 broadcast_in_dim.79
  39.7 0.1 copy.15
  39.8 0.1 broadcast_in_dim.71
  39.9 14.0 %fusion.2 = f32[16,128,8,128,1]{3,1,4,2,0:T(8,128)} fusion(bf16[16,16,128,128]{2,3,0,1:T(8,128)(2,1)} %copy.14, pred[16,16]{0,1:T(8,128)(4,1)S(1)} %copy.13, bf16[8,16,128,128]{3,2,1,0:T(8,128)(2,1)} %bitcast.93, pred[8,16]{1,0:T(8,128)(4,1)S(1)} %broadcast_in_dim.76), kind=kOutput, calls=%fused_computation.12 | convolution fusion | flops 8596226048 | bytes 20971904 | tf_op jit(solution)/shard_map/rkab,kcbd->rcad/dot_general | solution.py:31
  53.9 0.0 collective-permute-done
  53.9 8.4 %gather_fusion.2 = bf16[256,128,128]{2,1,0:T(8,128)(2,1)} fusion(bf16[64,128,128]{2,1,0:T(8,128)(2,1)S(1)} %collective-permute-done, s32[1024]{0:T(1024)S(1)} %pad_clamp_fusion.2), kind=kCustom, calls=%fused_computation.2 | custom fusion | bytes 16778240 | tf_op jit(solution)/shard_map/gather | solution.py:24
  62.3 12.3 %copy.16 = bf16[16,16,128,128]{2,3,0,1:T(8,128)(2,1)} copy(bf16[16,16,128,128]{3,2,1,0:T(8,128)(2,1)} %bitcast.86) | data formatting | bytes 16777216 | tf_op jit(solution)/shard_map/gather | solution.py:24
  74.6 0.0 collective-permute-done.1
  74.6 4.6 %gather_fusion.3 = bf16[128,128,128]{2,1,0:T(8,128)(2,1)} fusion(bf16[64,128,128]{2,1,0:T(8,128)(2,1)} %collective-permute-done.1, s32[1024]{0:T(1024)S(1)} %pad_clamp_fusion.1), kind=kCustom, calls=%fused_computation.3 | custom fusion | bytes 8389120 | tf_op jit(solution)/shard_map/gather | solution.py:24
  79.2 14.6 %fusion.9 = bf16[8,16,128,128]{2,3,0,1:T(8,128)(2,1)} fusion(f32[16,128,8,128,1]{3,1,4,2,0:T(8,128)} %fusion.2, bf16[8,16,128,128]{3,2,1,0:T(8,128)(2,1)} %bitcast.94, pred[8,16]{1,0:T(8,128)(4,1)S(1)} %broadcast_in_dim.82, bf16[16,16,128,128]{2,3,0,1:T(8,128)(2,1)} %copy.16, pred[16,16]{0,1:T(8,128)(4,1)S(1)} %copy.15), kind=kOutput, calls=%fused_computation.21 | convolution fusion | flops 8600420352 | bytes 25166208 | tf_op jit(solution)/shard_map/rkab,kcbd->rcad/dot_general | solution.py:31
  93.8 6.4 %copy.17 = bf16[8,16,128,128]{3,2,1,0:T(8,128)(2,1)} copy(bf16[8,16,128,128]{2,3,0,1:T(8,128)(2,1)} %fusion.9) | data formatting | bytes 8388608 | tf_op jit(solution)/shard_map/convert_element_type | solution.py:54
  100.2 11.0 %gather_fusion.4 = bf16[256,128,128]{2,1,0:T(8,128)(2,1)} fusion(bf16[128,128,128]{2,1,0:T(8,128)(2,1)} %bitcast.84, s32[1024]{0:T(1024)S(1)} %pad_clamp_fusion), kind=kCustom, calls=%fused_computation.4 | custom fusion | bytes 16778240 | tf_op jit(solution)/shard_map/gather | solution.py:67
  111.2 7.4 %broadcast_select_fusion = bf16[32,8,128,128]{3,2,1,0:T(8,128)(2,1)} fusion(bf16[32,8,128,128]{3,2,1,0:T(8,128)(2,1)} %bitcast.85, pred[32,8]{1,0:T(8,128)(4,1)S(1)} %broadcast_in_dim.71), kind=kLoop, calls=%fused_computation.20 | loop fusion | flops 4194304 | bytes 16777472 | tf_op jit(solution)/shard_map/jit(_where)/select_n | solution.py:68
  118.7 189.2 %all_to_all.5 = bf16[32,8,128,128]{3,2,1,0:T(8,128)(2,1)} all-to-all(bf16[32,8,128,128]{3,2,1,0:T(8,128)(2,1)} %broadcast_select_fusion), channel_id=1, replica_groups=mesh['row'=8,'col'=4] {'row','col'}, dimensions={0} | all-to-all | bytes 16777216 | tf_op jit(solution)/shard_map/all_to_all | solution.py:70
  307.9 10.5 %copy.23 = bf16[1,32,8,128,128]{4,3,2,1,0:T(8,128)(2,1)} copy(bf16[1,32,8,128,128]{4,3,2,1,0:T(8,128)(2,1)} %bitcast.88) | data formatting | bytes 16777216
  (19 shorter events, 0.1 us)
Async XLA Ops:
  0.0 53.9 %collective-permute-start = (bf16[64,128,128]{2,1,0:T(8,128)(2,1)}, bf16[64,128,128]{2,1,0:T(8,128)(2,1)S(1)}, u32[]{:S(2)}, u32[]{:S(2)}) collective-permute-start(bf16[64,128,128]{2,1,0:T(8,128)(2,1)} %bitcast.89), channel_id=1, source_target_pairs={{4,0},{8,4},{12,8},{16,12},{20,16},{24,20},{28,24},{0,28},{5,1},{9... | collective-permute-start | bytes 6291464 | tf_op jit(solution)/shard_map/ppermute | solution.py:14
  0.1 74.5 %collective-permute-start.1 = (bf16[64,128,128]{2,1,0:T(8,128)(2,1)}, bf16[64,128,128]{2,1,0:T(8,128)(2,1)}, u32[]{:S(2)}, u32[]{:S(2)}) collective-permute-start(bf16[64,128,128]{2,1,0:T(8,128)(2,1)} %bitcast.91), channel_id=1, source_target_pairs={{1,0},{2,1},{3,2},{0,3},{5,4},{6,5},{7,6},{4,7},{9,8},{10,9},{11,1... | collective-permute-start | bytes 6291464 | tf_op jit(solution)/shard_map/ppermute | solution.py:14

commit v2 on v1

v2 whole, which is shorter than its diff:
```python
import functools

import jax
import jax.numpy as jnp
from jax import lax
from jax.experimental import pallas as pl
from jax.experimental.pallas import tpu as pltpu
from jax.sharding import PartitionSpec as P

ROWB = 8
KBLK = 16
COLB = 16
COL_GROUP = 2
ROW_GROUP = 2


def from_behind(block, axis, distance):
    devices = range(lax.axis_size(axis))
    route = [((i - distance) % len(devices), i) for i in devices]
    return lax.ppermute(block, axis, route)


def product_kernel(
    rows_grid, cols_grid, capacity,
    left_places, right_places, owners,
    left_first, left_second, right_first, right_second,
    out,
    left_dense, right_column, left_index, right_index, slot_of, filled, counts,
):
    side = left_first.shape[-1]
    stored = left_first.shape[0]
    row_here = lax.axis_index("row")
    col_here = lax.axis_index("col")
    row_next = lax.rem(row_here + 1, rows_grid)
    col_next = lax.rem(col_here + 1, cols_grid)
    tile_len = left_places.shape[0] // (rows_grid * cols_grid)
    left_bases = ((row_here * cols_grid + col_here) * tile_len, (row_here * cols_grid + col_next) * tile_len)
    right_bases = ((row_here * cols_grid + col_here) * tile_len, (row_next * cols_grid + col_here) * tile_len)
    left_positions = ROWB * KBLK
    right_positions = KBLK * COLB
    slots = out.shape[0]
    products = ROWB * COLB

    def clear_left(p, carry):
        left_index[p] = -1
        return carry

    lax.fori_loop(0, 2 * left_positions, clear_left, 0)

    def clear_right(p, carry):
        right_index[p] = -1
        return carry

    lax.fori_loop(0, 2 * right_positions, clear_right, 0)

    def clear_slots(s, carry):
        filled[s] = 0
        return carry

    lax.fori_loop(0, slots, clear_slots, 0)

    def clear_counts(d, carry):
        counts[d] = 0
        return carry

    lax.fori_loop(0, counts.shape[0], clear_counts, 0)

    def invert(n, carry):
        for t in range(2):
            left_index[t * left_positions + left_places[left_bases[t] + n]] = n
            right_index[t * right_positions + right_places[right_bases[t] + n]] = n
        return carry

    lax.fori_loop(0, stored, invert, 0)

    def assign(m, carry):
        owner = owners[m]
        taken = counts[owner]
        slot = owner * capacity + taken
        slot_of[m] = slot
        filled[slot] = 1
        counts[owner] = taken + 1
        return carry

    lax.fori_loop(0, products, assign, 0)

    left_tiles = (left_first, left_second)
    right_tiles = (right_first, right_second)
    zero_block = jnp.zeros((side, side), left_first.dtype)

    def densify_left(r, carry):
        rows = pl.ds(pl.multiple_of(r * side, side), side)
        for t in range(2):
            for k in range(KBLK):
                index = left_index[t * left_positions + r * KBLK + k]
                block = left_tiles[t][jnp.maximum(index, 0)]
                column = (t * KBLK + k) * side
                left_dense[rows, column:column + side] = jnp.where(index >= 0, block, zero_block)
        return carry

    lax.fori_loop(0, ROWB, densify_left, 0)

    def column_pair(cp, carry):
        for t in range(2):
            for k in range(KBLK):
                for cc in range(COL_GROUP):
                    index = right_index[t * right_positions + k * COLB + cp * COL_GROUP + cc]
                    block = right_tiles[t][jnp.maximum(index, 0)]
                    row = (t * KBLK + k) * side
                    right_column[row:row + side, cc * side:(cc + 1) * side] = jnp.where(
                        index >= 0, block, zero_block
                    )

        def row_pair(rp, inner):
            rows = pl.ds(pl.multiple_of(rp * ROW_GROUP * side, ROW_GROUP * side), ROW_GROUP * side)
            result = jnp.dot(left_dense[rows, :], right_column[...], preferred_element_type=jnp.float32)
            for rr in range(ROW_GROUP):
                for cc in range(COL_GROUP):
                    m = (rp * ROW_GROUP + rr) * COLB + cp * COL_GROUP + cc
                    piece = result[rr * side:(rr + 1) * side, cc * side:(cc + 1) * side]
                    out[slot_of[m]] = piece.astype(out.dtype)
            return inner

        lax.fori_loop(0, ROWB // ROW_GROUP, row_pair, 0)
        return carry

    lax.fori_loop(0, COLB // COL_GROUP, column_pair, 0)

    def zero_slot(s, carry):
        @pl.when(filled[s] == 0)
        def _():
            out[s] = zero_block

        return carry

    lax.fori_loop(0, slots, zero_slot, 0)


def body(left_values, left_places, right_values, right_places, owners):
    rows_grid = lax.axis_size("row")
    cols_grid = lax.axis_size("col")
    devices_all = rows_grid * cols_grid
    left_here = left_values[0, 0]
    right_here = right_values[0, 0]
    side = left_here.shape[-1]
    left_next = from_behind(left_here, "col", -1)
    right_next = from_behind(right_here, "row", -1)
    capacity = 2 * ROWB * COLB // devices_all
    slots = devices_all * capacity
    smem = pl.BlockSpec(memory_space=pltpu.SMEM)
    vmem = pl.BlockSpec(memory_space=pltpu.VMEM)
    kernel = functools.partial(product_kernel, rows_grid, cols_grid, capacity)
    flops = 2 * (ROWB * side) * (2 * KBLK * side) * (COLB * side)
    outgoing = pl.pallas_call(
        kernel,
        out_shape=jax.ShapeDtypeStruct((slots, side, side), jnp.bfloat16),
        in_specs=[smem, smem, smem, vmem, vmem, vmem, vmem],
        out_specs=vmem,
        scratch_shapes=[
            pltpu.VMEM((ROWB * side, 2 * KBLK * side), jnp.bfloat16),
            pltpu.VMEM((2 * KBLK * side, COL_GROUP * side), jnp.bfloat16),
            pltpu.SMEM((2 * ROWB * KBLK,), jnp.int32),
            pltpu.SMEM((2 * KBLK * COLB,), jnp.int32),
            pltpu.SMEM((ROWB * COLB,), jnp.int32),
            pltpu.SMEM((slots,), jnp.int32),
            pltpu.SMEM((devices_all,), jnp.int32),
        ],
        compiler_params=pltpu.CompilerParams(vmem_limit_bytes=60 * 1024 * 1024),
        cost_estimate=pl.CostEstimate(
            flops=flops, bytes_accessed=4 * left_here.size * 2 + slots * side * side * 2, transcendentals=0
        ),
    )(
        left_places.reshape(-1),
        right_places.reshape(-1),
        owners[0],
        left_here,
        left_next,
        right_here,
        right_next,
    )
    outgoing = outgoing.reshape(devices_all, capacity, side, side)
    received = lax.all_to_all(outgoing, ("row", "col"), split_axis=0, concat_axis=0, tiled=True)
    return received[None]


def solution(mesh):
    placed = (
        P("row", "col", None, None, None),
        P(),
        P("row", "col", None, None, None),
        P(),
        P(("row", "col"), None),
    )
    return jax.shard_map(
        body,
        mesh=mesh,
        in_specs=placed,
        out_specs=P(("row", "col"), None, None, None, None),
        check_vma=False,
    )
```

time: 320 us -> 301 us (0.941)
  local copies, waits for them, and re-layouts: 85 us -> 14.6 us
  Pallas kernels: 0 us -> 48.9 us
  waiting for transfers between devices: 0.01 us -> 40.9 us
  matrix products: 28.6 us -> 0 us
  other arithmetic: 10.6 us -> 0 us
    gather x7 -> x0, local copies, waits for them, and re-layouts: 63.4 us -> none  [the longest x6 52.4 us: dense_blocks(): taken = values[jnp.minimum(index, count - 1)]]
    pallas_call x0 -> x1, Pallas kernels: none -> 48.9 us  [body(): pl.pallas_call(kernel, out_shape=jax.ShapeDtypeStruct((slots, side, side)...]
    ppermute x2, waiting for transfers between devices: 0.01 us -> 40.9 us  [from_behind(): return lax.ppermute(block, axis, route)]
    dot_general x2 -> x0, matrix products: 28.6 us -> none  [term(): jnp.einsum('rkab,kcbd->rcad', left_blocks, right_blocks, preferred_elemen...]
    select_n x8 -> x0, other arithmetic: 9.59 us -> none  [the longest x1 7.43 us: body(): jnp.where(filled[:, None, None], outgoing, jnp.zeros_like(outgoing))]
    convert_element_type x1 -> x0, local copies, waits for them, and re-layouts: 6.45 us -> none  [body(): product.astype(jnp.bfloat16).reshape(ROWB * COLB, side_len, side_len)]
    scatter x5 -> x0, local copies, waits for them, and re-layouts: 4.06 us -> none  [the longest x4 3.09 us: dense_blocks(): jnp.full((positions,), count, jnp.int32).at[places]]
    unnamed x1 -> x3, local copies, waits for them, and re-layouts: 10.5 us -> 11.8 us
  transfers between devices with their start and end apart: 2 -> 2, of which waited for: 0 -> 1; matrix products, arithmetic and copies ran while one was open for 22% -> 1% of each run, Pallas kernels for 0% -> 0%
where the time goes in v2:
time: 301 us
  blocking collectives  191 us (63%)
  Pallas kernels  48.9 us (16%)
  waiting for transfers between devices  40.9 us (14%)
  local copies, waits for them, and re-layouts  14.6 us (5%)
  starting transfers between devices  5.11 us (2%)
    all_to_all x1, blocking collectives, body(): lax.all_to_all(outgoing, ('row', 'col'), split_axis=0, concat_axis=0, til...  191 us
    pallas_call x1, Pallas kernels, body(): pl.pallas_call(kernel, out_shape=jax.ShapeDtypeStruct((slots, side, side)...  48.9 us
    ppermute x2, waiting for transfers between devices, from_behind(): return lax.ppermute(block, axis, route)  40.9 us
    unnamed x3, local copies, waits for them, and re-layouts  11.8 us
  transfers between devices with their start and end apart: 2, of which 1 were waited for; matrix products, arithmetic and copies ran while one was open for 1% of the time, Pallas kernels for 0%

profile of v2, /device:TPU:1, one launch (start us, length us, event | category | flops | bytes accessed | tf_op | source)
XLA Modules:
  0.0 301.0 jit_solution(4976334758627613878)
XLA Ops:
  0.0 4.2 %collective-permute-start = (bf16[64,128,128]{2,1,0:T(8,128)(2,1)}, bf16[64,128,128]{2,1,0:T(8,128)(2,1)S(1)}, u32[]{:S(2)}, u32[]{:S(2)}) collective-permute-start(bf16[64,128,128]{2,1,0:T(8,128)(2,1)} %bitcast.7), channel_id=1, source_target_pairs={{1,0},{2,1},{3,2},{0,3},{5,4},{6,5},{7,6},{4,7},{9,8},{10,9},{11,1... | collective-permute-start | bytes 6291464 | tf_op jit(solution)/shard_map/ppermute | solution.py:20
  4.2 1.0 collective-permute-start.1
  5.1 1.4 reshape.9.left_places
  6.5 1.4 reshape.10.right_places
  7.9 40.9 %collective-permute-done.left_second = bf16[64,128,128]{2,1,0:T(8,128)(2,1)S(1)} collective-permute-done((bf16[64,128,128]{2,1,0:T(8,128)(2,1)}, bf16[64,128,128]{2,1,0:T(8,128)(2,1)S(1)}, u32[]{:S(2)}, u32[]{:S(2)}) %collective-permute-start) | collective-permute-done | bytes 2097184 | tf_op jit(solution)/shard_map/ppermute | solution.py:20
  48.8 0.0 copy-start
  48.8 0.0 collective-permute-done.1.right_second
  48.8 1.3 copy-done
  50.1 48.9 %shard_map.55 = bf16[256,128,128]{2,1,0:T(8,128)(2,1)} custom-call(s32[2048]{0:T(1024)} %reshape.9.left_places, s32[2048]{0:T(1024)} %reshape.10.right_places, s32[128]{0:T(128)} %bitcast.11, bf16[64,128,128]{2,1,0:T(8,128)(2,1)} %bitcast.8, bf16[64,128,128]{2,1,0:T(8,128)(2,1)} %copy-done, bf16[64,128,128]{2,1,0:T(8,128)(2,1)} %bitcast.10, ...), custom_call_target="tpu_custom_call" | custom-call | flops 17179869184 | bytes 16777216 | tf_op jit(solution)/shard_map/pallas_call | solution.py:154
  99.0 191.5 %all_to_all.5 = bf16[32,8,128,128]{3,2,1,0:T(8,128)(2,1)} all-to-all(bf16[32,8,128,128]{3,2,1,0:T(8,128)(2,1)} %bitcast.6), channel_id=1, replica_groups=mesh['row'=8,'col'=4] {'row','col'}, dimensions={0} | all-to-all | bytes 16777216 | tf_op jit(solution)/shard_map/all_to_all | solution.py:182
  290.5 10.5 %copy.7 = bf16[1,32,8,128,128]{4,3,2,1,0:T(8,128)(2,1)} copy(bf16[1,32,8,128,128]{4,3,2,1,0:T(8,128)(2,1)} %bitcast.5) | data formatting | bytes 16777216
Async XLA Ops:
  0.0 48.8 %collective-permute-start = (bf16[64,128,128]{2,1,0:T(8,128)(2,1)}, bf16[64,128,128]{2,1,0:T(8,128)(2,1)S(1)}, u32[]{:S(2)}, u32[]{:S(2)}) collective-permute-start(bf16[64,128,128]{2,1,0:T(8,128)(2,1)} %bitcast.7), channel_id=1, source_target_pairs={{1,0},{2,1},{3,2},{0,3},{5,4},{6,5},{7,6},{4,7},{9,8},{10,9},{11,1... | collective-permute-start | bytes 6291464 | tf_op jit(solution)/shard_map/ppermute | solution.py:20
  4.2 44.6 %collective-permute-start.1 = (bf16[64,128,128]{2,1,0:T(8,128)(2,1)}, bf16[64,128,128]{2,1,0:T(8,128)(2,1)}, u32[]{:S(2)}, u32[]{:S(2)}) collective-permute-start(bf16[64,128,128]{2,1,0:T(8,128)(2,1)} %bitcast.9), channel_id=1, source_target_pairs={{4,0},{8,4},{12,8},{16,12},{20,16},{24,20},{28,24},{0,28},{5,1},{9... | collective-permute-start | bytes 6291464 | tf_op jit(solution)/shard_map/ppermute | solution.py:20
  48.8 1.3 copy-start

commit v3 on v1

v3 whole, which is shorter than its diff:
```python
import functools

import jax
import jax.numpy as jnp
from jax import lax
from jax.experimental import pallas as pl
from jax.experimental.pallas import tpu as pltpu
from jax.sharding import PartitionSpec as P

ROWB = 8
KBLK = 16
COLB = 16
COL_GROUP = 2
ROW_GROUP = 2


def from_behind(block, axis, distance):
    devices = range(lax.axis_size(axis))
    route = [((i - distance) % len(devices), i) for i in devices]
    return lax.ppermute(block, axis, route)


def fill(ref, count, value):
    def step(i, carry):
        ref[i] = value
        return carry

    lax.fori_loop(0, count, step, 0)


def tile_bases(rows_grid, cols_grid, tile_len, second):
    row_here = lax.axis_index("row")
    col_here = lax.axis_index("col")
    if second:
        left_tile = row_here * cols_grid + lax.rem(col_here + 1, cols_grid)
        right_tile = lax.rem(row_here + 1, rows_grid) * cols_grid + col_here
    else:
        left_tile = row_here * cols_grid + col_here
        right_tile = left_tile
    return left_tile * tile_len, right_tile * tile_len


def multiply_tiles(
    rows_grid, cols_grid, left_places, right_places, left_tile, right_tile,
    left_dense, right_column, left_index, right_index, second, emit,
):
    side = left_tile.shape[-1]
    stored = left_tile.shape[0]
    tile_len = left_places.shape[0] // (rows_grid * cols_grid)
    left_base, right_base = tile_bases(rows_grid, cols_grid, tile_len, second)
    fill(left_index, ROWB * KBLK, -1)
    fill(right_index, KBLK * COLB, -1)

    def invert(n, carry):
        left_index[left_places[left_base + n]] = n
        right_index[right_places[right_base + n]] = n
        return carry

    lax.fori_loop(0, stored, invert, 0)
    zero_block = jnp.zeros((side, side), left_tile.dtype)

    def densify_left(r, carry):
        rows = pl.ds(pl.multiple_of(r * side, side), side)
        for k in range(KBLK):
            index = left_index[r * KBLK + k]
            block = left_tile[jnp.maximum(index, 0)]
            left_dense[rows, k * side:(k + 1) * side] = jnp.where(index >= 0, block, zero_block)
        return carry

    lax.fori_loop(0, ROWB, densify_left, 0)

    def column_pair(cp, carry):
        for k in range(KBLK):
            for cc in range(COL_GROUP):
                index = right_index[k * COLB + cp * COL_GROUP + cc]
                block = right_tile[jnp.maximum(index, 0)]
                right_column[k * side:(k + 1) * side, cc * side:(cc + 1) * side] = jnp.where(
                    index >= 0, block, zero_block
                )

        def row_pair(rp, inner):
            rows = pl.ds(pl.multiple_of(rp * ROW_GROUP * side, ROW_GROUP * side), ROW_GROUP * side)
            result = jnp.dot(left_dense[rows, :], right_column[...], preferred_element_type=jnp.float32)
            emit(rp, cp, rows, result)
            return inner

        lax.fori_loop(0, ROWB // ROW_GROUP, row_pair, 0)
        return carry

    lax.fori_loop(0, COLB // COL_GROUP, column_pair, 0)


def first_kernel(
    rows_grid, cols_grid, capacity,
    left_places, right_places, owners, left_tile, right_tile,
    partial, slot_of, filled,
    left_dense, right_column, left_index, right_index, counts,
):
    side = left_tile.shape[-1]
    fill(filled, filled.shape[0], 0)
    fill(counts, counts.shape[0], 0)

    def assign(m, carry):
        owner = owners[m]
        taken = counts[owner]
        slot = owner * capacity + taken
        slot_of[m] = slot
        filled[slot] = 1
        counts[owner] = taken + 1
        return carry

    lax.fori_loop(0, ROWB * COLB, assign, 0)

    def emit(rp, cp, rows, result):
        columns = pl.ds(pl.multiple_of(cp * COL_GROUP * side, COL_GROUP * side), COL_GROUP * side)
        partial[rows, columns] = result

    multiply_tiles(
        rows_grid, cols_grid, left_places, right_places, left_tile, right_tile,
        left_dense, right_column, left_index, right_index, False, emit,
    )


def second_kernel(
    rows_grid, cols_grid,
    left_places, right_places, slot_of, filled, left_tile, right_tile, partial,
    out,
    left_dense, right_column, left_index, right_index,
):
    side = left_tile.shape[-1]

    def emit(rp, cp, rows, result):
        columns = pl.ds(pl.multiple_of(cp * COL_GROUP * side, COL_GROUP * side), COL_GROUP * side)
        total = result + partial[rows, columns]
        for rr in range(ROW_GROUP):
            for cc in range(COL_GROUP):
                m = (rp * ROW_GROUP + rr) * COLB + cp * COL_GROUP + cc
                piece = total[rr * side:(rr + 1) * side, cc * side:(cc + 1) * side]
                out[slot_of[m]] = piece.astype(out.dtype)

    multiply_tiles(
        rows_grid, cols_grid, left_places, right_places, left_tile, right_tile,
        left_dense, right_column, left_index, right_index, True, emit,
    )
    zero_block = jnp.zeros((side, side), out.dtype)

    def zero_slot(s, carry):
        @pl.when(filled[s] == 0)
        def _():
            out[s] = zero_block

        return carry

    lax.fori_loop(0, out.shape[0], zero_slot, 0)


def body(left_values, left_places, right_values, right_places, owners):
    rows_grid = lax.axis_size("row")
    cols_grid = lax.axis_size("col")
    devices_all = rows_grid * cols_grid
    left_here = left_values[0, 0]
    right_here = right_values[0, 0]
    side = left_here.shape[-1]
    left_next = from_behind(left_here, "col", -1)
    right_next = from_behind(right_here, "row", -1)
    capacity = 2 * ROWB * COLB // devices_all
    slots = devices_all * capacity
    products = ROWB * COLB
    smem = pl.BlockSpec(memory_space=pltpu.SMEM)
    vmem = pl.BlockSpec(memory_space=pltpu.VMEM)
    left_flat = left_places.reshape(-1)
    right_flat = right_places.reshape(-1)
    work = [
        pltpu.VMEM((ROWB * side, KBLK * side), jnp.bfloat16),
        pltpu.VMEM((KBLK * side, COL_GROUP * side), jnp.bfloat16),
        pltpu.SMEM((ROWB * KBLK,), jnp.int32),
        pltpu.SMEM((KBLK * COLB,), jnp.int32),
    ]
    flops = 2 * (ROWB * side) * (KBLK * side) * (COLB * side)
    tile_bytes = 2 * left_here.size * 2
    partial_bytes = ROWB * COLB * side * side * 4
    partial, slot_of, filled = pl.pallas_call(
        functools.partial(first_kernel, rows_grid, cols_grid, capacity),
        out_shape=(
            jax.ShapeDtypeStruct((ROWB * side, COLB * side), jnp.float32),
            jax.ShapeDtypeStruct((products,), jnp.int32),
            jax.ShapeDtypeStruct((slots,), jnp.int32),
        ),
        in_specs=[smem, smem, smem, vmem, vmem],
        out_specs=(vmem, smem, smem),
        scratch_shapes=work + [pltpu.SMEM((devices_all,), jnp.int32)],
        compiler_params=pltpu.CompilerParams(vmem_limit_bytes=60 * 1024 * 1024),
        cost_estimate=pl.CostEstimate(flops=flops, bytes_accessed=tile_bytes + partial_bytes, transcendentals=0),
    )(left_flat, right_flat, owners[0], left_here, right_here)
    outgoing = pl.pallas_call(
        functools.partial(second_kernel, rows_grid, cols_grid),
        out_shape=jax.ShapeDtypeStruct((slots, side, side), jnp.bfloat16),
        in_specs=[smem, smem, smem, smem, vmem, vmem, vmem],
        out_specs=vmem,
        scratch_shapes=work,
        compiler_params=pltpu.CompilerParams(vmem_limit_bytes=60 * 1024 * 1024),
        cost_estimate=pl.CostEstimate(
            flops=flops, bytes_accessed=tile_bytes + partial_bytes + slots * side * side * 2, transcendentals=0
        ),
    )(left_flat, right_flat, slot_of, filled, left_next, right_next, partial)
    outgoing = outgoing.reshape(devices_all, capacity, side, side)
    received = lax.all_to_all(outgoing, ("row", "col"), split_axis=0, concat_axis=0, tiled=True)
    return received[None]


def solution(mesh):
    placed = (
        P("row", "col", None, None, None),
        P(),
        P("row", "col", None, None, None),
        P(),
        P(("row", "col"), None),
    )
    return jax.shard_map(
        body,
        mesh=mesh,
        in_specs=placed,
        out_specs=P(("row", "col"), None, None, None, None),
        check_vma=False,
    )
```

time: 320 us -> 285 us (0.89)
  local copies, waits for them, and re-layouts: 85 us -> 14.6 us
  Pallas kernels: 0 us -> 61.7 us
  matrix products: 28.6 us -> 0 us
  waiting for transfers between devices: 0.01 us -> 11.7 us
  other arithmetic: 10.6 us -> 0 us
    gather x7 -> x0, local copies, waits for them, and re-layouts: 63.4 us -> none  [the longest x6 52.4 us: dense_blocks(): taken = values[jnp.minimum(index, count - 1)]]
    pallas_call x0 -> x2, Pallas kernels: none -> 61.7 us  [the longest x1 32.4 us: body(): pl.pallas_call(functools.partial(second_kernel, rows_grid, cols_grid), ou...]
    dot_general x2 -> x0, matrix products: 28.6 us -> none  [term(): jnp.einsum('rkab,kcbd->rcad', left_blocks, right_blocks, preferred_elemen...]
    ppermute x2, waiting for transfers between devices: 0.01 us -> 11.7 us  [from_behind(): return lax.ppermute(block, axis, route)]
    select_n x8 -> x0, other arithmetic: 9.59 us -> none  [the longest x1 7.43 us: body(): jnp.where(filled[:, None, None], outgoing, jnp.zeros_like(outgoing))]
    convert_element_type x1 -> x0, local copies, waits for them, and re-layouts: 6.45 us -> none  [body(): product.astype(jnp.bfloat16).reshape(ROWB * COLB, side_len, side_len)]
    scatter x5 -> x0, local copies, waits for them, and re-layouts: 4.06 us -> none  [the longest x4 3.09 us: dense_blocks(): jnp.full((positions,), count, jnp.int32).at[places]]
    unnamed x1 -> x3, local copies, waits for them, and re-layouts: 10.5 us -> 11.9 us
  transfers between devices with their start and end apart: 2 -> 2, of which waited for: 0 -> 1; matrix products, arithmetic and copies ran while one was open for 22% -> 1% of each run, Pallas kernels for 0% -> 10%
where the time goes in v3:
time: 285 us
  blocking collectives  191 us (67%)
  Pallas kernels  61.7 us (22%)
  local copies, waits for them, and re-layouts  14.6 us (5%)
  waiting for transfers between devices  11.7 us (4%)
  starting transfers between devices  5.11 us (2%)
    all_to_all x1, blocking collectives, body(): lax.all_to_all(outgoing, ('row', 'col'), split_axis=0, concat_axis=0, til...  191 us
    pallas_call x1, Pallas kernels, body(): pl.pallas_call(functools.partial(second_kernel, rows_grid, cols_grid), ou...  32.4 us
    pallas_call x1, Pallas kernels, body(): pl.pallas_call(functools.partial(first_kernel, rows_grid, cols_grid, capa...  29.2 us
    unnamed x3, local copies, waits for them, and re-layouts  11.9 us
    ppermute x2, waiting for transfers between devices, from_behind(): return lax.ppermute(block, axis, route)  11.7 us
  transfers between devices with their start and end apart: 2, of which 1 were waited for; matrix products, arithmetic and copies ran while one was open for 1% of the time, Pallas kernels for 10%

profile of v3, /device:TPU:1, one launch (start us, length us, event | category | flops | bytes accessed | tf_op | source)
XLA Modules:
  0.0 284.5 jit_solution(6585027928264866555)
XLA Ops:
  0.0 4.2 %collective-permute-start = (bf16[64,128,128]{2,1,0:T(8,128)(2,1)}, bf16[64,128,128]{2,1,0:T(8,128)(2,1)S(1)}, u32[]{:S(2)}, u32[]{:S(2)}) collective-permute-start(bf16[64,128,128]{2,1,0:T(8,128)(2,1)} %bitcast.7), channel_id=1, source_target_pairs={{1,0},{2,1},{3,2},{0,3},{5,4},{6,5},{7,6},{4,7},{9,8},{10,9},{11,1... | collective-permute-start | bytes 6291464 | tf_op jit(solution)/shard_map/ppermute | solution.py:20
  4.2 1.0 collective-permute-start.1
  5.1 1.4 reshape.9.left_places
  6.5 1.4 reshape.10.right_places
  7.9 29.2 %shard_map.55 = (f32[1024,2048]{1,0:T(8,128)}, s32[128]{0:T(128)}, s32[256]{0:T(256)}) custom-call(s32[2048]{0:T(1024)} %reshape.9.left_places, s32[2048]{0:T(1024)} %reshape.10.right_places, s32[128]{0:T(128)} %bitcast.11, bf16[64,128,128]{2,1,0:T(8,128)(2,1)} %bitcast.8, bf16[64,128,128]{2,1,0:T(8,128)(2,1)} %bitcast.10), custom_call_target="tpu_custom_call" | custom-call | flops 8589934592 | bytes 12582912 | tf_op jit(solution)/shard_map/pallas_call | solution.py:182
  37.1 11.7 %collective-permute-done.left_tile = bf16[64,128,128]{2,1,0:T(8,128)(2,1)S(1)} collective-permute-done((bf16[64,128,128]{2,1,0:T(8,128)(2,1)}, bf16[64,128,128]{2,1,0:T(8,128)(2,1)S(1)}, u32[]{:S(2)}, u32[]{:S(2)}) %collective-permute-start) | collective-permute-done | bytes 2097184 | tf_op jit(solution)/shard_map/ppermute | solution.py:20
  48.8 0.0 copy-start
  48.8 0.0 collective-permute-done.1.right_tile
  48.8 1.3 copy-done
  50.1 32.4 %shard_map.56 = bf16[256,128,128]{2,1,0:T(8,128)(2,1)} custom-call(s32[2048]{0:T(1024)} %reshape.9.left_places, s32[2048]{0:T(1024)} %reshape.10.right_places, s32[128]{0:T(128)} %get-tuple-element.8.slot_of, s32[256]{0:T(256)} %get-tuple-element.9.filled, bf16[64,128,128]{2,1,0:T(8,128)(2,1)} %copy-done, ...), custom_call_target="tpu_custom_call" | custom-call | flops 8589934592 | bytes 20971520 | tf_op jit(solution)/shard_map/pallas_call | solution.py:195
  82.6 191.5 %all_to_all.5 = bf16[32,8,128,128]{3,2,1,0:T(8,128)(2,1)} all-to-all(bf16[32,8,128,128]{3,2,1,0:T(8,128)(2,1)} %bitcast.6), channel_id=1, replica_groups=mesh['row'=8,'col'=4] {'row','col'}, dimensions={0} | all-to-all | bytes 16777216 | tf_op jit(solution)/shard_map/all_to_all | solution.py:207
  274.0 10.5 %copy.7 = bf16[1,32,8,128,128]{4,3,2,1,0:T(8,128)(2,1)} copy(bf16[1,32,8,128,128]{4,3,2,1,0:T(8,128)(2,1)} %bitcast.5) | data formatting | bytes 16777216
Async XLA Ops:
  0.0 48.8 %collective-permute-start = (bf16[64,128,128]{2,1,0:T(8,128)(2,1)}, bf16[64,128,128]{2,1,0:T(8,128)(2,1)S(1)}, u32[]{:S(2)}, u32[]{:S(2)}) collective-permute-start(bf16[64,128,128]{2,1,0:T(8,128)(2,1)} %bitcast.7), channel_id=1, source_target_pairs={{1,0},{2,1},{3,2},{0,3},{5,4},{6,5},{7,6},{4,7},{9,8},{10,9},{11,1... | collective-permute-start | bytes 6291464 | tf_op jit(solution)/shard_map/ppermute | solution.py:20
  4.2 44.6 %collective-permute-start.1 = (bf16[64,128,128]{2,1,0:T(8,128)(2,1)}, bf16[64,128,128]{2,1,0:T(8,128)(2,1)}, u32[]{:S(2)}, u32[]{:S(2)}) collective-permute-start(bf16[64,128,128]{2,1,0:T(8,128)(2,1)} %bitcast.9), channel_id=1, source_target_pairs={{4,0},{8,4},{12,8},{16,12},{20,16},{24,20},{28,24},{0,28},{5,1},{9... | collective-permute-start | bytes 6291464 | tf_op jit(solution)/shard_map/ppermute | solution.py:20
  48.8 1.4 copy-start

commit v4 on v3

v4 whole, which is shorter than its diff:
```python
import functools

import jax
import jax.numpy as jnp
from jax import lax
from jax.experimental import pallas as pl
from jax.experimental.pallas import tpu as pltpu
from jax.sharding import PartitionSpec as P

ROWB = 8
KBLK = 16
COLB = 16
COL_GROUP = 2
ROW_GROUP = 2


def from_behind(block, axis, distance):
    devices = range(lax.axis_size(axis))
    route = [((i - distance) % len(devices), i) for i in devices]
    return lax.ppermute(block, axis, route)


def fill(ref, count, value):
    def step(i, carry):
        ref[i] = value
        return carry

    lax.fori_loop(0, count, step, 0)


def invert_places(places, base, index_ref, positions, stored):
    fill(index_ref, positions, -1)

    def step(n, carry):
        index_ref[places[base + n]] = n
        return carry

    lax.fori_loop(0, stored, step, 0)


def multiply_tiles(left_tile, right_tile, left_index, right_index, left_dense, right_column, emit, before=None):
    side = left_tile.shape[-1]
    zero_block = jnp.zeros((side, side), left_tile.dtype)

    def densify_left(r, carry):
        rows = pl.ds(pl.multiple_of(r * side, side), side)
        for k in range(KBLK):
            index = left_index[r * KBLK + k]
            block = left_tile[jnp.maximum(index, 0)]
            left_dense[rows, k * side:(k + 1) * side] = jnp.where(index >= 0, block, zero_block)
        return carry

    lax.fori_loop(0, ROWB, densify_left, 0)

    def column_pair(cp, carry):
        if before is not None:
            before(cp)
        for k in range(KBLK):
            for cc in range(COL_GROUP):
                index = right_index[k * COLB + cp * COL_GROUP + cc]
                block = right_tile[jnp.maximum(index, 0)]
                right_column[k * side:(k + 1) * side, cc * side:(cc + 1) * side] = jnp.where(
                    index >= 0, block, zero_block
                )

        def row_pair(rp, inner):
            rows = pl.ds(pl.multiple_of(rp * ROW_GROUP * side, ROW_GROUP * side), ROW_GROUP * side)
            result = jnp.dot(left_dense[rows, :], right_column[...], preferred_element_type=jnp.float32)
            emit(rp, cp, rows, result)
            return inner

        lax.fori_loop(0, ROWB // ROW_GROUP, row_pair, 0)
        return carry

    lax.fori_loop(0, COLB // COL_GROUP, column_pair, 0)


def first_kernel(
    rows_grid, cols_grid, capacity,
    left_places, right_places, owners, left_tile, right_tile,
    partial, slot_of, filled, left_index_next, right_index_next,
    left_dense, right_column, left_index, right_index, counts,
):
    side = left_tile.shape[-1]
    stored = left_tile.shape[0]
    tile_len = left_places.shape[0] // (rows_grid * cols_grid)
    row_here = lax.axis_index("row")
    col_here = lax.axis_index("col")
    tile_here = (row_here * cols_grid + col_here) * tile_len
    left_next = (row_here * cols_grid + lax.rem(col_here + 1, cols_grid)) * tile_len
    right_next = (lax.rem(row_here + 1, rows_grid) * cols_grid + col_here) * tile_len
    invert_places(left_places, tile_here, left_index, ROWB * KBLK, stored)
    invert_places(right_places, tile_here, right_index, KBLK * COLB, stored)
    invert_places(left_places, left_next, left_index_next, ROWB * KBLK, stored)
    invert_places(right_places, right_next, right_index_next, KBLK * COLB, stored)
    fill(filled, filled.shape[0], 0)
    fill(counts, counts.shape[0], 0)

    def assign(m, carry):
        owner = owners[m]
        taken = counts[owner]
        slot = owner * capacity + taken
        slot_of[m] = slot
        filled[slot] = 1
        counts[owner] = taken + 1
        return carry

    lax.fori_loop(0, ROWB * COLB, assign, 0)

    def emit(rp, cp, rows, result):
        partial[cp, rows, :] = result

    multiply_tiles(left_tile, right_tile, left_index, right_index, left_dense, right_column, emit)


def second_kernel(
    slot_of, filled, left_index, right_index, left_tile, right_tile, partial,
    out,
    left_dense, right_column, partial_buf, staging, zero_ref, partial_sems, out_sems,
):
    side = left_tile.shape[-1]
    pairs = COLB // COL_GROUP
    slots = out.shape[0]
    zero_ref[...] = jnp.zeros(zero_ref.shape, zero_ref.dtype)

    def partial_copy(cp, buffer):
        return pltpu.make_async_copy(partial.at[cp], partial_buf.at[buffer], partial_sems.at[buffer])

    partial_copy(0, 0).start()

    def zero_slot(s, carry):
        @pl.when(filled[s] == 0)
        def _():
            pltpu.make_async_copy(zero_ref, out.at[s], out_sems.at[s]).start()

        return carry

    lax.fori_loop(0, slots, zero_slot, 0)

    def send_pair(cp):
        for r in range(ROWB):
            for cc in range(COL_GROUP):
                m = r * COLB + cp * COL_GROUP + cc
                slot = slot_of[m]
                pltpu.make_async_copy(staging.at[m], out.at[slot], out_sems.at[slot]).start()

    def before(cp):
        buffer = lax.rem(cp, 2)

        @pl.when(cp + 1 < pairs)
        def _():
            partial_copy(cp + 1, 1 - buffer).start()

        @pl.when(cp > 0)
        def _():
            send_pair(cp - 1)

        partial_copy(cp, buffer).wait()

    def emit(rp, cp, rows, result):
        buffer = lax.rem(cp, 2)
        total = result + partial_buf[buffer, rows, :]
        for rr in range(ROW_GROUP):
            for cc in range(COL_GROUP):
                m = (rp * ROW_GROUP + rr) * COLB + cp * COL_GROUP + cc
                piece = total[rr * side:(rr + 1) * side, cc * side:(cc + 1) * side]
                staging[m] = piece.astype(staging.dtype)

    multiply_tiles(left_tile, right_tile, left_index, right_index, left_dense, right_column, emit, before)
    send_pair(pairs - 1)

    def wait_slot(s, carry):
        pltpu.make_async_copy(zero_ref, out.at[s], out_sems.at[s]).wait()
        return carry

    lax.fori_loop(0, slots, wait_slot, 0)


def body(left_values, left_places, right_values, right_places, owners):
    rows_grid = lax.axis_size("row")
    cols_grid = lax.axis_size("col")
    devices_all = rows_grid * cols_grid
    left_here = left_values[0, 0]
    right_here = right_values[0, 0]
    side = left_here.shape[-1]
    left_next = from_behind(left_here, "col", -1)
    right_next = from_behind(right_here, "row", -1)
    capacity = 2 * ROWB * COLB // devices_all
    slots = devices_all * capacity
    products = ROWB * COLB
    pairs = COLB // COL_GROUP
    smem = pl.BlockSpec(memory_space=pltpu.SMEM)
    vmem = pl.BlockSpec(memory_space=pltpu.VMEM)
    anywhere = pl.BlockSpec(memory_space=pl.ANY)
    left_flat = left_places.reshape(-1)
    right_flat = right_places.reshape(-1)
    work = [
        pltpu.VMEM((ROWB * side, KBLK * side), jnp.bfloat16),
        pltpu.VMEM((KBLK * side, COL_GROUP * side), jnp.bfloat16),
    ]
    flops = 2 * (ROWB * side) * (KBLK * side) * (COLB * side)
    tile_bytes = 2 * left_here.size * 2
    partial_bytes = ROWB * COLB * side * side * 4
    partial, slot_of, filled, left_index, right_index = pl.pallas_call(
        functools.partial(first_kernel, rows_grid, cols_grid, capacity),
        out_shape=(
            jax.ShapeDtypeStruct((pairs, ROWB * side, COL_GROUP * side), jnp.float32),
            jax.ShapeDtypeStruct((products,), jnp.int32),
            jax.ShapeDtypeStruct((slots,), jnp.int32),
            jax.ShapeDtypeStruct((ROWB * KBLK,), jnp.int32),
            jax.ShapeDtypeStruct((KBLK * COLB,), jnp.int32),
        ),
        in_specs=[smem, smem, smem, vmem, vmem],
        out_specs=(vmem, smem, smem, smem, smem),
        scratch_shapes=work + [
            pltpu.SMEM((ROWB * KBLK,), jnp.int32),
            pltpu.SMEM((KBLK * COLB,), jnp.int32),
            pltpu.SMEM((devices_all,), jnp.int32),
        ],
        compiler_params=pltpu.CompilerParams(vmem_limit_bytes=60 * 1024 * 1024),
        cost_estimate=pl.CostEstimate(flops=flops, bytes_accessed=tile_bytes + partial_bytes, transcendentals=0),
    )(left_flat, right_flat, owners[0], left_here, right_here)
    outgoing = pl.pallas_call(
        second_kernel,
        out_shape=jax.ShapeDtypeStruct((slots, side, side), jnp.bfloat16),
        in_specs=[smem, smem, smem, smem, vmem, vmem, anywhere],
        out_specs=anywhere,
        scratch_shapes=work + [
            pltpu.VMEM((2, ROWB * side, COL_GROUP * side), jnp.float32),
            pltpu.VMEM((products, side, side), jnp.bfloat16),
            pltpu.VMEM((side, side), jnp.bfloat16),
            pltpu.SemaphoreType.DMA((2,)),
            pltpu.SemaphoreType.DMA((slots,)),
        ],
        compiler_params=pltpu.CompilerParams(vmem_limit_bytes=60 * 1024 * 1024),
        cost_estimate=pl.CostEstimate(
            flops=flops, bytes_accessed=tile_bytes + partial_bytes + slots * side * side * 2, transcendentals=0
        ),
    )(slot_of, filled, left_index, right_index, left_next, right_next, partial)
    outgoing = outgoing.reshape(devices_all, capacity, side, side)
    received = lax.all_to_all(outgoing, ("row", "col"), split_axis=0, concat_axis=0, tiled=True)
    return received[None]


def solution(mesh):
    placed = (
        P("row", "col", None, None, None),
        P(),
        P("row", "col", None, None, None),
        P(),
        P(("row", "col"), None),
    )
    return jax.shard_map(
        body,
        mesh=mesh,
        in_specs=placed,
        out_specs=P(("row", "col"), None, None, None, None),
        check_vma=False,
    )
```

time: 285 us -> 279 us (0.979)
  waiting for transfers between devices: 11.7 us -> 7.34 us
    pallas_call x1, Pallas kernels: 32.4 us -> 26.7 us  [body(): pl.pallas_call(second_kernel, out_shape=jax.ShapeDtypeStruct((slots, side...]
    ppermute x2, waiting for transfers between devices: 11.7 us -> 7.34 us  [from_behind(): return lax.ppermute(block, axis, route)]
    pallas_call x1, Pallas kernels: 29.2 us -> 33.5 us  [body(): pl.pallas_call(functools.partial(first_kernel, rows_grid, cols_grid, capa...]
  transfers between devices with their start and end apart: 2 -> 2, of which waited for: 1 -> 1; matrix products, arithmetic and copies ran while one was open for 1% -> 1% of each run, Pallas kernels for 10% -> 12%
where the time goes in v4:
time: 279 us
  blocking collectives  191 us (68%)
  Pallas kernels  60.2 us (22%)
  local copies, waits for them, and re-layouts  14.6 us (5%)
  waiting for transfers between devices  7.34 us (3%)
  starting transfers between devices  5.11 us (2%)
    all_to_all x1, blocking collectives, body(): lax.all_to_all(outgoing, ('row', 'col'), split_axis=0, concat_axis=0, til...  191 us
    pallas_call x1, Pallas kernels, body(): pl.pallas_call(functools.partial(first_kernel, rows_grid, cols_grid, capa...  33.5 us
    pallas_call x1, Pallas kernels, body(): pl.pallas_call(second_kernel, out_shape=jax.ShapeDtypeStruct((slots, side...  26.7 us
    unnamed x3, local copies, waits for them, and re-layouts  11.8 us
    ppermute x2, waiting for transfers between devices, from_behind(): return lax.ppermute(block, axis, route)  7.34 us
  transfers between devices with their start and end apart: 2, of which 1 were waited for; matrix products, arithmetic and copies ran while one was open for 1% of the time, Pallas kernels for 12%

profile of v4, /device:TPU:1, one launch (start us, length us, event | category | flops | bytes accessed | tf_op | source)
XLA Modules:
  0.0 278.7 jit_solution(13946819579643939568)
XLA Ops:
  0.0 4.2 %collective-permute-start = (bf16[64,128,128]{2,1,0:T(8,128)(2,1)}, bf16[64,128,128]{2,1,0:T(8,128)(2,1)S(1)}, u32[]{:S(2)}, u32[]{:S(2)}) collective-permute-start(bf16[64,128,128]{2,1,0:T(8,128)(2,1)} %bitcast.7), channel_id=1, source_target_pairs={{1,0},{2,1},{3,2},{0,3},{5,4},{6,5},{7,6},{4,7},{9,8},{10,9},{11,1... | collective-permute-start | bytes 6291464 | tf_op jit(solution)/shard_map/ppermute | solution.py:20
  4.2 1.0 collective-permute-start.1
  5.1 1.4 reshape.9.left_places
  6.5 1.4 reshape.10.right_places
  7.9 33.5 %shard_map.55 = (f32[8,1024,256]{2,1,0:T(8,128)}, s32[128]{0:T(128)}, s32[256]{0:T(256)}, s32[128]{0:T(128)}, s32[256]{0:T(256)}) custom-call(s32[2048]{0:T(1024)} %reshape.9.left_places, s32[2048]{0:T(1024)} %reshape.10.right_places, s32[128]{0:T(128)} %bitcast.11, bf16[64,128,128]{2,1,0:T(8,128)(2,1)} %bitcast.8, bf16[64,128,128]{2,1,0:T(8,128)(2,1)} %bitcast.10), custom_call_target="tpu_custom_call" | custom-call | flops 8589934592 | bytes 12582912 | tf_op jit(solution)/shard_map/pallas_call | solution.py:204
  41.4 7.3 %collective-permute-done.left_tile = bf16[64,128,128]{2,1,0:T(8,128)(2,1)S(1)} collective-permute-done((bf16[64,128,128]{2,1,0:T(8,128)(2,1)}, bf16[64,128,128]{2,1,0:T(8,128)(2,1)S(1)}, u32[]{:S(2)}, u32[]{:S(2)}) %collective-permute-start) | collective-permute-done | bytes 2097184 | tf_op jit(solution)/shard_map/ppermute | solution.py:20
  48.8 0.0 copy-start
  48.8 0.0 collective-permute-done.1.right_tile
  48.8 1.3 copy-done
  50.1 26.7 %shard_map.56 = bf16[256,128,128]{2,1,0:T(8,128)(2,1)} custom-call(s32[128]{0:T(128)} %get-tuple-element.10.slot_of, s32[256]{0:T(256)} %get-tuple-element.11.filled, s32[128]{0:T(128)} %get-tuple-element.12.left_index, s32[256]{0:T(256)} %get-tuple-element.13.right_index, bf16[64,128,128]{2,1,0:T(8,128)(2,1)} %copy-done, ...), custom_call_target="tpu_custom_call" | custom-call | flops 8589934592 | bytes 20971520 | tf_op jit(solution)/shard_map/pallas_call | solution.py:223
  76.7 191.5 %all_to_all.5 = bf16[32,8,128,128]{3,2,1,0:T(8,128)(2,1)} all-to-all(bf16[32,8,128,128]{3,2,1,0:T(8,128)(2,1)} %bitcast.6), channel_id=1, replica_groups=mesh['row'=8,'col'=4] {'row','col'}, dimensions={0} | all-to-all | bytes 16777216 | tf_op jit(solution)/shard_map/all_to_all | solution.py:241
  268.2 10.5 %copy.7 = bf16[1,32,8,128,128]{4,3,2,1,0:T(8,128)(2,1)} copy(bf16[1,32,8,128,128]{4,3,2,1,0:T(8,128)(2,1)} %bitcast.5) | data formatting | bytes 16777216
Async XLA Ops:
  0.0 48.8 %collective-permute-start = (bf16[64,128,128]{2,1,0:T(8,128)(2,1)}, bf16[64,128,128]{2,1,0:T(8,128)(2,1)S(1)}, u32[]{:S(2)}, u32[]{:S(2)}) collective-permute-start(bf16[64,128,128]{2,1,0:T(8,128)(2,1)} %bitcast.7), channel_id=1, source_target_pairs={{1,0},{2,1},{3,2},{0,3},{5,4},{6,5},{7,6},{4,7},{9,8},{10,9},{11,1... | collective-permute-start | bytes 6291464 | tf_op jit(solution)/shard_map/ppermute | solution.py:20
  4.2 44.6 %collective-permute-start.1 = (bf16[64,128,128]{2,1,0:T(8,128)(2,1)}, bf16[64,128,128]{2,1,0:T(8,128)(2,1)}, u32[]{:S(2)}, u32[]{:S(2)}) collective-permute-start(bf16[64,128,128]{2,1,0:T(8,128)(2,1)} %bitcast.9), channel_id=1, source_target_pairs={{4,0},{8,4},{12,8},{16,12},{20,16},{24,20},{28,24},{0,28},{5,1},{9... | collective-permute-start | bytes 6291464 | tf_op jit(solution)/shard_map/ppermute | solution.py:20
  48.8 1.3 copy-start

commit v5 on v4

--- a/solution.py
+++ b/solution.py
@@ -11,7 +11,7 @@
 KBLK = 16
 COLB = 16
 COL_GROUP = 2
-ROW_GROUP = 2
+ROW_GROUP = 8
 
 
 def from_behind(block, axis, distance):
@@ -28,11 +28,11 @@
     lax.fori_loop(0, count, step, 0)
 
 
-def invert_places(places, base, index_ref, positions, stored):
+def invert_places(places, tile, index_ref, positions, stored):
     fill(index_ref, positions, -1)
 
     def step(n, carry):
-        index_ref[places[base + n]] = n
+        index_ref[places[tile[0], tile[1], n]] = n
         return carry
 
     lax.fori_loop(0, stored, step, 0)
@@ -83,16 +83,14 @@
 ):
     side = left_tile.shape[-1]
     stored = left_tile.shape[0]
-    tile_len = left_places.shape[0] // (rows_grid * cols_grid)
     row_here = lax.axis_index("row")
     col_here = lax.axis_index("col")
-    tile_here = (row_here * cols_grid + col_here) * tile_len
-    left_next = (row_here * cols_grid + lax.rem(col_here + 1, cols_grid)) * tile_len
-    right_next = (lax.rem(row_here + 1, rows_grid) * cols_grid + col_here) * tile_len
-    invert_places(left_places, tile_here, left_index, ROWB * KBLK, stored)
-    invert_places(right_places, tile_here, right_index, KBLK * COLB, stored)
-    invert_places(left_places, left_next, left_index_next, ROWB * KBLK, stored)
-    invert_places(right_places, right_next, right_index_next, KBLK * COLB, stored)
+    row_next = lax.rem(row_here + 1, rows_grid)
+    col_next = lax.rem(col_here + 1, cols_grid)
+    invert_places(left_places, (row_here, col_here), left_index, ROWB * KBLK, stored)
+    invert_places(right_places, (row_here, col_here), right_index, KBLK * COLB, stored)
+    invert_places(left_places, (row_here, col_next), left_index_next, ROWB * KBLK, stored)
+    invert_places(right_places, (row_next, col_here), right_index_next, KBLK * COLB, stored)
     fill(filled, filled.shape[0], 0)
     fill(counts, counts.shape[0], 0)
 
@@ -192,8 +190,6 @@
     smem = pl.BlockSpec(memory_space=pltpu.SMEM)
     vmem = pl.BlockSpec(memory_space=pltpu.VMEM)
     anywhere = pl.BlockSpec(memory_space=pl.ANY)
-    left_flat = left_places.reshape(-1)
-    right_flat = right_places.reshape(-1)
     work = [
         pltpu.VMEM((ROWB * side, KBLK * side), jnp.bfloat16),
         pltpu.VMEM((KBLK * side, COL_GROUP * side), jnp.bfloat16),
@@ -219,7 +215,7 @@
         ],
         compiler_params=pltpu.CompilerParams(vmem_limit_bytes=60 * 1024 * 1024),
         cost_estimate=pl.CostEstimate(flops=flops, bytes_accessed=tile_bytes + partial_bytes, transcendentals=0),
-    )(left_flat, right_flat, owners[0], left_here, right_here)
+    )(left_places, right_places, owners[0], left_here, right_here)
     outgoing = pl.pallas_call(
         second_kernel,
         out_shape=jax.ShapeDtypeStruct((slots, side, side), jnp.bfloat16),

time: 279 us -> 274 us (0.982)
  Pallas kernels: 60.2 us -> 50.5 us
  waiting for transfers between devices: 7.34 us -> 14.6 us
    ppermute x2, waiting for transfers between devices: 7.34 us -> 14.6 us  [from_behind(): return lax.ppermute(block, axis, route)]
    pallas_call x1, Pallas kernels: 26.7 us -> 21.4 us  [body(): pl.pallas_call(second_kernel, out_shape=jax.ShapeDtypeStruct((slots, side...]
    pallas_call x1, Pallas kernels: 33.5 us -> 29.1 us  [body(): pl.pallas_call(functools.partial(first_kernel, rows_grid, cols_grid, capa...]
  transfers between devices with their start and end apart: 2 -> 2, of which waited for: 1 -> 1; matrix products, arithmetic and copies ran while one was open for 1% -> 0% of each run, Pallas kernels for 12% -> 11%
where the time goes in v5:
time: 274 us
  blocking collectives  192 us (70%)
  Pallas kernels  50.5 us (18%)
  waiting for transfers between devices  14.6 us (5%)
  local copies, waits for them, and re-layouts  11.9 us (4%)
  starting transfers between devices  5.11 us (2%)
    all_to_all x1, blocking collectives, body(): lax.all_to_all(outgoing, ('row', 'col'), split_axis=0, concat_axis=0, til...  192 us
    pallas_call x1, Pallas kernels, body(): pl.pallas_call(functools.partial(first_kernel, rows_grid, cols_grid, capa...  29.1 us
    pallas_call x1, Pallas kernels, body(): pl.pallas_call(second_kernel, out_shape=jax.ShapeDtypeStruct((slots, side...  21.4 us
    ppermute x2, waiting for transfers between devices, from_behind(): return lax.ppermute(block, axis, route)  14.6 us
    unnamed x3, local copies, waits for them, and re-layouts  11.9 us
  transfers between devices with their start and end apart: 2, of which 1 were waited for; matrix products, arithmetic and copies ran while one was open for 0% of the time, Pallas kernels for 11%

profile of v5, /device:TPU:1, one launch (start us, length us, event | category | flops | bytes accessed | tf_op | source)
XLA Modules:
  0.0 273.7 jit_solution(504309010771310580)
XLA Ops:
  0.0 4.2 %collective-permute-start = (bf16[64,128,128]{2,1,0:T(8,128)(2,1)}, bf16[64,128,128]{2,1,0:T(8,128)(2,1)S(1)}, u32[]{:S(2)}, u32[]{:S(2)}) collective-permute-start(bf16[64,128,128]{2,1,0:T(8,128)(2,1)} %bitcast.7), channel_id=1, source_target_pairs={{1,0},{2,1},{3,2},{0,3},{5,4},{6,5},{7,6},{4,7},{9,8},{10,9},{11,1... | collective-permute-start | bytes 6291464 | tf_op jit(solution)/shard_map/ppermute | solution.py:20
  4.2 1.0 collective-permute-start.1
  5.1 29.1 %shard_map.55 = (f32[8,1024,256]{2,1,0:T(8,128)}, s32[128]{0:T(128)}, s32[256]{0:T(256)}, s32[128]{0:T(128)}, s32[256]{0:T(256)}) custom-call(s32[8,4,64]{2,1,0:T(4,128)} %left_places.1, s32[8,4,64]{2,1,0:T(4,128)} %right_places.1, s32[128]{0:T(128)} %bitcast.11, bf16[64,128,128]{2,1,0:T(8,128)(2,1)} %bitcast.8, bf16[64,128,128]{2,1,0:T(8,128)(2,1)} %bitcast.10), custom_call_target="tpu_custom_call" | custom-call | flops 8589934592 | bytes 12582912 | tf_op jit(solution)/shard_map/pallas_call | solution.py:200
  34.2 14.6 %collective-permute-done.left_tile = bf16[64,128,128]{2,1,0:T(8,128)(2,1)S(1)} collective-permute-done((bf16[64,128,128]{2,1,0:T(8,128)(2,1)}, bf16[64,128,128]{2,1,0:T(8,128)(2,1)S(1)}, u32[]{:S(2)}, u32[]{:S(2)}) %collective-permute-start) | collective-permute-done | bytes 2097184 | tf_op jit(solution)/shard_map/ppermute | solution.py:20
  48.8 0.0 copy-start
  48.8 0.0 collective-permute-done.1.right_tile
  48.8 1.3 copy-done
  50.1 21.4 %shard_map.56 = bf16[256,128,128]{2,1,0:T(8,128)(2,1)} custom-call(s32[128]{0:T(128)} %get-tuple-element.10.slot_of, s32[256]{0:T(256)} %get-tuple-element.11.filled, s32[128]{0:T(128)} %get-tuple-element.12.left_index, s32[256]{0:T(256)} %get-tuple-element.13.right_index, bf16[64,128,128]{2,1,0:T(8,128)(2,1)} %copy-done, ...), custom_call_target="tpu_custom_call" | custom-call | flops 8589934592 | bytes 20971520 | tf_op jit(solution)/shard_map/pallas_call | solution.py:219
  71.5 191.7 %all_to_all.5 = bf16[32,8,128,128]{3,2,1,0:T(8,128)(2,1)} all-to-all(bf16[32,8,128,128]{3,2,1,0:T(8,128)(2,1)} %bitcast.6), channel_id=1, replica_groups=mesh['row'=8,'col'=4] {'row','col'}, dimensions={0} | all-to-all | bytes 16777216 | tf_op jit(solution)/shard_map/all_to_all | solution.py:237
  263.2 10.5 %copy.7 = bf16[1,32,8,128,128]{4,3,2,1,0:T(8,128)(2,1)} copy(bf16[1,32,8,128,128]{4,3,2,1,0:T(8,128)(2,1)} %bitcast.5) | data formatting | bytes 16777216
Async XLA Ops:
  0.0 48.8 %collective-permute-start = (bf16[64,128,128]{2,1,0:T(8,128)(2,1)}, bf16[64,128,128]{2,1,0:T(8,128)(2,1)S(1)}, u32[]{:S(2)}, u32[]{:S(2)}) collective-permute-start(bf16[64,128,128]{2,1,0:T(8,128)(2,1)} %bitcast.7), channel_id=1, source_target_pairs={{1,0},{2,1},{3,2},{0,3},{5,4},{6,5},{7,6},{4,7},{9,8},{10,9},{11,1... | collective-permute-start | bytes 6291464 | tf_op jit(solution)/shard_map/ppermute | solution.py:20
  4.2 44.6 %collective-permute-start.1 = (bf16[64,128,128]{2,1,0:T(8,128)(2,1)}, bf16[64,128,128]{2,1,0:T(8,128)(2,1)}, u32[]{:S(2)}, u32[]{:S(2)}) collective-permute-start(bf16[64,128,128]{2,1,0:T(8,128)(2,1)} %bitcast.9), channel_id=1, source_target_pairs={{4,0},{8,4},{12,8},{16,12},{20,16},{24,20},{28,24},{0,28},{5,1},{9... | collective-permute-start | bytes 6291464 | tf_op jit(solution)/shard_map/ppermute | solution.py:20
  48.8 1.4 copy-start

commit v6 on v5

--- a/solution.py
+++ b/solution.py
@@ -52,16 +52,22 @@
 
     lax.fori_loop(0, ROWB, densify_left, 0)
 
+    right_column[...] = jnp.zeros(right_column.shape, right_column.dtype)
+
+    def place_column(cp, clear):
+        for k in range(KBLK):
+            for cc in range(COL_GROUP):
+                index = right_index[k * COLB + cp * COL_GROUP + cc]
+
+                @pl.when(index >= 0)
+                def _():
+                    block = zero_block if clear else right_tile[index]
+                    right_column[k * side:(k + 1) * side, cc * side:(cc + 1) * side] = block
+
     def column_pair(cp, carry):
         if before is not None:
             before(cp)
-        for k in range(KBLK):
-            for cc in range(COL_GROUP):
-                index = right_index[k * COLB + cp * COL_GROUP + cc]
-                block = right_tile[jnp.maximum(index, 0)]
-                right_column[k * side:(k + 1) * side, cc * side:(cc + 1) * side] = jnp.where(
-                    index >= 0, block, zero_block
-                )
+        place_column(cp, False)
 
         def row_pair(rp, inner):
             rows = pl.ds(pl.multiple_of(rp * ROW_GROUP * side, ROW_GROUP * side), ROW_GROUP * side)
@@ -70,6 +76,7 @@
             return inner
 
         lax.fori_loop(0, ROWB // ROW_GROUP, row_pair, 0)
+        place_column(cp, True)
         return carry
 
     lax.fori_loop(0, COLB // COL_GROUP, column_pair, 0)
@@ -78,8 +85,8 @@
 def first_kernel(
     rows_grid, cols_grid, capacity,
     left_places, right_places, owners, left_tile, right_tile,
-    partial, slot_of, filled, left_index_next, right_index_next,
-    left_dense, right_column, left_index, right_index, counts,
+    partial, slot_of, left_index_next, right_index_next, outgoing,
+    left_dense, right_column, left_index, right_index, counts, filled, zero_ref, zero_sems,
 ):
     side = left_tile.shape[-1]
     stored = left_tile.shape[0]
@@ -104,43 +111,51 @@
         return carry
 
     lax.fori_loop(0, ROWB * COLB, assign, 0)
+    zero_ref[...] = jnp.zeros(zero_ref.shape, zero_ref.dtype)
+
+    def zero_slot(s, carry):
+        @pl.when(filled[s] == 0)
+        def _():
+            pltpu.make_async_copy(zero_ref, outgoing.at[s], zero_sems.at[s]).start()
+
+        return carry
+
+    lax.fori_loop(0, outgoing.shape[0], zero_slot, 0)
 
     def emit(rp, cp, rows, result):
         partial[cp, rows, :] = result
 
     multiply_tiles(left_tile, right_tile, left_index, right_index, left_dense, right_column, emit)
 
+    def wait_slot(s, carry):
+        @pl.when(filled[s] == 0)
+        def _():
+            pltpu.make_async_copy(zero_ref, outgoing.at[s], zero_sems.at[s]).wait()
+
+        return carry
+
+    lax.fori_loop(0, outgoing.shape[0], wait_slot, 0)
+
 
 def second_kernel(
-    slot_of, filled, left_index, right_index, left_tile, right_tile, partial,
+    slot_of, left_index, right_index, left_tile, right_tile, partial, outgoing,
     out,
-    left_dense, right_column, partial_buf, staging, zero_ref, partial_sems, out_sems,
+    left_dense, right_column, partial_buf, staging, partial_sems, out_sems,
 ):
     side = left_tile.shape[-1]
     pairs = COLB // COL_GROUP
-    slots = out.shape[0]
-    zero_ref[...] = jnp.zeros(zero_ref.shape, zero_ref.dtype)
+    products = ROWB * COLB
 
     def partial_copy(cp, buffer):
         return pltpu.make_async_copy(partial.at[cp], partial_buf.at[buffer], partial_sems.at[buffer])
 
     partial_copy(0, 0).start()
-
-    def zero_slot(s, carry):
-        @pl.when(filled[s] == 0)
-        def _():
-            pltpu.make_async_copy(zero_ref, out.at[s], out_sems.at[s]).start()
-
-        return carry
-
-    lax.fori_loop(0, slots, zero_slot, 0)
 
     def send_pair(cp):
         for r in range(ROWB):
             for cc in range(COL_GROUP):
                 m = r * COLB + cp * COL_GROUP + cc
-                slot = slot_of[m]
-                pltpu.make_async_copy(staging.at[m], out.at[slot], out_sems.at[slot]).start()
+                pltpu.make_async_copy(staging.at[m], out.at[slot_of[m]], out_sems.at[m]).start()
 
     def before(cp):
         buffer = lax.rem(cp, 2)
@@ -167,11 +182,11 @@
     multiply_tiles(left_tile, right_tile, left_index, right_index, left_dense, right_column, emit, before)
     send_pair(pairs - 1)
 
-    def wait_slot(s, carry):
-        pltpu.make_async_copy(zero_ref, out.at[s], out_sems.at[s]).wait()
-        return carry
-
-    lax.fori_loop(0, slots, wait_slot, 0)
+    def wait_block(m, carry):
+        pltpu.make_async_copy(staging.at[m], out.at[slot_of[m]], out_sems.at[m]).wait()
+        return carry
+
+    lax.fori_loop(0, products, wait_block, 0)
 
 
 def body(left_values, left_places, right_values, right_places, owners):
@@ -197,21 +212,24 @@
     flops = 2 * (ROWB * side) * (KBLK * side) * (COLB * side)
     tile_bytes = 2 * left_here.size * 2
     partial_bytes = ROWB * COLB * side * side * 4
-    partial, slot_of, filled, left_index, right_index = pl.pallas_call(
+    partial, slot_of, left_index, right_index, outgoing = pl.pallas_call(
         functools.partial(first_kernel, rows_grid, cols_grid, capacity),
         out_shape=(
             jax.ShapeDtypeStruct((pairs, ROWB * side, COL_GROUP * side), jnp.float32),
             jax.ShapeDtypeStruct((products,), jnp.int32),
-            jax.ShapeDtypeStruct((slots,), jnp.int32),
             jax.ShapeDtypeStruct((ROWB * KBLK,), jnp.int32),
             jax.ShapeDtypeStruct((KBLK * COLB,), jnp.int32),
+            jax.ShapeDtypeStruct((slots, side, side), jnp.bfloat16),
         ),
         in_specs=[smem, smem, smem, vmem, vmem],
-        out_specs=(vmem, smem, smem, smem, smem),
+        out_specs=(vmem, smem, smem, smem, anywhere),
         scratch_shapes=work + [
             pltpu.SMEM((ROWB * KBLK,), jnp.int32),
             pltpu.SMEM((KBLK * COLB,), jnp.int32),
             pltpu.SMEM((devices_all,), jnp.int32),
+            pltpu.SMEM((slots,), jnp.int32),
+            pltpu.VMEM((side, side), jnp.bfloat16),
+            pltpu.SemaphoreType.DMA((slots,)),
         ],
         compiler_params=pltpu.CompilerParams(vmem_limit_bytes=60 * 1024 * 1024),
         cost_estimate=pl.CostEstimate(flops=flops, bytes_accessed=tile_bytes + partial_bytes, transcendentals=0),
@@ -219,20 +237,20 @@
     outgoing = pl.pallas_call(
         second_kernel,
         out_shape=jax.ShapeDtypeStruct((slots, side, side), jnp.bfloat16),
-        in_specs=[smem, smem, smem, smem, vmem, vmem, anywhere],
+        in_specs=[smem, smem, smem, vmem, vmem, anywhere, anywhere],
         out_specs=anywhere,
+        input_output_aliases={6: 0},
         scratch_shapes=work + [
             pltpu.VMEM((2, ROWB * side, COL_GROUP * side), jnp.float32),
             pltpu.VMEM((products, side, side), jnp.bfloat16),
-            pltpu.VMEM((side, side), jnp.bfloat16),
             pltpu.SemaphoreType.DMA((2,)),
-            pltpu.SemaphoreType.DMA((slots,)),
+            pltpu.SemaphoreType.DMA((products,)),
         ],
         compiler_params=pltpu.CompilerParams(vmem_limit_bytes=60 * 1024 * 1024),
         cost_estimate=pl.CostEstimate(
             flops=flops, bytes_accessed=tile_bytes + partial_bytes + slots * side * side * 2, transcendentals=0
         ),
-    )(slot_of, filled, left_index, right_index, left_next, right_next, partial)
+    )(slot_of, left_index, right_index, left_next, right_next, partial, outgoing)
     outgoing = outgoing.reshape(devices_all, capacity, side, side)
     received = lax.all_to_all(outgoing, ("row", "col"), split_axis=0, concat_axis=0, tiled=True)
     return received[None]

time: 274 us -> 273 us (level)
  waiting for transfers between devices: 14.6 us -> 4.54 us
  Pallas kernels: 50.5 us -> 60 us
    pallas_call x1, Pallas kernels: 29.1 us -> 39.1 us  [body(): pl.pallas_call(functools.partial(first_kernel, rows_grid, cols_grid, capa...]
    ppermute x2, waiting for transfers between devices: 14.6 us -> 4.54 us  [from_behind(): return lax.ppermute(block, axis, route)]
  transfers between devices with their start and end apart: 2 -> 2, of which waited for: 1 -> 1; matrix products, arithmetic and copies ran while one was open for 0% -> 0% of each run, Pallas kernels for 11% -> 14%
where the time goes in v6:
time: 273 us
  blocking collectives  191 us (70%)
  Pallas kernels  60 us (22%)
  local copies, waits for them, and re-layouts  11.9 us (4%)
  starting transfers between devices  5.11 us (2%)
  waiting for transfers between devices  4.54 us (2%)
    all_to_all x1, blocking collectives, body(): lax.all_to_all(outgoing, ('row', 'col'), split_axis=0, concat_axis=0, til...  191 us
    pallas_call x1, Pallas kernels, body(): pl.pallas_call(functools.partial(first_kernel, rows_grid, cols_grid, capa...  39.1 us
    pallas_call x1, Pallas kernels, body(): pl.pallas_call(second_kernel, out_shape=jax.ShapeDtypeStruct((slots, side...  20.8 us
    unnamed x3, local copies, waits for them, and re-layouts  11.9 us
  transfers between devices with their start and end apart: 2, of which 1 were waited for; matrix products, arithmetic and copies ran while one was open for 0% of the time, Pallas kernels for 14%

profile of v6, /device:TPU:1, one launch (start us, length us, event | category | flops | bytes accessed | tf_op | source)
XLA Modules:
  0.0 273.0 jit_solution(17121556217014001529)
XLA Ops:
  0.0 4.2 %collective-permute-start = (bf16[64,128,128]{2,1,0:T(8,128)(2,1)}, bf16[64,128,128]{2,1,0:T(8,128)(2,1)S(1)}, u32[]{:S(2)}, u32[]{:S(2)}) collective-permute-start(bf16[64,128,128]{2,1,0:T(8,128)(2,1)} %bitcast.7), channel_id=1, source_target_pairs={{1,0},{2,1},{3,2},{0,3},{5,4},{6,5},{7,6},{4,7},{9,8},{10,9},{11,1... | collective-permute-start | bytes 6291464 | tf_op jit(solution)/shard_map/ppermute | solution.py:20
  4.2 1.0 collective-permute-start.1
  5.1 39.1 %shard_map.55 = (f32[8,1024,256]{2,1,0:T(8,128)}, s32[128]{0:T(128)}, s32[128]{0:T(128)}, s32[256]{0:T(256)}, bf16[256,128,128]{2,1,0:T(8,128)(2,1)}) custom-call(s32[8,4,64]{2,1,0:T(4,128)} %left_places.1, s32[8,4,64]{2,1,0:T(4,128)} %right_places.1, s32[128]{0:T(128)} %bitcast.11, bf16[64,128,128]{2,1,0:T(8,128)(2,1)} %bitcast.8, ...), custom_call_target="tpu_custom_call" | custom-call | flops 8589934592 | bytes 12582912 | tf_op jit(solution)/shard_map/pallas_call | solution.py:215
  44.2 4.5 %collective-permute-done.left_tile = bf16[64,128,128]{2,1,0:T(8,128)(2,1)S(1)} collective-permute-done((bf16[64,128,128]{2,1,0:T(8,128)(2,1)}, bf16[64,128,128]{2,1,0:T(8,128)(2,1)S(1)}, u32[]{:S(2)}, u32[]{:S(2)}) %collective-permute-start) | collective-permute-done | bytes 2097184 | tf_op jit(solution)/shard_map/ppermute | solution.py:20
  48.8 0.0 copy-start
  48.8 0.0 collective-permute-done.1.right_tile
  48.8 1.3 copy-done
  50.1 20.8 %shard_map.56 = bf16[256,128,128]{2,1,0:T(8,128)(2,1)} custom-call(s32[128]{0:T(128)} %get-tuple-element.10.slot_of, s32[128]{0:T(128)} %get-tuple-element.11.left_index, s32[256]{0:T(256)} %get-tuple-element.12.right_index, bf16[64,128,128]{2,1,0:T(8,128)(2,1)} %copy-done, ...), custom_call_target="tpu_custom_call", output_to_operand_aliasing={{}: (6, {})} | custom-call | flops 8589934592 | bytes 20971520 | tf_op jit(solution)/shard_map/pallas_call | solution.py:237
  71.0 191.5 %all_to_all.5 = bf16[32,8,128,128]{3,2,1,0:T(8,128)(2,1)} all-to-all(bf16[32,8,128,128]{3,2,1,0:T(8,128)(2,1)} %bitcast.6), channel_id=1, replica_groups=mesh['row'=8,'col'=4] {'row','col'}, dimensions={0} | all-to-all | bytes 16777216 | tf_op jit(solution)/shard_map/all_to_all | solution.py:255
  262.4 10.5 %copy.9 = bf16[1,32,8,128,128]{4,3,2,1,0:T(8,128)(2,1)} copy(bf16[1,32,8,128,128]{4,3,2,1,0:T(8,128)(2,1)} %bitcast.5) | data formatting | bytes 16777216
Async XLA Ops:
  0.0 48.8 %collective-permute-start = (bf16[64,128,128]{2,1,0:T(8,128)(2,1)}, bf16[64,128,128]{2,1,0:T(8,128)(2,1)S(1)}, u32[]{:S(2)}, u32[]{:S(2)}) collective-permute-start(bf16[64,128,128]{2,1,0:T(8,128)(2,1)} %bitcast.7), channel_id=1, source_target_pairs={{1,0},{2,1},{3,2},{0,3},{5,4},{6,5},{7,6},{4,7},{9,8},{10,9},{11,1... | collective-permute-start | bytes 6291464 | tf_op jit(solution)/shard_map/ppermute | solution.py:20
  4.2 44.6 %collective-permute-start.1 = (bf16[64,128,128]{2,1,0:T(8,128)(2,1)}, bf16[64,128,128]{2,1,0:T(8,128)(2,1)}, u32[]{:S(2)}, u32[]{:S(2)}) collective-permute-start(bf16[64,128,128]{2,1,0:T(8,128)(2,1)} %bitcast.9), channel_id=1, source_target_pairs={{4,0},{8,4},{12,8},{16,12},{20,16},{24,20},{28,24},{0,28},{5,1},{9... | collective-permute-start | bytes 6291464 | tf_op jit(solution)/shard_map/ppermute | solution.py:20
  48.8 1.4 copy-start

commit v7 on v6

--- a/solution.py
+++ b/solution.py
@@ -12,6 +12,7 @@
 COLB = 16
 COL_GROUP = 2
 ROW_GROUP = 8
+COPY_STEPS = 8
 
 
 def from_behind(block, axis, distance):
@@ -187,6 +188,10 @@
         return carry
 
     lax.fori_loop(0, products, wait_block, 0)
+
+
+def pass_through(source, target):
+    target[...] = source[...]
 
 
 def body(left_values, left_places, right_values, right_places, owners):
@@ -253,6 +258,16 @@
     )(slot_of, left_index, right_index, left_next, right_next, partial, outgoing)
     outgoing = outgoing.reshape(devices_all, capacity, side, side)
     received = lax.all_to_all(outgoing, ("row", "col"), split_axis=0, concat_axis=0, tiled=True)
+    chunk = devices_all // COPY_STEPS
+    block = pl.BlockSpec((chunk, capacity, side, side), lambda i: (i, 0, 0, 0))
+    received = pl.pallas_call(
+        pass_through,
+        out_shape=jax.ShapeDtypeStruct(received.shape, received.dtype),
+        grid=(COPY_STEPS,),
+        in_specs=[block],
+        out_specs=block,
+        cost_estimate=pl.CostEstimate(flops=0, bytes_accessed=2 * received.size * 2, transcendentals=0),
+    )(received)
     return received[None]
 
 

time: 273 us -> 272 us (level)
  local copies, waits for them, and re-layouts: 11.9 us -> 1.35 us
  Pallas kernels: 60 us -> 68.9 us
    unnamed x3 -> x2, local copies, waits for them, and re-layouts: 11.9 us -> 1.35 us
    pallas_call x0 -> x1, Pallas kernels: none -> 8.95 us  [body(): pl.pallas_call(pass_through, out_shape=jax.ShapeDtypeStruct(received.shap...]
where the time goes in v7:
time: 272 us; the launch traced here: 271 us
  blocking collectives  191 us (70%)
  Pallas kernels  68.9 us (25%)
  starting transfers between devices  5.11 us (2%)
  waiting for transfers between devices  4.54 us (2%)
    all_to_all x1, blocking collectives, body(): lax.all_to_all(outgoing, ('row', 'col'), split_axis=0, concat_axis=0, til...  191 us
    pallas_call x1, Pallas kernels, body(): pl.pallas_call(functools.partial(first_kernel, rows_grid, cols_grid, capa...  39.1 us
    pallas_call x1, Pallas kernels, body(): pl.pallas_call(second_kernel, out_shape=jax.ShapeDtypeStruct((slots, side...  20.8 us
    pallas_call x1, Pallas kernels, body(): pl.pallas_call(pass_through, out_shape=jax.ShapeDtypeStruct(received.shap...  8.95 us
  transfers between devices with their start and end apart: 2, of which 1 were waited for; matrix products, arithmetic and copies ran while one was open for 0% of the time, Pallas kernels for 14%

profile of v7, /device:TPU:1, one launch (start us, length us, event | category | flops | bytes accessed | tf_op | source)
XLA Modules:
  0.0 271.4 jit_solution(4664162649010853184)
XLA Ops:
  0.0 4.2 %collective-permute-start = (bf16[64,128,128]{2,1,0:T(8,128)(2,1)}, bf16[64,128,128]{2,1,0:T(8,128)(2,1)S(1)}, u32[]{:S(2)}, u32[]{:S(2)}) collective-permute-start(bf16[64,128,128]{2,1,0:T(8,128)(2,1)} %bitcast.6), channel_id=1, source_target_pairs={{1,0},{2,1},{3,2},{0,3},{5,4},{6,5},{7,6},{4,7},{9,8},{10,9},{11,1... | collective-permute-start | bytes 6291464 | tf_op jit(solution)/shard_map/ppermute | solution.py:21
  4.2 1.0 collective-permute-start.1
  5.1 39.1 %shard_map.55 = (f32[8,1024,256]{2,1,0:T(8,128)}, s32[128]{0:T(128)}, s32[128]{0:T(128)}, s32[256]{0:T(256)}, bf16[256,128,128]{2,1,0:T(8,128)(2,1)}) custom-call(s32[8,4,64]{2,1,0:T(4,128)} %left_places.1, s32[8,4,64]{2,1,0:T(4,128)} %right_places.1, s32[128]{0:T(128)} %bitcast.10, bf16[64,128,128]{2,1,0:T(8,128)(2,1)} %bitcast.7, bf16[64,128,128]{2,1,0:T(8,128)(2,1)} %bitcast.9), custom_call_target="tpu_custom_call" | custom-call | flops 8589934592 | bytes 12582912 | tf_op jit(solution)/shard_map/pallas_call | solution.py:220
  44.2 4.5 %collective-permute-done.left_tile = bf16[64,128,128]{2,1,0:T(8,128)(2,1)S(1)} collective-permute-done((bf16[64,128,128]{2,1,0:T(8,128)(2,1)}, bf16[64,128,128]{2,1,0:T(8,128)(2,1)S(1)}, u32[]{:S(2)}, u32[]{:S(2)}) %collective-permute-start) | collective-permute-done | bytes 2097184 | tf_op jit(solution)/shard_map/ppermute | solution.py:21
  48.8 0.0 copy-start
  48.8 0.0 collective-permute-done.1.right_tile
  48.8 1.3 copy-done
  50.1 20.8 %shard_map.56 = bf16[256,128,128]{2,1,0:T(8,128)(2,1)} custom-call(s32[128]{0:T(128)} %get-tuple-element.10.slot_of, s32[128]{0:T(128)} %get-tuple-element.11.left_index, s32[256]{0:T(256)} %get-tuple-element.12.right_index, bf16[64,128,128]{2,1,0:T(8,128)(2,1)} %copy-done, ...), custom_call_target="tpu_custom_call", output_to_operand_aliasing={{}: (6, {})} | custom-call | flops 8589934592 | bytes 20971520 | tf_op jit(solution)/shard_map/pallas_call | solution.py:242
  71.0 191.5 %all_to_all.5.source = bf16[32,8,128,128]{3,2,1,0:T(8,128)(2,1)} all-to-all(bf16[32,8,128,128]{3,2,1,0:T(8,128)(2,1)} %bitcast.5), channel_id=1, replica_groups=mesh['row'=8,'col'=4] {'row','col'}, dimensions={0} | all-to-all | bytes 16777216 | tf_op jit(solution)/shard_map/all_to_all | solution.py:260
  262.4 8.9 %shard_map.57 = bf16[32,8,128,128]{3,2,1,0:T(8,128)(2,1)} custom-call(bf16[32,8,128,128]{3,2,1,0:T(8,128)(2,1)} %all_to_all.5.source), custom_call_target="tpu_custom_call" | custom-call | bytes 16777216 | tf_op jit(solution)/shard_map/pallas_call | solution.py:263
Async XLA Ops:
  0.0 48.8 %collective-permute-start = (bf16[64,128,128]{2,1,0:T(8,128)(2,1)}, bf16[64,128,128]{2,1,0:T(8,128)(2,1)S(1)}, u32[]{:S(2)}, u32[]{:S(2)}) collective-permute-start(bf16[64,128,128]{2,1,0:T(8,128)(2,1)} %bitcast.6), channel_id=1, source_target_pairs={{1,0},{2,1},{3,2},{0,3},{5,4},{6,5},{7,6},{4,7},{9,8},{10,9},{11,1... | collective-permute-start | bytes 6291464 | tf_op jit(solution)/shard_map/ppermute | solution.py:21
  4.2 44.6 %collective-permute-start.1 = (bf16[64,128,128]{2,1,0:T(8,128)(2,1)}, bf16[64,128,128]{2,1,0:T(8,128)(2,1)}, u32[]{:S(2)}, u32[]{:S(2)}) collective-permute-start(bf16[64,128,128]{2,1,0:T(8,128)(2,1)} %bitcast.8), channel_id=1, source_target_pairs={{4,0},{8,4},{12,8},{16,12},{20,16},{24,20},{28,24},{0,28},{5,1},{9... | collective-permute-start | bytes 6291464 | tf_op jit(solution)/shard_map/ppermute | solution.py:21
  48.8 1.4 copy-start

commit v8 on v7

--- a/solution.py
+++ b/solution.py
@@ -12,7 +12,7 @@
 COLB = 16
 COL_GROUP = 2
 ROW_GROUP = 8
-COPY_STEPS = 8
+COPY_STEPS = 32
 
 
 def from_behind(block, axis, distance):
@@ -39,9 +39,15 @@
     lax.fori_loop(0, stored, step, 0)
 
 
-def multiply_tiles(left_tile, right_tile, left_index, right_index, left_dense, right_column, emit, before=None):
+def multiply_tiles(
+    left_tile, right_tile, left_index, right_index, left_dense, right_column, emit, before=None,
+    left_ready=None, right_ready=None,
+):
     side = left_tile.shape[-1]
     zero_block = jnp.zeros((side, side), left_tile.dtype)
+    right_column[...] = jnp.zeros(right_column.shape, right_column.dtype)
+    if left_ready is not None:
+        left_ready()
 
     def densify_left(r, carry):
         rows = pl.ds(pl.multiple_of(r * side, side), side)
@@ -52,8 +58,8 @@
         return carry
 
     lax.fori_loop(0, ROWB, densify_left, 0)
-
-    right_column[...] = jnp.zeros(right_column.shape, right_column.dtype)
+    if right_ready is not None:
+        right_ready()
 
     def place_column(cp, clear):
         for k in range(KBLK):
@@ -139,13 +145,17 @@
 
 
 def second_kernel(
-    slot_of, left_index, right_index, left_tile, right_tile, partial, outgoing,
+    slot_of, left_index, right_index, left_hbm, right_hbm, partial, outgoing,
     out,
-    left_dense, right_column, partial_buf, staging, partial_sems, out_sems,
+    left_dense, right_column, partial_buf, staging, left_tile, right_tile, partial_sems, out_sems, tile_sems,
 ):
     side = left_tile.shape[-1]
     pairs = COLB // COL_GROUP
     products = ROWB * COLB
+    left_copy = pltpu.make_async_copy(left_hbm, left_tile, tile_sems.at[0])
+    right_copy = pltpu.make_async_copy(right_hbm, right_tile, tile_sems.at[1])
+    left_copy.start()
+    right_copy.start()
 
     def partial_copy(cp, buffer):
         return pltpu.make_async_copy(partial.at[cp], partial_buf.at[buffer], partial_sems.at[buffer])
@@ -180,7 +190,10 @@
                 piece = total[rr * side:(rr + 1) * side, cc * side:(cc + 1) * side]
                 staging[m] = piece.astype(staging.dtype)
 
-    multiply_tiles(left_tile, right_tile, left_index, right_index, left_dense, right_column, emit, before)
+    multiply_tiles(
+        left_tile, right_tile, left_index, right_index, left_dense, right_column, emit, before,
+        left_copy.wait, right_copy.wait,
+    )
     send_pair(pairs - 1)
 
     def wait_block(m, carry):
@@ -242,14 +255,17 @@
     outgoing = pl.pallas_call(
         second_kernel,
         out_shape=jax.ShapeDtypeStruct((slots, side, side), jnp.bfloat16),
-        in_specs=[smem, smem, smem, vmem, vmem, anywhere, anywhere],
+        in_specs=[smem, smem, smem, anywhere, anywhere, anywhere, anywhere],
         out_specs=anywhere,
         input_output_aliases={6: 0},
         scratch_shapes=work + [
             pltpu.VMEM((2, ROWB * side, COL_GROUP * side), jnp.float32),
             pltpu.VMEM((products, side, side), jnp.bfloat16),
+            pltpu.VMEM(left_here.shape, left_here.dtype),
+            pltpu.VMEM(right_here.shape, right_here.dtype),
             pltpu.SemaphoreType.DMA((2,)),
             pltpu.SemaphoreType.DMA((products,)),
+            pltpu.SemaphoreType.DMA((2,)),
         ],
         compiler_params=pltpu.CompilerParams(vmem_limit_bytes=60 * 1024 * 1024),
         cost_estimate=pl.CostEstimate(

time: 272 us -> 282 us (1.037)
  Pallas kernels: 68.9 us -> 79.1 us
    pallas_call x1, Pallas kernels: 8.95 us -> 19.1 us  [body(): pl.pallas_call(pass_through, out_shape=jax.ShapeDtypeStruct(received.shap...]
where the time goes in v8:
time: 282 us
  blocking collectives  191 us (68%)
  Pallas kernels  79.1 us (28%)
  starting transfers between devices  5.11 us (2%)
  waiting for transfers between devices  4.54 us (2%)
    all_to_all x1, blocking collectives, body(): lax.all_to_all(outgoing, ('row', 'col'), split_axis=0, concat_axis=0, til...  191 us
    pallas_call x1, Pallas kernels, body(): pl.pallas_call(functools.partial(first_kernel, rows_grid, cols_grid, capa...  39.1 us
    pallas_call x1, Pallas kernels, body(): pl.pallas_call(second_kernel, out_shape=jax.ShapeDtypeStruct((slots, side...  20.8 us
    pallas_call x1, Pallas kernels, body(): pl.pallas_call(pass_through, out_shape=jax.ShapeDtypeStruct(received.shap...  19.1 us
  transfers between devices with their start and end apart: 2, of which 1 were waited for; matrix products, arithmetic and copies ran while one was open for 0% of the time, Pallas kernels for 14%

profile of v8, /device:TPU:1, one launch (start us, length us, event | category | flops | bytes accessed | tf_op | source)
XLA Modules:
  0.0 281.6 jit_solution(14052945229565395675)
XLA Ops:
  0.0 4.2 %collective-permute-start = (bf16[64,128,128]{2,1,0:T(8,128)(2,1)}, bf16[64,128,128]{2,1,0:T(8,128)(2,1)S(1)}, u32[]{:S(2)}, u32[]{:S(2)}) collective-permute-start(bf16[64,128,128]{2,1,0:T(8,128)(2,1)} %bitcast.6), channel_id=1, source_target_pairs={{1,0},{2,1},{3,2},{0,3},{5,4},{6,5},{7,6},{4,7},{9,8},{10,9},{11,1... | collective-permute-start | bytes 6291464 | tf_op jit(solution)/shard_map/ppermute | solution.py:21
  4.2 1.0 collective-permute-start.1
  5.1 39.1 %shard_map.55 = (f32[8,1024,256]{2,1,0:T(8,128)}, s32[128]{0:T(128)}, s32[128]{0:T(128)}, s32[256]{0:T(256)}, bf16[256,128,128]{2,1,0:T(8,128)(2,1)}) custom-call(s32[8,4,64]{2,1,0:T(4,128)} %left_places.1, s32[8,4,64]{2,1,0:T(4,128)} %right_places.1, s32[128]{0:T(128)} %bitcast.10, bf16[64,128,128]{2,1,0:T(8,128)(2,1)} %bitcast.7, bf16[64,128,128]{2,1,0:T(8,128)(2,1)} %bitcast.9), custom_call_target="tpu_custom_call" | custom-call | flops 8589934592 | bytes 12582912 | tf_op jit(solution)/shard_map/pallas_call | solution.py:233
  44.2 4.5 %collective-permute-done.left_hbm = bf16[64,128,128]{2,1,0:T(8,128)(2,1)S(1)} collective-permute-done((bf16[64,128,128]{2,1,0:T(8,128)(2,1)}, bf16[64,128,128]{2,1,0:T(8,128)(2,1)S(1)}, u32[]{:S(2)}, u32[]{:S(2)}) %collective-permute-start) | collective-permute-done | bytes 2097184 | tf_op jit(solution)/shard_map/ppermute | solution.py:21
  48.8 0.0 copy-start
  48.8 0.0 collective-permute-done.1.right_hbm
  48.8 1.3 copy-done
  50.1 20.8 %shard_map.56 = bf16[256,128,128]{2,1,0:T(8,128)(2,1)} custom-call(s32[128]{0:T(128)} %get-tuple-element.10.slot_of, s32[128]{0:T(128)} %get-tuple-element.11.left_index, s32[256]{0:T(256)} %get-tuple-element.12.right_index, bf16[64,128,128]{2,1,0:T(8,128)(2,1)} %copy-done, ...), custom_call_target="tpu_custom_call", output_to_operand_aliasing={{}: (6, {})} | custom-call | flops 8589934592 | bytes 20971520 | tf_op jit(solution)/shard_map/pallas_call | solution.py:255
  71.0 191.5 %all_to_all.5.source = bf16[32,8,128,128]{3,2,1,0:T(8,128)(2,1)} all-to-all(bf16[32,8,128,128]{3,2,1,0:T(8,128)(2,1)} %bitcast.5), channel_id=1, replica_groups=mesh['row'=8,'col'=4] {'row','col'}, dimensions={0} | all-to-all | bytes 16777216 | tf_op jit(solution)/shard_map/all_to_all | solution.py:276
  262.5 19.1 %shard_map.57 = bf16[32,8,128,128]{3,2,1,0:T(8,128)(2,1)} custom-call(bf16[32,8,128,128]{3,2,1,0:T(8,128)(2,1)} %all_to_all.5.source), custom_call_target="tpu_custom_call" | custom-call | bytes 16777216 | tf_op jit(solution)/shard_map/pallas_call | solution.py:279
Async XLA Ops:
  0.0 48.8 %collective-permute-start = (bf16[64,128,128]{2,1,0:T(8,128)(2,1)}, bf16[64,128,128]{2,1,0:T(8,128)(2,1)S(1)}, u32[]{:S(2)}, u32[]{:S(2)}) collective-permute-start(bf16[64,128,128]{2,1,0:T(8,128)(2,1)} %bitcast.6), channel_id=1, source_target_pairs={{1,0},{2,1},{3,2},{0,3},{5,4},{6,5},{7,6},{4,7},{9,8},{10,9},{11,1... | collective-permute-start | bytes 6291464 | tf_op jit(solution)/shard_map/ppermute | solution.py:21
  4.2 44.6 %collective-permute-start.1 = (bf16[64,128,128]{2,1,0:T(8,128)(2,1)}, bf16[64,128,128]{2,1,0:T(8,128)(2,1)}, u32[]{:S(2)}, u32[]{:S(2)}) collective-permute-start(bf16[64,128,128]{2,1,0:T(8,128)(2,1)} %bitcast.8), channel_id=1, source_target_pairs={{4,0},{8,4},{12,8},{16,12},{20,16},{24,20},{28,24},{0,28},{5,1},{9... | collective-permute-start | bytes 6291464 | tf_op jit(solution)/shard_map/ppermute | solution.py:21
  48.8 1.4 copy-start

commit v9 on v8

--- a/solution.py
+++ b/solution.py
@@ -12,7 +12,7 @@
 COLB = 16
 COL_GROUP = 2
 ROW_GROUP = 8
-COPY_STEPS = 32
+COPY_STEPS = 8
 
 
 def from_behind(block, axis, distance):
@@ -145,16 +145,14 @@
 
 
 def second_kernel(
-    slot_of, left_index, right_index, left_hbm, right_hbm, partial, outgoing,
+    slot_of, left_index, right_index, left_tile, right_hbm, partial, outgoing,
     out,
-    left_dense, right_column, partial_buf, staging, left_tile, right_tile, partial_sems, out_sems, tile_sems,
+    left_dense, right_column, partial_buf, staging, right_tile, partial_sems, out_sems, tile_sems,
 ):
     side = left_tile.shape[-1]
     pairs = COLB // COL_GROUP
     products = ROWB * COLB
-    left_copy = pltpu.make_async_copy(left_hbm, left_tile, tile_sems.at[0])
-    right_copy = pltpu.make_async_copy(right_hbm, right_tile, tile_sems.at[1])
-    left_copy.start()
+    right_copy = pltpu.make_async_copy(right_hbm, right_tile, tile_sems.at[0])
     right_copy.start()
 
     def partial_copy(cp, buffer):
@@ -192,7 +190,7 @@
 
     multiply_tiles(
         left_tile, right_tile, left_index, right_index, left_dense, right_column, emit, before,
-        left_copy.wait, right_copy.wait,
+        None, right_copy.wait,
     )
     send_pair(pairs - 1)
 
@@ -255,17 +253,16 @@
     outgoing = pl.pallas_call(
         second_kernel,
         out_shape=jax.ShapeDtypeStruct((slots, side, side), jnp.bfloat16),
-        in_specs=[smem, smem, smem, anywhere, anywhere, anywhere, anywhere],
+        in_specs=[smem, smem, smem, vmem, anywhere, anywhere, anywhere],
         out_specs=anywhere,
         input_output_aliases={6: 0},
         scratch_shapes=work + [
             pltpu.VMEM((2, ROWB * side, COL_GROUP * side), jnp.float32),
             pltpu.VMEM((products, side, side), jnp.bfloat16),
-            pltpu.VMEM(left_here.shape, left_here.dtype),
             pltpu.VMEM(right_here.shape, right_here.dtype),
             pltpu.SemaphoreType.DMA((2,)),
             pltpu.SemaphoreType.DMA((products,)),
-            pltpu.SemaphoreType.DMA((2,)),
+            pltpu.SemaphoreType.DMA((1,)),
         ],
         compiler_params=pltpu.CompilerParams(vmem_limit_bytes=60 * 1024 * 1024),
         cost_estimate=pl.CostEstimate(

time: 282 us -> 272 us (0.965)
  Pallas kernels: 79.1 us -> 68.7 us
    pallas_call x1, Pallas kernels: 19.1 us -> 8.95 us  [body(): pl.pallas_call(pass_through, out_shape=jax.ShapeDtypeStruct(received.shap...]
where the time goes in v9:
time: 272 us; the launch traced here: 271 us
  blocking collectives  191 us (70%)
  Pallas kernels  68.7 us (25%)
  starting transfers between devices  5.11 us (2%)
  waiting for transfers between devices  4.54 us (2%)
    all_to_all x1, blocking collectives, body(): lax.all_to_all(outgoing, ('row', 'col'), split_axis=0, concat_axis=0, til...  191 us
    pallas_call x1, Pallas kernels, body(): pl.pallas_call(functools.partial(first_kernel, rows_grid, cols_grid, capa...  39.1 us
    pallas_call x1, Pallas kernels, body(): pl.pallas_call(second_kernel, out_shape=jax.ShapeDtypeStruct((slots, side...  20.6 us
    pallas_call x1, Pallas kernels, body(): pl.pallas_call(pass_through, out_shape=jax.ShapeDtypeStruct(received.shap...  8.95 us
  transfers between devices with their start and end apart: 2, of which 1 were waited for; matrix products, arithmetic and copies ran while one was open for 0% of the time, Pallas kernels for 14%

profile of v9, /device:TPU:1, one launch (start us, length us, event | category | flops | bytes accessed | tf_op | source)
XLA Modules:
  0.0 271.2 jit_solution(5384991511355011685)
XLA Ops:
  0.0 4.2 %collective-permute-start = (bf16[64,128,128]{2,1,0:T(8,128)(2,1)}, bf16[64,128,128]{2,1,0:T(8,128)(2,1)S(1)}, u32[]{:S(2)}, u32[]{:S(2)}) collective-permute-start(bf16[64,128,128]{2,1,0:T(8,128)(2,1)} %bitcast.6), channel_id=1, source_target_pairs={{1,0},{2,1},{3,2},{0,3},{5,4},{6,5},{7,6},{4,7},{9,8},{10,9},{11,1... | collective-permute-start | bytes 6291464 | tf_op jit(solution)/shard_map/ppermute | solution.py:21
  4.2 1.0 collective-permute-start.1
  5.1 39.1 %shard_map.55 = (f32[8,1024,256]{2,1,0:T(8,128)}, s32[128]{0:T(128)}, s32[128]{0:T(128)}, s32[256]{0:T(256)}, bf16[256,128,128]{2,1,0:T(8,128)(2,1)}) custom-call(s32[8,4,64]{2,1,0:T(4,128)} %left_places.1, s32[8,4,64]{2,1,0:T(4,128)} %right_places.1, s32[128]{0:T(128)} %bitcast.10, bf16[64,128,128]{2,1,0:T(8,128)(2,1)} %bitcast.7, bf16[64,128,128]{2,1,0:T(8,128)(2,1)} %bitcast.9), custom_call_target="tpu_custom_call" | custom-call | flops 8589934592 | bytes 12582912 | tf_op jit(solution)/shard_map/pallas_call | solution.py:231
  44.2 4.5 %collective-permute-done.left_tile = bf16[64,128,128]{2,1,0:T(8,128)(2,1)S(1)} collective-permute-done((bf16[64,128,128]{2,1,0:T(8,128)(2,1)}, bf16[64,128,128]{2,1,0:T(8,128)(2,1)S(1)}, u32[]{:S(2)}, u32[]{:S(2)}) %collective-permute-start) | collective-permute-done | bytes 2097184 | tf_op jit(solution)/shard_map/ppermute | solution.py:21
  48.8 0.0 copy-start
  48.8 0.0 collective-permute-done.1.right_hbm
  48.8 1.3 copy-done
  50.1 20.6 %shard_map.56 = bf16[256,128,128]{2,1,0:T(8,128)(2,1)} custom-call(s32[128]{0:T(128)} %get-tuple-element.10.slot_of, s32[128]{0:T(128)} %get-tuple-element.11.left_index, s32[256]{0:T(256)} %get-tuple-element.12.right_index, bf16[64,128,128]{2,1,0:T(8,128)(2,1)} %copy-done, ...), custom_call_target="tpu_custom_call", output_to_operand_aliasing={{}: (6, {})} | custom-call | flops 8589934592 | bytes 20971520 | tf_op jit(solution)/shard_map/pallas_call | solution.py:253
  70.7 191.5 %all_to_all.5.source = bf16[32,8,128,128]{3,2,1,0:T(8,128)(2,1)} all-to-all(bf16[32,8,128,128]{3,2,1,0:T(8,128)(2,1)} %bitcast.5), channel_id=1, replica_groups=mesh['row'=8,'col'=4] {'row','col'}, dimensions={0} | all-to-all | bytes 16777216 | tf_op jit(solution)/shard_map/all_to_all | solution.py:273
  262.2 8.9 %shard_map.57 = bf16[32,8,128,128]{3,2,1,0:T(8,128)(2,1)} custom-call(bf16[32,8,128,128]{3,2,1,0:T(8,128)(2,1)} %all_to_all.5.source), custom_call_target="tpu_custom_call" | custom-call | bytes 16777216 | tf_op jit(solution)/shard_map/pallas_call | solution.py:276
Async XLA Ops:
  0.0 48.8 %collective-permute-start = (bf16[64,128,128]{2,1,0:T(8,128)(2,1)}, bf16[64,128,128]{2,1,0:T(8,128)(2,1)S(1)}, u32[]{:S(2)}, u32[]{:S(2)}) collective-permute-start(bf16[64,128,128]{2,1,0:T(8,128)(2,1)} %bitcast.6), channel_id=1, source_target_pairs={{1,0},{2,1},{3,2},{0,3},{5,4},{6,5},{7,6},{4,7},{9,8},{10,9},{11,1... | collective-permute-start | bytes 6291464 | tf_op jit(solution)/shard_map/ppermute | solution.py:21
  4.2 44.6 %collective-permute-start.1 = (bf16[64,128,128]{2,1,0:T(8,128)(2,1)}, bf16[64,128,128]{2,1,0:T(8,128)(2,1)}, u32[]{:S(2)}, u32[]{:S(2)}) collective-permute-start(bf16[64,128,128]{2,1,0:T(8,128)(2,1)} %bitcast.8), channel_id=1, source_target_pairs={{4,0},{8,4},{12,8},{16,12},{20,16},{24,20},{28,24},{0,28},{5,1},{9... | collective-permute-start | bytes 6291464 | tf_op jit(solution)/shard_map/ppermute | solution.py:21
  48.8 1.4 copy-start

commit v10 on v9

--- a/solution.py
+++ b/solution.py
@@ -12,7 +12,7 @@
 COLB = 16
 COL_GROUP = 2
 ROW_GROUP = 8
-COPY_STEPS = 8
+COPY_STEPS = 2
 
 
 def from_behind(block, axis, distance):

time: 272 us -> 268 us (0.985)
  Pallas kernels: 68.7 us -> 65.6 us
    pallas_call x1, Pallas kernels: 8.95 us -> 5.85 us  [body(): pl.pallas_call(pass_through, out_shape=jax.ShapeDtypeStruct(received.shap...]
  transfers between devices with their start and end apart: 2 -> 2, of which waited for: 1 -> 1; matrix products, arithmetic and copies ran while one was open for 0% -> 0% of each run, Pallas kernels for 14% -> 15%
where the time goes in v10:
time: 268 us
  blocking collectives  192 us (72%)
  Pallas kernels  65.6 us (24%)
  starting transfers between devices  5.11 us (2%)
  waiting for transfers between devices  4.54 us (2%)
    all_to_all x1, blocking collectives, body(): lax.all_to_all(outgoing, ('row', 'col'), split_axis=0, concat_axis=0, til...  192 us
    pallas_call x1, Pallas kernels, body(): pl.pallas_call(functools.partial(first_kernel, rows_grid, cols_grid, capa...  39.1 us
    pallas_call x1, Pallas kernels, body(): pl.pallas_call(second_kernel, out_shape=jax.ShapeDtypeStruct((slots, side...  20.6 us
    pallas_call x1, Pallas kernels, body(): pl.pallas_call(pass_through, out_shape=jax.ShapeDtypeStruct(received.shap...  5.85 us
  transfers between devices with their start and end apart: 2, of which 1 were waited for; matrix products, arithmetic and copies ran while one was open for 0% of the time, Pallas kernels for 15%

profile of v10, /device:TPU:1, one launch (start us, length us, event | category | flops | bytes accessed | tf_op | source)
XLA Modules:
  0.0 268.2 jit_solution(7990653132601291992)
XLA Ops:
  0.0 4.2 %collective-permute-start = (bf16[64,128,128]{2,1,0:T(8,128)(2,1)}, bf16[64,128,128]{2,1,0:T(8,128)(2,1)S(1)}, u32[]{:S(2)}, u32[]{:S(2)}) collective-permute-start(bf16[64,128,128]{2,1,0:T(8,128)(2,1)} %bitcast.6), channel_id=1, source_target_pairs={{1,0},{2,1},{3,2},{0,3},{5,4},{6,5},{7,6},{4,7},{9,8},{10,9},{11,1... | collective-permute-start | bytes 6291464 | tf_op jit(solution)/shard_map/ppermute | solution.py:21
  4.2 1.0 collective-permute-start.1
  5.1 39.1 %shard_map.55 = (f32[8,1024,256]{2,1,0:T(8,128)}, s32[128]{0:T(128)}, s32[128]{0:T(128)}, s32[256]{0:T(256)}, bf16[256,128,128]{2,1,0:T(8,128)(2,1)}) custom-call(s32[8,4,64]{2,1,0:T(4,128)} %left_places.1, s32[8,4,64]{2,1,0:T(4,128)} %right_places.1, s32[128]{0:T(128)} %bitcast.10, bf16[64,128,128]{2,1,0:T(8,128)(2,1)} %bitcast.7, bf16[64,128,128]{2,1,0:T(8,128)(2,1)} %bitcast.9), custom_call_target="tpu_custom_call" | custom-call | flops 8589934592 | bytes 12582912 | tf_op jit(solution)/shard_map/pallas_call | solution.py:231
  44.2 4.5 %collective-permute-done.left_tile = bf16[64,128,128]{2,1,0:T(8,128)(2,1)S(1)} collective-permute-done((bf16[64,128,128]{2,1,0:T(8,128)(2,1)}, bf16[64,128,128]{2,1,0:T(8,128)(2,1)S(1)}, u32[]{:S(2)}, u32[]{:S(2)}) %collective-permute-start) | collective-permute-done | bytes 2097184 | tf_op jit(solution)/shard_map/ppermute | solution.py:21
  48.8 0.0 copy-start
  48.8 0.0 collective-permute-done.1.right_hbm
  48.8 1.3 copy-done
  50.1 20.6 %shard_map.56 = bf16[256,128,128]{2,1,0:T(8,128)(2,1)} custom-call(s32[128]{0:T(128)} %get-tuple-element.10.slot_of, s32[128]{0:T(128)} %get-tuple-element.11.left_index, s32[256]{0:T(256)} %get-tuple-element.12.right_index, bf16[64,128,128]{2,1,0:T(8,128)(2,1)} %copy-done, ...), custom_call_target="tpu_custom_call", output_to_operand_aliasing={{}: (6, {})} | custom-call | flops 8589934592 | bytes 20971520 | tf_op jit(solution)/shard_map/pallas_call | solution.py:253
  70.7 191.6 %all_to_all.5.source = bf16[32,8,128,128]{3,2,1,0:T(8,128)(2,1)} all-to-all(bf16[32,8,128,128]{3,2,1,0:T(8,128)(2,1)} %bitcast.5), channel_id=1, replica_groups=mesh['row'=8,'col'=4] {'row','col'}, dimensions={0} | all-to-all | bytes 16777216 | tf_op jit(solution)/shard_map/all_to_all | solution.py:273
  262.3 5.9 %shard_map.57 = bf16[32,8,128,128]{3,2,1,0:T(8,128)(2,1)} custom-call(bf16[32,8,128,128]{3,2,1,0:T(8,128)(2,1)} %all_to_all.5.source), custom_call_target="tpu_custom_call" | custom-call | bytes 16777216 | tf_op jit(solution)/shard_map/pallas_call | solution.py:276
Async XLA Ops:
  0.0 48.8 %collective-permute-start = (bf16[64,128,128]{2,1,0:T(8,128)(2,1)}, bf16[64,128,128]{2,1,0:T(8,128)(2,1)S(1)}, u32[]{:S(2)}, u32[]{:S(2)}) collective-permute-start(bf16[64,128,128]{2,1,0:T(8,128)(2,1)} %bitcast.6), channel_id=1, source_target_pairs={{1,0},{2,1},{3,2},{0,3},{5,4},{6,5},{7,6},{4,7},{9,8},{10,9},{11,1... | collective-permute-start | bytes 6291464 | tf_op jit(solution)/shard_map/ppermute | solution.py:21
  4.2 44.6 %collective-permute-start.1 = (bf16[64,128,128]{2,1,0:T(8,128)(2,1)}, bf16[64,128,128]{2,1,0:T(8,128)(2,1)}, u32[]{:S(2)}, u32[]{:S(2)}) collective-permute-start(bf16[64,128,128]{2,1,0:T(8,128)(2,1)} %bitcast.8), channel_id=1, source_target_pairs={{4,0},{8,4},{12,8},{16,12},{20,16},{24,20},{28,24},{0,28},{5,1},{9... | collective-permute-start | bytes 6291464 | tf_op jit(solution)/shard_map/ppermute | solution.py:21
  48.8 1.4 copy-start

commit v11 on v10

--- a/solution.py
+++ b/solution.py
@@ -41,11 +41,12 @@
 
 def multiply_tiles(
     left_tile, right_tile, left_index, right_index, left_dense, right_column, emit, before=None,
-    left_ready=None, right_ready=None,
+    left_ready=None, right_ready=None, column_of=None,
 ):
     side = left_tile.shape[-1]
     zero_block = jnp.zeros((side, side), left_tile.dtype)
-    right_column[...] = jnp.zeros(right_column.shape, right_column.dtype)
+    if column_of is None:
+        right_column[...] = jnp.zeros(right_column.shape, right_column.dtype)
     if left_ready is not None:
         left_ready()
 
@@ -74,16 +75,21 @@
     def column_pair(cp, carry):
         if before is not None:
             before(cp)
-        place_column(cp, False)
+        if column_of is None:
+            place_column(cp, False)
+            column = right_column
+        else:
+            column = column_of(cp)
 
         def row_pair(rp, inner):
             rows = pl.ds(pl.multiple_of(rp * ROW_GROUP * side, ROW_GROUP * side), ROW_GROUP * side)
-            result = jnp.dot(left_dense[rows, :], right_column[...], preferred_element_type=jnp.float32)
+            result = jnp.dot(left_dense[rows, :], column[...], preferred_element_type=jnp.float32)
             emit(rp, cp, rows, result)
             return inner
 
         lax.fori_loop(0, ROWB // ROW_GROUP, row_pair, 0)
-        place_column(cp, True)
+        if column_of is None:
+            place_column(cp, True)
         return carry
 
     lax.fori_loop(0, COLB // COL_GROUP, column_pair, 0)
@@ -144,21 +150,53 @@
     lax.fori_loop(0, outgoing.shape[0], wait_slot, 0)
 
 
+def column_kernel(right_index, right_tile, columns, column_buf, sems):
+    side = right_tile.shape[-1]
+    pairs = COLB // COL_GROUP
+    zero_block = jnp.zeros((side, side), right_tile.dtype)
+
+    def send(cp, buffer):
+        return pltpu.make_async_copy(column_buf.at[buffer], columns.at[cp], sems.at[buffer])
+
+    def column_pair(cp, carry):
+        buffer = lax.rem(cp, 2)
+
+        @pl.when(cp >= 2)
+        def _():
+            send(cp - 2, buffer).wait()
+
+        for k in range(KBLK):
+            for cc in range(COL_GROUP):
+                index = right_index[k * COLB + cp * COL_GROUP + cc]
+                block = right_tile[jnp.maximum(index, 0)]
+                column_buf[buffer, k * side:(k + 1) * side, cc * side:(cc + 1) * side] = jnp.where(
+                    index >= 0, block, zero_block
+                )
+        send(cp, buffer).start()
+        return carry
+
+    lax.fori_loop(0, pairs, column_pair, 0)
+    send(pairs - 2, 0).wait()
+    send(pairs - 1, 1).wait()
+
+
 def second_kernel(
-    slot_of, left_index, right_index, left_tile, right_hbm, partial, outgoing,
+    slot_of, left_index, left_tile, columns, partial, outgoing,
     out,
-    left_dense, right_column, partial_buf, staging, right_tile, partial_sems, out_sems, tile_sems,
+    left_dense, column_buf, partial_buf, staging, partial_sems, column_sems, out_sems,
 ):
     side = left_tile.shape[-1]
     pairs = COLB // COL_GROUP
     products = ROWB * COLB
-    right_copy = pltpu.make_async_copy(right_hbm, right_tile, tile_sems.at[0])
-    right_copy.start()
 
     def partial_copy(cp, buffer):
         return pltpu.make_async_copy(partial.at[cp], partial_buf.at[buffer], partial_sems.at[buffer])
 
+    def column_copy(cp, buffer):
+        return pltpu.make_async_copy(columns.at[cp], column_buf.at[buffer], column_sems.at[buffer])
+
     partial_copy(0, 0).start()
+    column_copy(0, 0).start()
 
     def send_pair(cp):
         for r in range(ROWB):
@@ -172,12 +210,14 @@
         @pl.when(cp + 1 < pairs)
         def _():
             partial_copy(cp + 1, 1 - buffer).start()
+            column_copy(cp + 1, 1 - buffer).start()
 
         @pl.when(cp > 0)
         def _():
             send_pair(cp - 1)
 
         partial_copy(cp, buffer).wait()
+        column_copy(cp, buffer).wait()
 
     def emit(rp, cp, rows, result):
         buffer = lax.rem(cp, 2)
@@ -189,8 +229,8 @@
                 staging[m] = piece.astype(staging.dtype)
 
     multiply_tiles(
-        left_tile, right_tile, left_index, right_index, left_dense, right_column, emit, before,
-        None, right_copy.wait,
+        left_tile, None, left_index, None, left_dense, None, emit, before,
+        column_of=lambda cp: column_buf.at[lax.rem(cp, 2)],
     )
     send_pair(pairs - 1)
 
@@ -250,25 +290,38 @@
         compiler_params=pltpu.CompilerParams(vmem_limit_bytes=60 * 1024 * 1024),
         cost_estimate=pl.CostEstimate(flops=flops, bytes_accessed=tile_bytes + partial_bytes, transcendentals=0),
     )(left_places, right_places, owners[0], left_here, right_here)
+    column_bytes = pairs * KBLK * side * COL_GROUP * side * 2
+    columns = pl.pallas_call(
+        column_kernel,
+        out_shape=jax.ShapeDtypeStruct((pairs, KBLK * side, COL_GROUP * side), jnp.bfloat16),
+        in_specs=[smem, vmem],
+        out_specs=anywhere,
+        scratch_shapes=[
+            pltpu.VMEM((2, KBLK * side, COL_GROUP * side), jnp.bfloat16),
+            pltpu.SemaphoreType.DMA((2,)),
+        ],
+        cost_estimate=pl.CostEstimate(flops=0, bytes_accessed=left_here.size * 2 + column_bytes, transcendentals=0),
+    )(right_index, right_next)
     outgoing = pl.pallas_call(
         second_kernel,
         out_shape=jax.ShapeDtypeStruct((slots, side, side), jnp.bfloat16),
-        in_specs=[smem, smem, smem, vmem, anywhere, anywhere, anywhere],
+        in_specs=[smem, smem, vmem, anywhere, anywhere, anywhere],
         out_specs=anywhere,
-        input_output_aliases={6: 0},
-        scratch_shapes=work + [
+        input_output_aliases={5: 0},
+        scratch_shapes=[
+            pltpu.VMEM((ROWB * side, KBLK * side), jnp.bfloat16),
+            pltpu.VMEM((2, KBLK * side, COL_GROUP * side), jnp.bfloat16),
             pltpu.VMEM((2, ROWB * side, COL_GROUP * side), jnp.float32),
             pltpu.VMEM((products, side, side), jnp.bfloat16),
-            pltpu.VMEM(right_here.shape, right_here.dtype),
+            pltpu.SemaphoreType.DMA((2,)),
             pltpu.SemaphoreType.DMA((2,)),
             pltpu.SemaphoreType.DMA((products,)),
-            pltpu.SemaphoreType.DMA((1,)),
         ],
         compiler_params=pltpu.CompilerParams(vmem_limit_bytes=60 * 1024 * 1024),
         cost_estimate=pl.CostEstimate(
             flops=flops, bytes_accessed=tile_bytes + partial_bytes + slots * side * side * 2, transcendentals=0
         ),
-    )(slot_of, left_index, right_index, left_next, right_next, partial, outgoing)
+    )(slot_of, left_index, left_next, columns, partial, outgoing)
     outgoing = outgoing.reshape(devices_all, capacity, side, side)
     received = lax.all_to_all(outgoing, ("row", "col"), split_axis=0, concat_axis=0, tiled=True)
     chunk = devices_all // COPY_STEPS

time: 268 us -> 266 us (level)
  waiting for transfers between devices: 4.54 us -> 0.01 us
  Pallas kernels: 65.6 us -> 69.4 us
    pallas_call x0 -> x1, Pallas kernels: none -> 7.07 us  [body(): pl.pallas_call(column_kernel, out_shape=jax.ShapeDtypeStruct((pairs, KBLK...]
    ppermute x2, waiting for transfers between devices: 4.54 us -> 0.01 us  [from_behind(): return lax.ppermute(block, axis, route)]
    pallas_call x1, Pallas kernels: 20.6 us -> 17.4 us  [body(): pl.pallas_call(second_kernel, out_shape=jax.ShapeDtypeStruct((slots, side...]
  transfers between devices with their start and end apart: 2 -> 2, of which waited for: 1 -> 0; matrix products, arithmetic and copies ran while one was open for 0% -> 0% of each run, Pallas kernels for 15% -> 17%
where the time goes in v11:
time: 266 us; the launch traced here: 265 us
  blocking collectives  190 us (71%)
  Pallas kernels  69.4 us (26%)
  starting transfers between devices  4.83 us (2%)
    all_to_all x1, blocking collectives, body(): lax.all_to_all(outgoing, ('row', 'col'), split_axis=0, concat_axis=0, til...  190 us
    pallas_call x1, Pallas kernels, body(): pl.pallas_call(functools.partial(first_kernel, rows_grid, cols_grid, capa...  39.1 us
    pallas_call x1, Pallas kernels, body(): pl.pallas_call(second_kernel, out_shape=jax.ShapeDtypeStruct((slots, side...  17.4 us
    pallas_call x1, Pallas kernels, body(): pl.pallas_call(column_kernel, out_shape=jax.ShapeDtypeStruct((pairs, KBLK...  7.07 us
    pallas_call x1, Pallas kernels, body(): pl.pallas_call(pass_through, out_shape=jax.ShapeDtypeStruct(received.shap...  5.85 us
  transfers between devices with their start and end apart: 2, of which 0 were waited for; matrix products, arithmetic and copies ran while one was open for 0% of the time, Pallas kernels for 17%

profile of v11, /device:TPU:1, one launch (start us, length us, event | category | flops | bytes accessed | tf_op | source)
XLA Modules:
  0.0 265.5 jit_solution(11463209944879916363)
XLA Ops:
  0.0 0.1 collective-permute-start.1
  0.1 4.8 %collective-permute-start = (bf16[64,128,128]{2,1,0:T(8,128)(2,1)}, bf16[64,128,128]{2,1,0:T(8,128)(2,1)S(1)}, u32[]{:S(2)}, u32[]{:S(2)}) collective-permute-start(bf16[64,128,128]{2,1,0:T(8,128)(2,1)} %bitcast.8), channel_id=1, source_target_pairs={{1,0},{2,1},{3,2},{0,3},{5,4},{6,5},{7,6},{4,7},{9,8},{10,9},{11,1... | collective-permute-start | bytes 6291464 | tf_op jit(solution)/shard_map/ppermute | solution.py:21
  4.8 39.1 %shard_map.55 = (f32[8,1024,256]{2,1,0:T(8,128)}, s32[128]{0:T(128)}, s32[128]{0:T(128)}, s32[256]{0:T(256)}, bf16[256,128,128]{2,1,0:T(8,128)(2,1)}) custom-call(s32[8,4,64]{2,1,0:T(4,128)} %left_places.1, s32[8,4,64]{2,1,0:T(4,128)} %right_places.1, s32[128]{0:T(128)} %bitcast.10, bf16[64,128,128]{2,1,0:T(8,128)(2,1)} %bitcast.9, bf16[64,128,128]{2,1,0:T(8,128)(2,1)} %bitcast.7), custom_call_target="tpu_custom_call" | custom-call | flops 8589934592 | bytes 12582912 | tf_op jit(solution)/shard_map/pallas_call | solution.py:271
  43.9 0.0 collective-permute-done.1.right_tile
  44.0 7.1 %shard_map.56.columns = bf16[8,2048,256]{2,1,0:T(8,128)(2,1)} custom-call(s32[256]{0:T(256)} %get-tuple-element.12.right_index, bf16[64,128,128]{2,1,0:T(8,128)(2,1)} %collective-permute-done.1.right_tile), custom_call_target="tpu_custom_call" | custom-call | bytes 10485760 | tf_op jit(solution)/shard_map/pallas_call | solution.py:294
  51.0 0.0 collective-permute-done.left_tile
  51.1 0.0 copy-start
  51.1 1.3 copy-done
  52.4 17.4 %shard_map.57 = bf16[256,128,128]{2,1,0:T(8,128)(2,1)} custom-call(s32[128]{0:T(128)} %get-tuple-element.10.slot_of, s32[128]{0:T(128)} %get-tuple-element.11.left_index, bf16[64,128,128]{2,1,0:T(8,128)(2,1)} %copy-done, bf16[8,2048,256]{2,1,0:T(8,128)(2,1)} %shard_map.56.columns, ...), custom_call_target="tpu_custom_call", output_to_operand_aliasing={{}: (5, {})} | custom-call | flops 8589934592 | bytes 20971520 | tf_op jit(solution)/shard_map/pallas_call | solution.py:305
  69.8 189.9 %all_to_all.5.source = bf16[32,8,128,128]{3,2,1,0:T(8,128)(2,1)} all-to-all(bf16[32,8,128,128]{3,2,1,0:T(8,128)(2,1)} %bitcast.5), channel_id=1, replica_groups=mesh['row'=8,'col'=4] {'row','col'}, dimensions={0} | all-to-all | bytes 16777216 | tf_op jit(solution)/shard_map/all_to_all | solution.py:326
  259.6 5.9 %shard_map.58 = bf16[32,8,128,128]{3,2,1,0:T(8,128)(2,1)} custom-call(bf16[32,8,128,128]{3,2,1,0:T(8,128)(2,1)} %all_to_all.5.source), custom_call_target="tpu_custom_call" | custom-call | bytes 16777216 | tf_op jit(solution)/shard_map/pallas_call | solution.py:329
Async XLA Ops:
  0.0 44.0 %collective-permute-start.1 = (bf16[64,128,128]{2,1,0:T(8,128)(2,1)}, bf16[64,128,128]{2,1,0:T(8,128)(2,1)}, u32[]{:S(2)}, u32[]{:S(2)}) collective-permute-start(bf16[64,128,128]{2,1,0:T(8,128)(2,1)} %bitcast.6), channel_id=1, source_target_pairs={{4,0},{8,4},{12,8},{16,12},{20,16},{24,20},{28,24},{0,28},{5,1},{9... | collective-permute-start | bytes 6291464 | tf_op jit(solution)/shard_map/ppermute | solution.py:21
  0.1 51.0 %collective-permute-start = (bf16[64,128,128]{2,1,0:T(8,128)(2,1)}, bf16[64,128,128]{2,1,0:T(8,128)(2,1)S(1)}, u32[]{:S(2)}, u32[]{:S(2)}) collective-permute-start(bf16[64,128,128]{2,1,0:T(8,128)(2,1)} %bitcast.8), channel_id=1, source_target_pairs={{1,0},{2,1},{3,2},{0,3},{5,4},{6,5},{7,6},{4,7},{9,8},{10,9},{11,1... | collective-permute-start | bytes 6291464 | tf_op jit(solution)/shard_map/ppermute | solution.py:21
  51.1 1.3 copy-start

commit v12 on v11

--- a/solution.py
+++ b/solution.py
@@ -45,8 +45,6 @@
 ):
     side = left_tile.shape[-1]
     zero_block = jnp.zeros((side, side), left_tile.dtype)
-    if column_of is None:
-        right_column[...] = jnp.zeros(right_column.shape, right_column.dtype)
     if left_ready is not None:
         left_ready()
 
@@ -63,14 +61,15 @@
         right_ready()
 
     def place_column(cp, clear):
+        if clear:
+            return
         for k in range(KBLK):
             for cc in range(COL_GROUP):
                 index = right_index[k * COLB + cp * COL_GROUP + cc]
-
-                @pl.when(index >= 0)
-                def _():
-                    block = zero_block if clear else right_tile[index]
-                    right_column[k * side:(k + 1) * side, cc * side:(cc + 1) * side] = block
+                block = right_tile[jnp.maximum(index, 0)]
+                right_column[k * side:(k + 1) * side, cc * side:(cc + 1) * side] = jnp.where(
+                    index >= 0, block, zero_block
+                )
 
     def column_pair(cp, carry):
         if before is not None:
@@ -129,7 +128,7 @@
     def zero_slot(s, carry):
         @pl.when(filled[s] == 0)
         def _():
-            pltpu.make_async_copy(zero_ref, outgoing.at[s], zero_sems.at[s]).start()
+            pltpu.make_async_copy(zero_ref, outgoing.at[s], zero_sems.at[0]).start()
 
         return carry
 
@@ -140,14 +139,8 @@
 
     multiply_tiles(left_tile, right_tile, left_index, right_index, left_dense, right_column, emit)
 
-    def wait_slot(s, carry):
-        @pl.when(filled[s] == 0)
-        def _():
-            pltpu.make_async_copy(zero_ref, outgoing.at[s], zero_sems.at[s]).wait()
-
-        return carry
-
-    lax.fori_loop(0, outgoing.shape[0], wait_slot, 0)
+    unfilled = outgoing.shape[0] - ROWB * COLB
+    pltpu.make_async_copy(outgoing.at[pl.ds(0, unfilled)], outgoing.at[pl.ds(0, unfilled)], zero_sems.at[0]).wait()
 
 
 def column_kernel(right_index, right_tile, columns, column_buf, sems):
@@ -202,7 +195,7 @@
         for r in range(ROWB):
             for cc in range(COL_GROUP):
                 m = r * COLB + cp * COL_GROUP + cc
-                pltpu.make_async_copy(staging.at[m], out.at[slot_of[m]], out_sems.at[m]).start()
+                pltpu.make_async_copy(staging.at[m], out.at[slot_of[m]], out_sems.at[0]).start()
 
     def before(cp):
         buffer = lax.rem(cp, 2)
@@ -234,11 +227,7 @@
     )
     send_pair(pairs - 1)
 
-    def wait_block(m, carry):
-        pltpu.make_async_copy(staging.at[m], out.at[slot_of[m]], out_sems.at[m]).wait()
-        return carry
-
-    lax.fori_loop(0, products, wait_block, 0)
+    pltpu.make_async_copy(staging, out.at[pl.ds(0, products)], out_sems.at[0]).wait()
 
 
 def pass_through(source, target):
@@ -285,7 +274,7 @@
             pltpu.SMEM((devices_all,), jnp.int32),
             pltpu.SMEM((slots,), jnp.int32),
             pltpu.VMEM((side, side), jnp.bfloat16),
-            pltpu.SemaphoreType.DMA((slots,)),
+            pltpu.SemaphoreType.DMA((1,)),
         ],
         compiler_params=pltpu.CompilerParams(vmem_limit_bytes=60 * 1024 * 1024),
         cost_estimate=pl.CostEstimate(flops=flops, bytes_accessed=tile_bytes + partial_bytes, transcendentals=0),
@@ -315,7 +304,7 @@
             pltpu.VMEM((products, side, side), jnp.bfloat16),
             pltpu.SemaphoreType.DMA((2,)),
             pltpu.SemaphoreType.DMA((2,)),
-            pltpu.SemaphoreType.DMA((products,)),
+            pltpu.SemaphoreType.DMA((1,)),
         ],
         compiler_params=pltpu.CompilerParams(vmem_limit_bytes=60 * 1024 * 1024),
         cost_estimate=pl.CostEstimate(

time: 266 us -> 264 us (level)
  Pallas kernels: 69.4 us -> 59.5 us
  waiting for transfers between devices: 0.01 us -> 5.4 us
  blocking collectives: 190 us -> 193 us
    pallas_call x1, Pallas kernels: 39.1 us -> 30.9 us  [body(): pl.pallas_call(functools.partial(first_kernel, rows_grid, cols_grid, capa...]
    ppermute x2, waiting for transfers between devices: 0.01 us -> 5.4 us  [from_behind(): return lax.ppermute(block, axis, route)]
    all_to_all x1, blocking collectives: 190 us -> 193 us  [body(): lax.all_to_all(outgoing, ('row', 'col'), split_axis=0, concat_axis=0, til...]
  transfers between devices with their start and end apart: 2 -> 2, of which waited for: 0 -> 1; matrix products, arithmetic and copies ran while one was open for 0% -> 0% of each run, Pallas kernels for 17% -> 14%
where the time goes in v12:
time: 264 us
  blocking collectives  193 us (73%)
  Pallas kernels  59.5 us (23%)
  waiting for transfers between devices  5.4 us (2%)
  starting transfers between devices  4.83 us (2%)
    all_to_all x1, blocking collectives, body(): lax.all_to_all(outgoing, ('row', 'col'), split_axis=0, concat_axis=0, til...  193 us
    pallas_call x1, Pallas kernels, body(): pl.pallas_call(functools.partial(first_kernel, rows_grid, cols_grid, capa...  30.9 us
    pallas_call x1, Pallas kernels, body(): pl.pallas_call(second_kernel, out_shape=jax.ShapeDtypeStruct((slots, side...  15.8 us
    pallas_call x1, Pallas kernels, body(): pl.pallas_call(column_kernel, out_shape=jax.ShapeDtypeStruct((pairs, KBLK...  7.07 us
    pallas_call x1, Pallas kernels, body(): pl.pallas_call(pass_through, out_shape=jax.ShapeDtypeStruct(received.shap...  5.85 us
    ppermute x2, waiting for transfers between devices, from_behind(): return lax.ppermute(block, axis, route)  5.4 us
  transfers between devices with their start and end apart: 2, of which 1 were waited for; matrix products, arithmetic and copies ran while one was open for 0% of the time, Pallas kernels for 14%

profile of v12, /device:TPU:1, one launch (start us, length us, event | category | flops | bytes accessed | tf_op | source)
XLA Modules:
  0.0 263.9 jit_solution(5363338373975965849)
XLA Ops:
  0.0 0.1 collective-permute-start.1
  0.1 4.8 %collective-permute-start = (bf16[64,128,128]{2,1,0:T(8,128)(2,1)}, bf16[64,128,128]{2,1,0:T(8,128)(2,1)S(1)}, u32[]{:S(2)}, u32[]{:S(2)}) collective-permute-start(bf16[64,128,128]{2,1,0:T(8,128)(2,1)} %bitcast.8), channel_id=1, source_target_pairs={{1,0},{2,1},{3,2},{0,3},{5,4},{6,5},{7,6},{4,7},{9,8},{10,9},{11,1... | collective-permute-start | bytes 6291464 | tf_op jit(solution)/shard_map/ppermute | solution.py:21
  4.8 30.9 %shard_map.55 = (f32[8,1024,256]{2,1,0:T(8,128)}, s32[128]{0:T(128)}, s32[128]{0:T(128)}, s32[256]{0:T(256)}, bf16[256,128,128]{2,1,0:T(8,128)(2,1)}) custom-call(s32[8,4,64]{2,1,0:T(4,128)} %left_places.1, s32[8,4,64]{2,1,0:T(4,128)} %right_places.1, s32[128]{0:T(128)} %bitcast.10, bf16[64,128,128]{2,1,0:T(8,128)(2,1)} %bitcast.9, bf16[64,128,128]{2,1,0:T(8,128)(2,1)} %bitcast.7), custom_call_target="tpu_custom_call" | custom-call | flops 8589934592 | bytes 12582912 | tf_op jit(solution)/shard_map/pallas_call | solution.py:260
  35.7 0.0 collective-permute-done.1.right_tile
  35.7 7.1 %shard_map.56.columns = bf16[8,2048,256]{2,1,0:T(8,128)(2,1)} custom-call(s32[256]{0:T(256)} %get-tuple-element.12.right_index, bf16[64,128,128]{2,1,0:T(8,128)(2,1)} %collective-permute-done.1.right_tile), custom_call_target="tpu_custom_call" | custom-call | bytes 10485760 | tf_op jit(solution)/shard_map/pallas_call | solution.py:283
  42.8 5.4 %collective-permute-done.left_tile = bf16[64,128,128]{2,1,0:T(8,128)(2,1)S(1)} collective-permute-done((bf16[64,128,128]{2,1,0:T(8,128)(2,1)}, bf16[64,128,128]{2,1,0:T(8,128)(2,1)S(1)}, u32[]{:S(2)}, u32[]{:S(2)}) %collective-permute-start) | collective-permute-done | bytes 2097184 | tf_op jit(solution)/shard_map/ppermute | solution.py:21
  48.2 0.0 copy-start
  48.2 1.3 copy-done
  49.5 15.8 %shard_map.57 = bf16[256,128,128]{2,1,0:T(8,128)(2,1)} custom-call(s32[128]{0:T(128)} %get-tuple-element.10.slot_of, s32[128]{0:T(128)} %get-tuple-element.11.left_index, bf16[64,128,128]{2,1,0:T(8,128)(2,1)} %copy-done, bf16[8,2048,256]{2,1,0:T(8,128)(2,1)} %shard_map.56.columns, ...), custom_call_target="tpu_custom_call", output_to_operand_aliasing={{}: (5, {})} | custom-call | flops 8589934592 | bytes 20971520 | tf_op jit(solution)/shard_map/pallas_call | solution.py:294
  65.3 192.7 %all_to_all.5.source = bf16[32,8,128,128]{3,2,1,0:T(8,128)(2,1)} all-to-all(bf16[32,8,128,128]{3,2,1,0:T(8,128)(2,1)} %bitcast.5), channel_id=1, replica_groups=mesh['row'=8,'col'=4] {'row','col'}, dimensions={0} | all-to-all | bytes 16777216 | tf_op jit(solution)/shard_map/all_to_all | solution.py:315
  258.0 5.9 %shard_map.58 = bf16[32,8,128,128]{3,2,1,0:T(8,128)(2,1)} custom-call(bf16[32,8,128,128]{3,2,1,0:T(8,128)(2,1)} %all_to_all.5.source), custom_call_target="tpu_custom_call" | custom-call | bytes 16777216 | tf_op jit(solution)/shard_map/pallas_call | solution.py:318
Async XLA Ops:
  0.0 35.7 %collective-permute-start.1 = (bf16[64,128,128]{2,1,0:T(8,128)(2,1)}, bf16[64,128,128]{2,1,0:T(8,128)(2,1)}, u32[]{:S(2)}, u32[]{:S(2)}) collective-permute-start(bf16[64,128,128]{2,1,0:T(8,128)(2,1)} %bitcast.6), channel_id=1, source_target_pairs={{4,0},{8,4},{12,8},{16,12},{20,16},{24,20},{28,24},{0,28},{5,1},{9... | collective-permute-start | bytes 6291464 | tf_op jit(solution)/shard_map/ppermute | solution.py:21
  0.1 48.1 %collective-permute-start = (bf16[64,128,128]{2,1,0:T(8,128)(2,1)}, bf16[64,128,128]{2,1,0:T(8,128)(2,1)S(1)}, u32[]{:S(2)}, u32[]{:S(2)}) collective-permute-start(bf16[64,128,128]{2,1,0:T(8,128)(2,1)} %bitcast.8), channel_id=1, source_target_pairs={{1,0},{2,1},{3,2},{0,3},{5,4},{6,5},{7,6},{4,7},{9,8},{10,9},{11,1... | collective-permute-start | bytes 6291464 | tf_op jit(solution)/shard_map/ppermute | solution.py:21
  48.2 1.3 copy-start

commit v13 on v12

--- a/solution.py
+++ b/solution.py
@@ -91,7 +91,7 @@
             place_column(cp, True)
         return carry
 
-    lax.fori_loop(0, COLB // COL_GROUP, column_pair, 0)
+    lax.fori_loop(0, COLB // COL_GROUP, column_pair, 0, unroll=column_of is not None)
 
 
 def first_kernel(

time: 264 us -> 271 us (1.027)
  Pallas kernels: 59.5 us -> 66.3 us
    pallas_call x1, Pallas kernels: 15.8 us -> 22.5 us  [body(): pl.pallas_call(second_kernel, out_shape=jax.ShapeDtypeStruct((slots, side...]
where the time goes in v13:
time: 271 us
  blocking collectives  193 us (71%)
  Pallas kernels  66.3 us (24%)
  waiting for transfers between devices  5.4 us (2%)
  starting transfers between devices  4.83 us (2%)
    all_to_all x1, blocking collectives, body(): lax.all_to_all(outgoing, ('row', 'col'), split_axis=0, concat_axis=0, til...  193 us
    pallas_call x1, Pallas kernels, body(): pl.pallas_call(functools.partial(first_kernel, rows_grid, cols_grid, capa...  30.9 us
    pallas_call x1, Pallas kernels, body(): pl.pallas_call(second_kernel, out_shape=jax.ShapeDtypeStruct((slots, side...  22.5 us
    pallas_call x1, Pallas kernels, body(): pl.pallas_call(column_kernel, out_shape=jax.ShapeDtypeStruct((pairs, KBLK...  7.07 us
    pallas_call x1, Pallas kernels, body(): pl.pallas_call(pass_through, out_shape=jax.ShapeDtypeStruct(received.shap...  5.85 us
  transfers between devices with their start and end apart: 2, of which 1 were waited for; matrix products, arithmetic and copies ran while one was open for 0% of the time, Pallas kernels for 14%

profile of v13, /device:TPU:1, one launch (start us, length us, event | category | flops | bytes accessed | tf_op | source)
XLA Modules:
  0.0 270.6 jit_solution(7326234555991566990)
XLA Ops:
  0.0 0.1 collective-permute-start.1
  0.1 4.8 %collective-permute-start = (bf16[64,128,128]{2,1,0:T(8,128)(2,1)}, bf16[64,128,128]{2,1,0:T(8,128)(2,1)S(1)}, u32[]{:S(2)}, u32[]{:S(2)}) collective-permute-start(bf16[64,128,128]{2,1,0:T(8,128)(2,1)} %bitcast.8), channel_id=1, source_target_pairs={{1,0},{2,1},{3,2},{0,3},{5,4},{6,5},{7,6},{4,7},{9,8},{10,9},{11,1... | collective-permute-start | bytes 6291464 | tf_op jit(solution)/shard_map/ppermute | solution.py:21
  4.8 30.9 %shard_map.55 = (f32[8,1024,256]{2,1,0:T(8,128)}, s32[128]{0:T(128)}, s32[128]{0:T(128)}, s32[256]{0:T(256)}, bf16[256,128,128]{2,1,0:T(8,128)(2,1)}) custom-call(s32[8,4,64]{2,1,0:T(4,128)} %left_places.1, s32[8,4,64]{2,1,0:T(4,128)} %right_places.1, s32[128]{0:T(128)} %bitcast.10, bf16[64,128,128]{2,1,0:T(8,128)(2,1)} %bitcast.9, bf16[64,128,128]{2,1,0:T(8,128)(2,1)} %bitcast.7), custom_call_target="tpu_custom_call" | custom-call | flops 8589934592 | bytes 12582912 | tf_op jit(solution)/shard_map/pallas_call | solution.py:260
  35.7 0.0 collective-permute-done.1.right_tile
  35.7 7.1 %shard_map.56.columns = bf16[8,2048,256]{2,1,0:T(8,128)(2,1)} custom-call(s32[256]{0:T(256)} %get-tuple-element.12.right_index, bf16[64,128,128]{2,1,0:T(8,128)(2,1)} %collective-permute-done.1.right_tile), custom_call_target="tpu_custom_call" | custom-call | bytes 10485760 | tf_op jit(solution)/shard_map/pallas_call | solution.py:283
  42.8 5.4 %collective-permute-done.left_tile = bf16[64,128,128]{2,1,0:T(8,128)(2,1)S(1)} collective-permute-done((bf16[64,128,128]{2,1,0:T(8,128)(2,1)}, bf16[64,128,128]{2,1,0:T(8,128)(2,1)S(1)}, u32[]{:S(2)}, u32[]{:S(2)}) %collective-permute-start) | collective-permute-done | bytes 2097184 | tf_op jit(solution)/shard_map/ppermute | solution.py:21
  48.2 0.0 copy-start
  48.2 1.3 copy-done
  49.5 22.5 %shard_map.57 = bf16[256,128,128]{2,1,0:T(8,128)(2,1)} custom-call(s32[128]{0:T(128)} %get-tuple-element.10.slot_of, s32[128]{0:T(128)} %get-tuple-element.11.left_index, bf16[64,128,128]{2,1,0:T(8,128)(2,1)} %copy-done, bf16[8,2048,256]{2,1,0:T(8,128)(2,1)} %shard_map.56.columns, ...), custom_call_target="tpu_custom_call", output_to_operand_aliasing={{}: (5, {})} | custom-call | flops 8589934592 | bytes 20971520 | tf_op jit(solution)/shard_map/pallas_call | solution.py:294
  72.1 192.7 %all_to_all.5.source = bf16[32,8,128,128]{3,2,1,0:T(8,128)(2,1)} all-to-all(bf16[32,8,128,128]{3,2,1,0:T(8,128)(2,1)} %bitcast.5), channel_id=1, replica_groups=mesh['row'=8,'col'=4] {'row','col'}, dimensions={0} | all-to-all | bytes 16777216 | tf_op jit(solution)/shard_map/all_to_all | solution.py:315
  264.8 5.9 %shard_map.58 = bf16[32,8,128,128]{3,2,1,0:T(8,128)(2,1)} custom-call(bf16[32,8,128,128]{3,2,1,0:T(8,128)(2,1)} %all_to_all.5.source), custom_call_target="tpu_custom_call" | custom-call | bytes 16777216 | tf_op jit(solution)/shard_map/pallas_call | solution.py:318
Async XLA Ops:
  0.0 35.7 %collective-permute-start.1 = (bf16[64,128,128]{2,1,0:T(8,128)(2,1)}, bf16[64,128,128]{2,1,0:T(8,128)(2,1)}, u32[]{:S(2)}, u32[]{:S(2)}) collective-permute-start(bf16[64,128,128]{2,1,0:T(8,128)(2,1)} %bitcast.6), channel_id=1, source_target_pairs={{4,0},{8,4},{12,8},{16,12},{20,16},{24,20},{28,24},{0,28},{5,1},{9... | collective-permute-start | bytes 6291464 | tf_op jit(solution)/shard_map/ppermute | solution.py:21
  0.1 48.1 %collective-permute-start = (bf16[64,128,128]{2,1,0:T(8,128)(2,1)}, bf16[64,128,128]{2,1,0:T(8,128)(2,1)S(1)}, u32[]{:S(2)}, u32[]{:S(2)}) collective-permute-start(bf16[64,128,128]{2,1,0:T(8,128)(2,1)} %bitcast.8), channel_id=1, source_target_pairs={{1,0},{2,1},{3,2},{0,3},{5,4},{6,5},{7,6},{4,7},{9,8},{10,9},{11,1... | collective-permute-start | bytes 6291464 | tf_op jit(solution)/shard_map/ppermute | solution.py:21
  48.2 1.3 copy-start

commit v14 on v12

--- a/solution.py
+++ b/solution.py
@@ -10,7 +10,7 @@
 ROWB = 8
 KBLK = 16
 COLB = 16
-COL_GROUP = 2
+COL_GROUP = 4
 ROW_GROUP = 8
 COPY_STEPS = 2
 

time: 264 us -> 263 us (level)
  Pallas kernels: 59.5 us -> 56.5 us
where the time goes in v14:
time: 263 us
  blocking collectives  193 us (73%)
  Pallas kernels  56.5 us (21%)
  waiting for transfers between devices  7.23 us (3%)
  starting transfers between devices  4.83 us (2%)
    all_to_all x1, blocking collectives, body(): lax.all_to_all(outgoing, ('row', 'col'), split_axis=0, concat_axis=0, til...  193 us
    pallas_call x1, Pallas kernels, body(): pl.pallas_call(functools.partial(first_kernel, rows_grid, cols_grid, capa...  30.1 us
    pallas_call x1, Pallas kernels, body(): pl.pallas_call(second_kernel, out_shape=jax.ShapeDtypeStruct((slots, side...  14.5 us
    ppermute x2, waiting for transfers between devices, from_behind(): return lax.ppermute(block, axis, route)  7.23 us
    pallas_call x1, Pallas kernels, body(): pl.pallas_call(column_kernel, out_shape=jax.ShapeDtypeStruct((pairs, KBLK...  6.01 us
    pallas_call x1, Pallas kernels, body(): pl.pallas_call(pass_through, out_shape=jax.ShapeDtypeStruct(received.shap...  5.85 us
  transfers between devices with their start and end apart: 2, of which 1 were waited for; matrix products, arithmetic and copies ran while one was open for 0% of the time, Pallas kernels for 14%

profile of v14, /device:TPU:1, one launch (start us, length us, event | category | flops | bytes accessed | tf_op | source)
XLA Modules:
  0.0 262.6 jit_solution(17189004527806880827)
XLA Ops:
  0.0 0.1 collective-permute-start.1
  0.1 4.8 %collective-permute-start = (bf16[64,128,128]{2,1,0:T(8,128)(2,1)}, bf16[64,128,128]{2,1,0:T(8,128)(2,1)S(1)}, u32[]{:S(2)}, u32[]{:S(2)}) collective-permute-start(bf16[64,128,128]{2,1,0:T(8,128)(2,1)} %bitcast.8), channel_id=1, source_target_pairs={{1,0},{2,1},{3,2},{0,3},{5,4},{6,5},{7,6},{4,7},{9,8},{10,9},{11,1... | collective-permute-start | bytes 6291464 | tf_op jit(solution)/shard_map/ppermute | solution.py:21
  4.8 30.1 %shard_map.55 = (f32[4,1024,512]{2,1,0:T(8,128)}, s32[128]{0:T(128)}, s32[128]{0:T(128)}, s32[256]{0:T(256)}, bf16[256,128,128]{2,1,0:T(8,128)(2,1)}) custom-call(s32[8,4,64]{2,1,0:T(4,128)} %left_places.1, s32[8,4,64]{2,1,0:T(4,128)} %right_places.1, s32[128]{0:T(128)} %bitcast.10, bf16[64,128,128]{2,1,0:T(8,128)(2,1)} %bitcast.9, bf16[64,128,128]{2,1,0:T(8,128)(2,1)} %bitcast.7), custom_call_target="tpu_custom_call" | custom-call | flops 8589934592 | bytes 12582912 | tf_op jit(solution)/shard_map/pallas_call | solution.py:260
  34.9 0.0 collective-permute-done.1.right_tile
  34.9 6.0 %shard_map.56.columns = bf16[4,2048,512]{2,1,0:T(8,128)(2,1)} custom-call(s32[256]{0:T(256)} %get-tuple-element.12.right_index, bf16[64,128,128]{2,1,0:T(8,128)(2,1)} %collective-permute-done.1.right_tile), custom_call_target="tpu_custom_call" | custom-call | bytes 10485760 | tf_op jit(solution)/shard_map/pallas_call | solution.py:283
  40.9 7.2 %collective-permute-done.left_tile = bf16[64,128,128]{2,1,0:T(8,128)(2,1)S(1)} collective-permute-done((bf16[64,128,128]{2,1,0:T(8,128)(2,1)}, bf16[64,128,128]{2,1,0:T(8,128)(2,1)S(1)}, u32[]{:S(2)}, u32[]{:S(2)}) %collective-permute-start) | collective-permute-done | bytes 2097184 | tf_op jit(solution)/shard_map/ppermute | solution.py:21
  48.2 0.0 copy-start
  48.2 1.3 copy-done
  49.5 14.5 %shard_map.57 = bf16[256,128,128]{2,1,0:T(8,128)(2,1)} custom-call(s32[128]{0:T(128)} %get-tuple-element.10.slot_of, s32[128]{0:T(128)} %get-tuple-element.11.left_index, bf16[64,128,128]{2,1,0:T(8,128)(2,1)} %copy-done, bf16[4,2048,512]{2,1,0:T(8,128)(2,1)} %shard_map.56.columns, ...), custom_call_target="tpu_custom_call", output_to_operand_aliasing={{}: (5, {})} | custom-call | flops 8589934592 | bytes 20971520 | tf_op jit(solution)/shard_map/pallas_call | solution.py:294
  64.0 192.8 %all_to_all.5.source = bf16[32,8,128,128]{3,2,1,0:T(8,128)(2,1)} all-to-all(bf16[32,8,128,128]{3,2,1,0:T(8,128)(2,1)} %bitcast.5), channel_id=1, replica_groups=mesh['row'=8,'col'=4] {'row','col'}, dimensions={0} | all-to-all | bytes 16777216 | tf_op jit(solution)/shard_map/all_to_all | solution.py:315
  256.8 5.9 %shard_map.58 = bf16[32,8,128,128]{3,2,1,0:T(8,128)(2,1)} custom-call(bf16[32,8,128,128]{3,2,1,0:T(8,128)(2,1)} %all_to_all.5.source), custom_call_target="tpu_custom_call" | custom-call | bytes 16777216 | tf_op jit(solution)/shard_map/pallas_call | solution.py:318
Async XLA Ops:
  0.0 34.9 %collective-permute-start.1 = (bf16[64,128,128]{2,1,0:T(8,128)(2,1)}, bf16[64,128,128]{2,1,0:T(8,128)(2,1)}, u32[]{:S(2)}, u32[]{:S(2)}) collective-permute-start(bf16[64,128,128]{2,1,0:T(8,128)(2,1)} %bitcast.6), channel_id=1, source_target_pairs={{4,0},{8,4},{12,8},{16,12},{20,16},{24,20},{28,24},{0,28},{5,1},{9... | collective-permute-start | bytes 6291464 | tf_op jit(solution)/shard_map/ppermute | solution.py:21
  0.1 48.1 %collective-permute-start = (bf16[64,128,128]{2,1,0:T(8,128)(2,1)}, bf16[64,128,128]{2,1,0:T(8,128)(2,1)S(1)}, u32[]{:S(2)}, u32[]{:S(2)}) collective-permute-start(bf16[64,128,128]{2,1,0:T(8,128)(2,1)} %bitcast.8), channel_id=1, source_target_pairs={{1,0},{2,1},{3,2},{0,3},{5,4},{6,5},{7,6},{4,7},{9,8},{10,9},{11,1... | collective-permute-start | bytes 6291464 | tf_op jit(solution)/shard_map/ppermute | solution.py:21
  48.2 1.3 copy-start

commit v15 on v14

--- a/solution.py
+++ b/solution.py
@@ -10,7 +10,7 @@
 ROWB = 8
 KBLK = 16
 COLB = 16
-COL_GROUP = 4
+COL_GROUP = 8
 ROW_GROUP = 8
 COPY_STEPS = 2
 

time: 263 us -> 264 us (level)
  no operation moved by 1% of the time
where the time goes in v15:
time: 264 us
  blocking collectives  193 us (73%)
  Pallas kernels  57.1 us (22%)
  waiting for transfers between devices  7.6 us (3%)
  starting transfers between devices  4.83 us (2%)
    all_to_all x1, blocking collectives, body(): lax.all_to_all(outgoing, ('row', 'col'), split_axis=0, concat_axis=0, til...  193 us
    pallas_call x1, Pallas kernels, body(): pl.pallas_call(functools.partial(first_kernel, rows_grid, cols_grid, capa...  29.6 us
    pallas_call x1, Pallas kernels, body(): pl.pallas_call(second_kernel, out_shape=jax.ShapeDtypeStruct((slots, side...  15.5 us
    ppermute x2, waiting for transfers between devices, from_behind(): return lax.ppermute(block, axis, route)  7.6 us
    pallas_call x1, Pallas kernels, body(): pl.pallas_call(column_kernel, out_shape=jax.ShapeDtypeStruct((pairs, KBLK...  6.12 us
    pallas_call x1, Pallas kernels, body(): pl.pallas_call(pass_through, out_shape=jax.ShapeDtypeStruct(received.shap...  5.85 us
  transfers between devices with their start and end apart: 2, of which 1 were waited for; matrix products, arithmetic and copies ran while one was open for 0% of the time, Pallas kernels for 14%

profile of v15, /device:TPU:1, one launch (start us, length us, event | category | flops | bytes accessed | tf_op | source)
XLA Modules:
  0.0 263.6 jit_solution(14273098441948519657)
XLA Ops:
  0.0 0.1 collective-permute-start.1
  0.1 4.8 %collective-permute-start = (bf16[64,128,128]{2,1,0:T(8,128)(2,1)}, bf16[64,128,128]{2,1,0:T(8,128)(2,1)S(1)}, u32[]{:S(2)}, u32[]{:S(2)}) collective-permute-start(bf16[64,128,128]{2,1,0:T(8,128)(2,1)} %bitcast.8), channel_id=1, source_target_pairs={{1,0},{2,1},{3,2},{0,3},{5,4},{6,5},{7,6},{4,7},{9,8},{10,9},{11,1... | collective-permute-start | bytes 6291464 | tf_op jit(solution)/shard_map/ppermute | solution.py:21
  4.8 29.6 %shard_map.55 = (f32[2,1024,1024]{2,1,0:T(8,128)}, s32[128]{0:T(128)}, s32[128]{0:T(128)}, s32[256]{0:T(256)}, bf16[256,128,128]{2,1,0:T(8,128)(2,1)}) custom-call(s32[8,4,64]{2,1,0:T(4,128)} %left_places.1, s32[8,4,64]{2,1,0:T(4,128)} %right_places.1, s32[128]{0:T(128)} %bitcast.10, bf16[64,128,128]{2,1,0:T(8,128)(2,1)} %bitcast.9, ...), custom_call_target="tpu_custom_call" | custom-call | flops 8589934592 | bytes 12582912 | tf_op jit(solution)/shard_map/pallas_call | solution.py:260
  34.4 0.0 collective-permute-done.1.right_tile
  34.5 6.1 %shard_map.56.columns = bf16[2,2048,1024]{2,1,0:T(8,128)(2,1)} custom-call(s32[256]{0:T(256)} %get-tuple-element.12.right_index, bf16[64,128,128]{2,1,0:T(8,128)(2,1)} %collective-permute-done.1.right_tile), custom_call_target="tpu_custom_call" | custom-call | bytes 10485760 | tf_op jit(solution)/shard_map/pallas_call | solution.py:283
  40.6 7.6 %collective-permute-done.left_tile = bf16[64,128,128]{2,1,0:T(8,128)(2,1)S(1)} collective-permute-done((bf16[64,128,128]{2,1,0:T(8,128)(2,1)}, bf16[64,128,128]{2,1,0:T(8,128)(2,1)S(1)}, u32[]{:S(2)}, u32[]{:S(2)}) %collective-permute-start) | collective-permute-done | bytes 2097184 | tf_op jit(solution)/shard_map/ppermute | solution.py:21
  48.2 0.0 copy-start
  48.2 1.3 copy-done
  49.5 15.5 %shard_map.57 = bf16[256,128,128]{2,1,0:T(8,128)(2,1)} custom-call(s32[128]{0:T(128)} %get-tuple-element.10.slot_of, s32[128]{0:T(128)} %get-tuple-element.11.left_index, bf16[64,128,128]{2,1,0:T(8,128)(2,1)} %copy-done, bf16[2,2048,1024]{2,1,0:T(8,128)(2,1)} %shard_map.56.columns, ...), custom_call_target="tpu_custom_call", output_to_operand_aliasing={{}: (5, {})} | custom-call | flops 8589934592 | bytes 20971520 | tf_op jit(solution)/shard_map/pallas_call | solution.py:294
  65.1 192.7 %all_to_all.5.source = bf16[32,8,128,128]{3,2,1,0:T(8,128)(2,1)} all-to-all(bf16[32,8,128,128]{3,2,1,0:T(8,128)(2,1)} %bitcast.5), channel_id=1, replica_groups=mesh['row'=8,'col'=4] {'row','col'}, dimensions={0} | all-to-all | bytes 16777216 | tf_op jit(solution)/shard_map/all_to_all | solution.py:315
  257.8 5.9 %shard_map.58 = bf16[32,8,128,128]{3,2,1,0:T(8,128)(2,1)} custom-call(bf16[32,8,128,128]{3,2,1,0:T(8,128)(2,1)} %all_to_all.5.source), custom_call_target="tpu_custom_call" | custom-call | bytes 16777216 | tf_op jit(solution)/shard_map/pallas_call | solution.py:318
Async XLA Ops:
  0.0 34.5 %collective-permute-start.1 = (bf16[64,128,128]{2,1,0:T(8,128)(2,1)}, bf16[64,128,128]{2,1,0:T(8,128)(2,1)}, u32[]{:S(2)}, u32[]{:S(2)}) collective-permute-start(bf16[64,128,128]{2,1,0:T(8,128)(2,1)} %bitcast.6), channel_id=1, source_target_pairs={{4,0},{8,4},{12,8},{16,12},{20,16},{24,20},{28,24},{0,28},{5,1},{9... | collective-permute-start | bytes 6291464 | tf_op jit(solution)/shard_map/ppermute | solution.py:21
  0.1 48.1 %collective-permute-start = (bf16[64,128,128]{2,1,0:T(8,128)(2,1)}, bf16[64,128,128]{2,1,0:T(8,128)(2,1)S(1)}, u32[]{:S(2)}, u32[]{:S(2)}) collective-permute-start(bf16[64,128,128]{2,1,0:T(8,128)(2,1)} %bitcast.8), channel_id=1, source_target_pairs={{1,0},{2,1},{3,2},{0,3},{5,4},{6,5},{7,6},{4,7},{9,8},{10,9},{11,1... | collective-permute-start | bytes 6291464 | tf_op jit(solution)/shard_map/ppermute | solution.py:21
  48.2 1.3 copy-start

commit v16 on v14

--- a/solution.py
+++ b/solution.py
@@ -11,7 +11,7 @@
 KBLK = 16
 COLB = 16
 COL_GROUP = 4
-ROW_GROUP = 8
+ROW_GROUP = 4
 COPY_STEPS = 2
 
 

time: 263 us -> 263 us (level)
  no operation moved by 1% of the time
where the time goes in v16:
time: 263 us
  blocking collectives  193 us (73%)
  Pallas kernels  58.7 us (22%)
  waiting for transfers between devices  5.57 us (2%)
  starting transfers between devices  4.83 us (2%)
    all_to_all x1, blocking collectives, body(): lax.all_to_all(outgoing, ('row', 'col'), split_axis=0, concat_axis=0, til...  193 us
    pallas_call x1, Pallas kernels, body(): pl.pallas_call(functools.partial(first_kernel, rows_grid, cols_grid, capa...  31.8 us
    pallas_call x1, Pallas kernels, body(): pl.pallas_call(second_kernel, out_shape=jax.ShapeDtypeStruct((slots, side...  15.1 us
    pallas_call x1, Pallas kernels, body(): pl.pallas_call(column_kernel, out_shape=jax.ShapeDtypeStruct((pairs, KBLK...  6.01 us
    pallas_call x1, Pallas kernels, body(): pl.pallas_call(pass_through, out_shape=jax.ShapeDtypeStruct(received.shap...  5.85 us
    ppermute x2, waiting for transfers between devices, from_behind(): return lax.ppermute(block, axis, route)  5.57 us
  transfers between devices with their start and end apart: 2, of which 1 were waited for; matrix products, arithmetic and copies ran while one was open for 0% of the time, Pallas kernels for 14%

profile of v16, /device:TPU:1, one launch (start us, length us, event | category | flops | bytes accessed | tf_op | source)
XLA Modules:
  0.0 263.2 jit_solution(12387551925236353898)
XLA Ops:
  0.0 0.1 collective-permute-start.1
  0.1 4.8 %collective-permute-start = (bf16[64,128,128]{2,1,0:T(8,128)(2,1)}, bf16[64,128,128]{2,1,0:T(8,128)(2,1)S(1)}, u32[]{:S(2)}, u32[]{:S(2)}) collective-permute-start(bf16[64,128,128]{2,1,0:T(8,128)(2,1)} %bitcast.8), channel_id=1, source_target_pairs={{1,0},{2,1},{3,2},{0,3},{5,4},{6,5},{7,6},{4,7},{9,8},{10,9},{11,1... | collective-permute-start | bytes 6291464 | tf_op jit(solution)/shard_map/ppermute | solution.py:21
  4.8 31.8 %shard_map.55 = (f32[4,1024,512]{2,1,0:T(8,128)}, s32[128]{0:T(128)}, s32[128]{0:T(128)}, s32[256]{0:T(256)}, bf16[256,128,128]{2,1,0:T(8,128)(2,1)}) custom-call(s32[8,4,64]{2,1,0:T(4,128)} %left_places.1, s32[8,4,64]{2,1,0:T(4,128)} %right_places.1, s32[128]{0:T(128)} %bitcast.10, bf16[64,128,128]{2,1,0:T(8,128)(2,1)} %bitcast.9, bf16[64,128,128]{2,1,0:T(8,128)(2,1)} %bitcast.7), custom_call_target="tpu_custom_call" | custom-call | flops 8589934592 | bytes 12582912 | tf_op jit(solution)/shard_map/pallas_call | solution.py:260
  36.6 0.0 collective-permute-done.1.right_tile
  36.6 6.0 %shard_map.56.columns = bf16[4,2048,512]{2,1,0:T(8,128)(2,1)} custom-call(s32[256]{0:T(256)} %get-tuple-element.12.right_index, bf16[64,128,128]{2,1,0:T(8,128)(2,1)} %collective-permute-done.1.right_tile), custom_call_target="tpu_custom_call" | custom-call | bytes 10485760 | tf_op jit(solution)/shard_map/pallas_call | solution.py:283
  42.6 5.6 %collective-permute-done.left_tile = bf16[64,128,128]{2,1,0:T(8,128)(2,1)S(1)} collective-permute-done((bf16[64,128,128]{2,1,0:T(8,128)(2,1)}, bf16[64,128,128]{2,1,0:T(8,128)(2,1)S(1)}, u32[]{:S(2)}, u32[]{:S(2)}) %collective-permute-start) | collective-permute-done | bytes 2097184 | tf_op jit(solution)/shard_map/ppermute | solution.py:21
  48.2 0.0 copy-start
  48.2 1.3 copy-done
  49.5 15.1 %shard_map.57 = bf16[256,128,128]{2,1,0:T(8,128)(2,1)} custom-call(s32[128]{0:T(128)} %get-tuple-element.10.slot_of, s32[128]{0:T(128)} %get-tuple-element.11.left_index, bf16[64,128,128]{2,1,0:T(8,128)(2,1)} %copy-done, bf16[4,2048,512]{2,1,0:T(8,128)(2,1)} %shard_map.56.columns, ...), custom_call_target="tpu_custom_call", output_to_operand_aliasing={{}: (5, {})} | custom-call | flops 8589934592 | bytes 20971520 | tf_op jit(solution)/shard_map/pallas_call | solution.py:294
  64.6 192.7 %all_to_all.5.source = bf16[32,8,128,128]{3,2,1,0:T(8,128)(2,1)} all-to-all(bf16[32,8,128,128]{3,2,1,0:T(8,128)(2,1)} %bitcast.5), channel_id=1, replica_groups=mesh['row'=8,'col'=4] {'row','col'}, dimensions={0} | all-to-all | bytes 16777216 | tf_op jit(solution)/shard_map/all_to_all | solution.py:315
  257.3 5.9 %shard_map.58 = bf16[32,8,128,128]{3,2,1,0:T(8,128)(2,1)} custom-call(bf16[32,8,128,128]{3,2,1,0:T(8,128)(2,1)} %all_to_all.5.source), custom_call_target="tpu_custom_call" | custom-call | bytes 16777216 | tf_op jit(solution)/shard_map/pallas_call | solution.py:318
Async XLA Ops:
  0.0 36.6 %collective-permute-start.1 = (bf16[64,128,128]{2,1,0:T(8,128)(2,1)}, bf16[64,128,128]{2,1,0:T(8,128)(2,1)}, u32[]{:S(2)}, u32[]{:S(2)}) collective-permute-start(bf16[64,128,128]{2,1,0:T(8,128)(2,1)} %bitcast.6), channel_id=1, source_target_pairs={{4,0},{8,4},{12,8},{16,12},{20,16},{24,20},{28,24},{0,28},{5,1},{9... | collective-permute-start | bytes 6291464 | tf_op jit(solution)/shard_map/ppermute | solution.py:21
  0.1 48.1 %collective-permute-start = (bf16[64,128,128]{2,1,0:T(8,128)(2,1)}, bf16[64,128,128]{2,1,0:T(8,128)(2,1)S(1)}, u32[]{:S(2)}, u32[]{:S(2)}) collective-permute-start(bf16[64,128,128]{2,1,0:T(8,128)(2,1)} %bitcast.8), channel_id=1, source_target_pairs={{1,0},{2,1},{3,2},{0,3},{5,4},{6,5},{7,6},{4,7},{9,8},{10,9},{11,1... | collective-permute-start | bytes 6291464 | tf_op jit(solution)/shard_map/ppermute | solution.py:21
  48.2 1.3 copy-start

commit v17 on v14

--- a/solution.py
+++ b/solution.py
@@ -241,7 +241,7 @@
     left_here = left_values[0, 0]
     right_here = right_values[0, 0]
     side = left_here.shape[-1]
-    left_next = from_behind(left_here, "col", -1)
+    left_next = lax.optimization_barrier(from_behind(left_here, "col", -1))
     right_next = from_behind(right_here, "row", -1)
     capacity = 2 * ROWB * COLB // devices_all
     slots = devices_all * capacity

time: 263 us -> 268 us (1.019)
  waiting for transfers between devices: 7.23 us -> 13.6 us
    ppermute x2, waiting for transfers between devices: 7.23 us -> 13.6 us  [from_behind(): return lax.ppermute(block, axis, route)]
  transfers between devices with their start and end apart: 2 -> 2, of which waited for: 1 -> 1; matrix products, arithmetic and copies ran while one was open for 0% -> 0% of each run, Pallas kernels for 14% -> 11%
where the time goes in v17:
time: 268 us; the launch traced here: 267 us
  blocking collectives  191 us (71%)
  Pallas kernels  57.2 us (21%)
  waiting for transfers between devices  13.6 us (5%)
  starting transfers between devices  5.11 us (2%)
    all_to_all x1, blocking collectives, body(): lax.all_to_all(outgoing, ('row', 'col'), split_axis=0, concat_axis=0, til...  191 us
    pallas_call x1, Pallas kernels, body(): pl.pallas_call(functools.partial(first_kernel, rows_grid, cols_grid, capa...  30.1 us
    pallas_call x1, Pallas kernels, body(): pl.pallas_call(second_kernel, out_shape=jax.ShapeDtypeStruct((slots, side...  14.5 us
    ppermute x2, waiting for transfers between devices, from_behind(): return lax.ppermute(block, axis, route)  13.6 us
    pallas_call x1, Pallas kernels, body(): pl.pallas_call(column_kernel, out_shape=jax.ShapeDtypeStruct((pairs, KBLK...  6.76 us
    pallas_call x1, Pallas kernels, body(): pl.pallas_call(pass_through, out_shape=jax.ShapeDtypeStruct(received.shap...  5.85 us
  transfers between devices with their start and end apart: 2, of which 1 were waited for; matrix products, arithmetic and copies ran while one was open for 0% of the time, Pallas kernels for 11%

profile of v17, /device:TPU:1, one launch (start us, length us, event | category | flops | bytes accessed | tf_op | source)
XLA Modules:
  0.0 267.4 jit_solution(7373827352591989194)
XLA Ops:
  0.0 4.2 %collective-permute-start = (bf16[64,128,128]{2,1,0:T(8,128)(2,1)}, bf16[64,128,128]{2,1,0:T(8,128)(2,1)S(1)}, u32[]{:S(2)}, u32[]{:S(2)}) collective-permute-start(bf16[64,128,128]{2,1,0:T(8,128)(2,1)} %bitcast.6), channel_id=1, source_target_pairs={{1,0},{2,1},{3,2},{0,3},{5,4},{6,5},{7,6},{4,7},{9,8},{10,9},{11,1... | collective-permute-start | bytes 6291464 | tf_op jit(solution)/shard_map/ppermute | solution.py:21
  4.2 1.0 collective-permute-start.1
  5.1 30.1 %shard_map.55 = (f32[4,1024,512]{2,1,0:T(8,128)}, s32[128]{0:T(128)}, s32[128]{0:T(128)}, s32[256]{0:T(256)}, bf16[256,128,128]{2,1,0:T(8,128)(2,1)}) custom-call(s32[8,4,64]{2,1,0:T(4,128)} %left_places.1, s32[8,4,64]{2,1,0:T(4,128)} %right_places.1, s32[128]{0:T(128)} %bitcast.10, bf16[64,128,128]{2,1,0:T(8,128)(2,1)} %bitcast.7, bf16[64,128,128]{2,1,0:T(8,128)(2,1)} %bitcast.9), custom_call_target="tpu_custom_call" | custom-call | flops 8589934592 | bytes 12582912 | tf_op jit(solution)/shard_map/pallas_call | solution.py:260
  35.2 13.6 %collective-permute-done.left_tile = bf16[64,128,128]{2,1,0:T(8,128)(2,1)S(1)} collective-permute-done((bf16[64,128,128]{2,1,0:T(8,128)(2,1)}, bf16[64,128,128]{2,1,0:T(8,128)(2,1)S(1)}, u32[]{:S(2)}, u32[]{:S(2)}) %collective-permute-start) | collective-permute-done | bytes 2097184 | tf_op jit(solution)/shard_map/ppermute | solution.py:21
  48.8 0.0 copy-start
  48.8 0.0 collective-permute-done.1.right_tile
  48.8 6.8 %shard_map.56.columns = bf16[4,2048,512]{2,1,0:T(8,128)(2,1)} custom-call(s32[256]{0:T(256)} %get-tuple-element.12.right_index, bf16[64,128,128]{2,1,0:T(8,128)(2,1)} %collective-permute-done.1.right_tile), custom_call_target="tpu_custom_call" | custom-call | bytes 10485760 | tf_op jit(solution)/shard_map/pallas_call | solution.py:283
  55.5 0.0 copy-done
  55.6 14.5 %shard_map.57 = bf16[256,128,128]{2,1,0:T(8,128)(2,1)} custom-call(s32[128]{0:T(128)} %get-tuple-element.10.slot_of, s32[128]{0:T(128)} %get-tuple-element.11.left_index, bf16[64,128,128]{2,1,0:T(8,128)(2,1)} %copy-done, bf16[4,2048,512]{2,1,0:T(8,128)(2,1)} %shard_map.56.columns, ...), custom_call_target="tpu_custom_call", output_to_operand_aliasing={{}: (5, {})} | custom-call | flops 8589934592 | bytes 20971520 | tf_op jit(solution)/shard_map/pallas_call | solution.py:294
  70.1 191.5 %all_to_all.5.source = bf16[32,8,128,128]{3,2,1,0:T(8,128)(2,1)} all-to-all(bf16[32,8,128,128]{3,2,1,0:T(8,128)(2,1)} %bitcast.5), channel_id=1, replica_groups=mesh['row'=8,'col'=4] {'row','col'}, dimensions={0} | all-to-all | bytes 16777216 | tf_op jit(solution)/shard_map/all_to_all | solution.py:315
  261.6 5.9 %shard_map.58 = bf16[32,8,128,128]{3,2,1,0:T(8,128)(2,1)} custom-call(bf16[32,8,128,128]{3,2,1,0:T(8,128)(2,1)} %all_to_all.5.source), custom_call_target="tpu_custom_call" | custom-call | bytes 16777216 | tf_op jit(solution)/shard_map/pallas_call | solution.py:318
Async XLA Ops:
  0.0 48.8 %collective-permute-start = (bf16[64,128,128]{2,1,0:T(8,128)(2,1)}, bf16[64,128,128]{2,1,0:T(8,128)(2,1)S(1)}, u32[]{:S(2)}, u32[]{:S(2)}) collective-permute-start(bf16[64,128,128]{2,1,0:T(8,128)(2,1)} %bitcast.6), channel_id=1, source_target_pairs={{1,0},{2,1},{3,2},{0,3},{5,4},{6,5},{7,6},{4,7},{9,8},{10,9},{11,1... | collective-permute-start | bytes 6291464 | tf_op jit(solution)/shard_map/ppermute | solution.py:21
  4.2 44.6 %collective-permute-start.1 = (bf16[64,128,128]{2,1,0:T(8,128)(2,1)}, bf16[64,128,128]{2,1,0:T(8,128)(2,1)}, u32[]{:S(2)}, u32[]{:S(2)}) collective-permute-start(bf16[64,128,128]{2,1,0:T(8,128)(2,1)} %bitcast.8), channel_id=1, source_target_pairs={{4,0},{8,4},{12,8},{16,12},{20,16},{24,20},{28,24},{0,28},{5,1},{9... | collective-permute-start | bytes 6291464 | tf_op jit(solution)/shard_map/ppermute | solution.py:21
  48.8 6.8 %copy-start = (bf16[64,128,128]{2,1,0:T(8,128)(2,1)}, bf16[64,128,128]{2,1,0:T(8,128)(2,1)S(1)}, u32[]{:S(2)}) copy-start(bf16[64,128,128]{2,1,0:T(8,128)(2,1)S(1)} %collective-permute-done.left_tile) | copy-start | bytes 6291460
